TPU v7x, 128 devices: a whole 4x4x4 slice. The times are simulated.
128 devices in a mesh: req: 16 (over z, x), mlp: 8 (over y, core).
Axes of the slice: x: 4, y: 4, z: 4, core: 2. Of those that a mesh axis runs over, the one named last changes fastest.
Arguments:
- residual_input: bfloat16 [9216, 5120], P('req', 'mlp'), as said below
- attention_output: bfloat16 [9216, 3072], P('req', 'mlp'), may hold values from -6 to 6
- request_length: int32 [16, 4], replicated, may hold values from 1 to 573, as said below
- request_group: int32 [64], replicated, may hold values from 0 to 7
- adapter_per_group: int32 [8], replicated, may hold values from 0 to 15
- output_weight: bfloat16 [3072, 5120], P('mlp', 'req'), may hold values from -0.109375 to 0.109375
- output_down_maps: bfloat16 [3072, 16, 16], P('mlp'), may hold values from -0.109375 to 0.109375
- output_up_maps: bfloat16 [16, 16, 5120], P(None, None, 'mlp'), may hold values from -1.5 to 1.5
- modulation: float32 [8, 3, 5120], replicated, may hold values from -3 to 3
- hidden_down_maps: bfloat16 [5120, 16, 16], P('mlp'), may hold values from -0.078125 to 0.078125
- hidden_up_maps: bfloat16 [16, 16, 6912], P(None, None, 'mlp'), may hold values from -1.5 to 1.5
- up_weight: bfloat16 [5120, 6912], P('req', 'mlp'), may hold values from -0.078125 to 0.078125
- down_weight: bfloat16 [6912, 5120], P('mlp', 'req'), may hold values from -0.078125 to 0.078125
Outputs:
- layer_out: bfloat16 [384, 16, 5120], P(None, 'req', 'mlp')
Inputs may be any that keep to these rules, and one draw needn't show every extreme that they name: `request_length`: the 4 lengths of one block sum to at most 576, and to exactly 576 for one block; all lengths together sum to 6144. One request has exactly the largest length. `residual_input`: rows of a block past its live rows are never read.
All inputs are finite; a program needn't handle non-finite values.
Results may differ from a plain program's by a relative error of at most 0.012.
Values may be sent and summed in bfloat16 or wider, within the bound.
No kernel may reach another device: no remote copies, remote signals or barrier semaphores. Data moves between devices by JAX's collectives and lax.ppermute only.
A program may use at most 192 MiB of HBM per device.

v0:
```python
import jax
import jax.numpy as jnp
from jax import lax
from jax.sharding import PartitionSpec as P

MODEL_WIDTH = 5120
ADAPTER_RANK = 16
ADAPTER_TOTAL = 16
TOK_DEV = 384
Y_COUNT = 4


norm_epsilon = 1e-06


def send_layout(packed, offset, req_count):
    shaped = packed.reshape(packed.shape[0] // req_count, req_count, packed.shape[1])
    return jnp.roll(shaped, offset, axis=1)


def compact(moved, starts, ends, req_count, token_rank):
    slots = moved.shape[0] * moved.shape[1]
    flat_rows = moved.reshape(slots, moved.shape[2])
    source = jnp.sum((ends[None, :] <= token_rank[:, None]).astype(jnp.int32), axis=1)
    source_hot = source[:, None] == jnp.arange(req_count, dtype=jnp.int32)[None, :]
    source_start = jnp.sum(jnp.where(source_hot, starts[None, :], 0), axis=1)
    position = (token_rank - source_start) // req_count * req_count + source
    return jnp.take(flat_rows, position, axis=0)


def token_groups(token_rank, request_length, request_group, adapter_per_group):
    req_ends = jnp.cumsum(request_length.reshape(-1))
    request_count = req_ends.shape[0]
    request = jnp.sum((req_ends[None, :] <= token_rank[:, None]).astype(jnp.int32), axis=1)
    request = jnp.minimum(request, request_count - 1)
    request_hot = request[:, None] == jnp.arange(request_count, dtype=jnp.int32)[None, :]
    group_ids = jnp.sum(jnp.where(request_hot, request_group[None, :], 0), axis=1)
    group_count = adapter_per_group.shape[0]
    group_hot = group_ids[:, None] == jnp.arange(group_count, dtype=jnp.int32)[None, :]
    adapter_of_row = jnp.sum(jnp.where(group_hot, adapter_per_group[None, :], 0), axis=1)
    adapter_hot = (
        adapter_of_row[:, None] == jnp.arange(ADAPTER_TOTAL, dtype=jnp.int32)[None, :]
    ).astype(jnp.float32)
    return group_ids, adapter_hot


def select_low(output_rank_rows, adapter_hot):
    shaped = output_rank_rows.reshape(output_rank_rows.shape[0], ADAPTER_TOTAL, ADAPTER_RANK)
    return jnp.sum(shaped * adapter_hot[:, :, None], axis=1)


def expand_rank_rows(low_rows, adapter_hot):
    spread_rows = adapter_hot.astype(jnp.bfloat16)[:, :, None] * low_rows[:, None, :]
    return spread_rows.reshape(low_rows.shape[0], ADAPTER_TOTAL * ADAPTER_RANK)


def mlp_sum(part):
    n = lax.axis_size("mlp")
    total = part.astype(jnp.float32)
    bit = 1
    while bit < n:
        total = total + lax.ppermute(total, "mlp", [(i, i ^ bit) for i in range(n)])
        bit *= 2
    return total


def mlp_move(block, target):
    n = lax.axis_size("mlp")
    return lax.ppermute(block, "mlp", [(i, target(i)) for i in range(n)])


def y_shift(step, y_count):
    return lambda i: ((i // 2 + step) % y_count) * 2 + i % 2


def scatter_mlp(payload):
    y_count = payload.shape[0]
    m = lax.axis_index("mlp")
    y_here = m // 2
    core = m % 2
    mine = lax.dynamic_index_in_dim(payload, core, 1, keepdims=False)
    other = lax.dynamic_index_in_dim(payload, 1 - core, 1, keepdims=False)
    pair = mine.astype(jnp.float32) + mlp_move(other, lambda i: i ^ 1).astype(jnp.float32)
    pair_b = pair.astype(jnp.bfloat16)
    total = lax.dynamic_index_in_dim(pair, y_here, 0, keepdims=False)
    for step in range(1, y_count):
        send = lax.dynamic_index_in_dim(pair_b, (y_here + step) % y_count, 0, keepdims=False)
        total = total + mlp_move(send, y_shift(step, y_count)).astype(jnp.float32)
    return total


def gather_mlp(block, y_count):
    m = lax.axis_index("mlp")
    y_here = m // 2
    core = m % 2
    pair = jnp.stack([block, mlp_move(block, lambda i: i ^ 1)], axis=0)
    rows = [pair] + [mlp_move(pair, y_shift(step, y_count)) for step in range(1, y_count)]
    held = jnp.stack(rows, axis=0).reshape((2 * y_count,) + block.shape)
    target = jnp.arange(2 * y_count, dtype=jnp.int32)
    slot = ((y_here - target // 2) % y_count) * 2 + (target % 2) ^ core
    return jnp.take(held, slot, axis=0)


def local(
    residual_input,
    attention_output,
    request_length,
    request_group,
    adapter_per_group,
    output_weight,
    output_down_maps,
    output_up_maps,
    modulation,
    hidden_down_maps,
    hidden_up_maps,
    up_weight,
    down_weight,
):
    req_count = lax.axis_size("req")
    mlp_count = lax.axis_size("mlp")
    device_index = lax.axis_index("req")
    column_index = lax.axis_index("mlp")
    width = residual_input.shape[1]
    head_width = attention_output.shape[1]

    out_w = lax.all_gather(output_weight, "req", axis=1, tiled=True)
    up_w = lax.all_gather(up_weight, "req", axis=0, tiled=True)
    down_w = lax.all_gather(down_weight, "req", axis=1, tiled=True)

    live_rows = jnp.sum(request_length, axis=1)
    dev_ends = jnp.cumsum(live_rows)
    dev_starts = dev_ends - live_rows
    offset = dev_starts[device_index]
    tok_dev = TOK_DEV
    token_rank = jnp.arange(tok_dev, dtype=jnp.int32) * req_count + device_index
    moved_attn = lax.all_to_all(
        send_layout(attention_output, offset, req_count), "req", split_axis=1, concat_axis=1, tiled=True
    )
    attention_rows = compact(moved_attn, dev_starts, dev_ends, req_count, token_rank)
    moved_res = lax.all_to_all(
        send_layout(residual_input, offset, req_count), "req", split_axis=1, concat_axis=1, tiled=True
    )
    residual_rows = compact(moved_res, dev_starts, dev_ends, req_count, token_rank)

    group_ids, adapter_hot = token_groups(token_rank, request_length, request_group, adapter_per_group)
    shift_rows = jnp.take(modulation[:, 0, :], group_ids, axis=0)
    scale_rows = jnp.take(modulation[:, 1, :], group_ids, axis=0)
    gate_table = lax.dynamic_slice_in_dim(modulation[:, 2, :], column_index * width, width, 1)
    gate_rows = jnp.take(gate_table, group_ids, axis=0)

    head_terms = jnp.einsum(
        "tk,kmc->mtc",
        attention_rows,
        out_w.reshape(head_width, mlp_count, width),
        preferred_element_type=jnp.float32,
    )
    out_low = select_low(
        jnp.dot(
            attention_rows,
            output_down_maps.reshape(head_width, ADAPTER_TOTAL * ADAPTER_RANK),
            preferred_element_type=jnp.float32,
        ),
        adapter_hot,
    )
    low_count = out_low.size
    low_rows = -(-low_count // width)
    low_flat = jnp.pad(out_low.reshape(-1), (0, low_rows * width - low_count)).reshape(
        1, low_rows, width
    )
    send = jnp.concatenate(
        [head_terms, jnp.broadcast_to(low_flat, (mlp_count, low_rows, width))], axis=1
    ).astype(jnp.bfloat16)
    summed = scatter_mlp(send.reshape((Y_COUNT, mlp_count // Y_COUNT) + send.shape[1:]))
    projection_rows = summed[:tok_dev]
    output_rank_values = (
        summed[tok_dev:].reshape(-1)[:low_count].reshape(tok_dev, ADAPTER_RANK).astype(jnp.bfloat16)
    )
    adapter_delta = jnp.dot(
        expand_rank_rows(output_rank_values, adapter_hot),
        output_up_maps.reshape(ADAPTER_TOTAL * ADAPTER_RANK, width),
        preferred_element_type=jnp.float32,
    )
    blended_rows = (residual_rows.astype(jnp.float32) + projection_rows + adapter_delta).astype(
        jnp.bfloat16
    )
    values = blended_rows.astype(jnp.float32)

    full_rows = gather_mlp(blended_rows, Y_COUNT).astype(jnp.float32)
    row_mean = jnp.sum(full_rows, axis=(0, 2)) / MODEL_WIDTH
    variance = jnp.sum(full_rows * full_rows, axis=(0, 2)) / MODEL_WIDTH - row_mean * row_mean
    inv = lax.rsqrt(variance + norm_epsilon)
    scale_m = (1.0 + scale_rows).reshape(-1, mlp_count, width).transpose(1, 0, 2)
    shift_m = shift_rows.reshape(-1, mlp_count, width).transpose(1, 0, 2)
    normalized = (
        (full_rows - row_mean[None, :, None]) * inv[None, :, None] * scale_m + shift_m
    ).astype(jnp.bfloat16)

    normed_local = lax.dynamic_index_in_dim(normalized, column_index, 0, keepdims=False)
    part_low = jnp.dot(
        normed_local,
        hidden_down_maps.reshape(width, ADAPTER_TOTAL * ADAPTER_RANK),
        preferred_element_type=jnp.float32,
    )
    hidden_rank_values = mlp_sum(select_low(part_low, adapter_hot).astype(jnp.bfloat16)).astype(
        jnp.bfloat16
    )
    hidden_units = up_weight.shape[1]
    hidden_total = jnp.einsum(
        "mtc,mch->th",
        normalized,
        up_w.reshape(mlp_count, width, hidden_units),
        preferred_element_type=jnp.float32,
    )
    hidden_total = hidden_total + jnp.dot(
        expand_rank_rows(hidden_rank_values, adapter_hot),
        hidden_up_maps.reshape(ADAPTER_TOTAL * ADAPTER_RANK, hidden_units),
        preferred_element_type=jnp.float32,
    )
    hidden = jax.nn.gelu(hidden_total, approximate=True).astype(jnp.bfloat16)
    down_terms = jnp.einsum(
        "th,hmc->mtc",
        hidden,
        down_w.reshape(hidden_units, mlp_count, width),
        preferred_element_type=jnp.float32,
    ).astype(jnp.bfloat16)
    down_sum = scatter_mlp(
        down_terms.reshape((Y_COUNT, mlp_count // Y_COUNT) + down_terms.shape[1:])
    )
    result = (values + gate_rows * down_sum).astype(jnp.bfloat16)
    return result.reshape(tok_dev, 1, width)


def solution(mesh):
    placed = (
        P("req", "mlp"),
        P("req", "mlp"),
        P(),
        P(),
        P(),
        P("mlp", "req"),
        P("mlp", None, None),
        P(None, None, "mlp"),
        P(),
        P("mlp", None, None),
        P(None, None, "mlp"),
        P("req", "mlp"),
        P("mlp", "req"),
    )
    return jax.shard_map(
        local, mesh=mesh, in_specs=placed, out_specs=P(None, "req", "mlp"), check_vma=False
    )
```

profile of v0, /device:TPU:1, one launch (start us, length us, event | category | flops | bytes accessed | tf_op | source)
XLA Modules:
  0.0 279.8 jit_solution(17899731412859381511)
XLA Ops:
  14.5 8.4 %all-to-all-start.1 = ((bf16[36,16,384]{2,0,1:T(8,128)(2,1)}), bf16[36,16,384]{2,0,1:T(8,128)(2,1)S(1)}, u32[]{:S(2)}, u32[]{:S(2)}) async-start(bf16[36,16,384]{2,0,1:T(8,128)(2,1)} %copy.91), calls=%async_computation.1 | async-start | bytes 983040 | tf_op jit(solution)/shard_map/all_to_all | solution.py:136
  23.9 12.7 %all-to-all-done.1 = bf16[36,16,384]{2,0,1:T(8,128)(2,1)S(1)} async-done(((bf16[36,16,384]{2,0,1:T(8,128)(2,1)}), bf16[36,16,384]{2,0,1:T(8,128)(2,1)S(1)}, u32[]{:S(2)}, u32[]{:S(2)}) %all-to-all-start.1) | async-done | bytes 442400 | tf_op jit(solution)/shard_map/all_to_all | solution.py:136
  36.7 2.1 gather_fusion.1
  39.5 26.5 %all-gather.4.cloned.1.call-done = bf16[384,5120]{0,1:T(8,128)(2,1)} async-done(((bf16[384,320]{0,1:T(8,128)(2,1)}), bf16[384,5120]{0,1:T(8,128)(2,1)}) %all-gather.4.cloned.1.call-update) | async-done | bytes 3932176 | tf_op jit(solution)/shard_map/all_gather | solution.py:126
  66.0 4.4 %convolution_convert_fusion.1 = bf16[384,8,640]{2,0,1:T(8,128)(2,1)S(1)} fusion(bf16[384,8,640]{0,2,1:T(8,128)(2,1)} %bitcast.160, bf16[384,384]{1,0:T(8,128)(2,1)S(1)} %gather_fusion.1, pred[384]{0:T(512)(128)(4,1)S(1)} %compare_and_fusion.2), kind=kOutput, calls=%fused_computation.27 | convolution fusion | flops 1512062976 | bytes 8159616 | tf_op jit(solution)/shard_map/tk,kmc->mtc/dot_general | solution.py:151
  70.6 2.3 copy.98
  75.7 4.7 %all-to-all-start = ((bf16[36,16,640]{2,0,1:T(8,128)(2,1)}), bf16[36,16,640]{2,0,1:T(8,128)(2,1)S(1)}, u32[]{:S(2)}, u32[]{:S(2)}) async-start(bf16[36,16,640]{2,0,1:T(8,128)(2,1)} %copy.89), calls=%async_computation | async-start | bytes 1638400 | tf_op jit(solution)/shard_map/all_to_all | solution.py:140
  80.5 4.9 %convert_add_fusion = (f32[4,394,640]{2,1,0:T(8,128)}, bf16[4,394,640]{2,1,0:T(8,128)(2,1)S(1)}) fusion(s32[]{:T(128)S(6)} %select_n.253, bf16[4,2,10,640]{3,2,0,1:T(8,128)(2,1)S(1)} %broadcast_in_dim.135, bf16[4,394,640]{2,0,1:T(4,128)(2,1)} %collective-permute-done, bf16[4,2,384,640]{3,2,1,0:T(8,128)(2,1)} %bitcast.152), kind=kLoop, calls=%fused_computation.19 | loop fusion | flops 14120960 | bytes 12103684 | tf_op jit(solution)/shard_map/add | solution.py:83
  87.6 2.4 collective-permute-start.2
  91.9 10.2 %all-to-all-done = bf16[36,16,640]{2,0,1:T(8,128)(2,1)S(1)} async-done(((bf16[36,16,640]{2,0,1:T(8,128)(2,1)}), bf16[36,16,640]{2,0,1:T(8,128)(2,1)S(1)}, u32[]{:S(2)}, u32[]{:S(2)}) %all-to-all-start) | async-done | bytes 737312 | tf_op jit(solution)/shard_map/all_to_all | solution.py:140
  102.2 2.6 gather_fusion
  104.8 8.0 %collective-permute-done.2 = bf16[394,640]{1,0:T(8,128)(2,1)} collective-permute-done((bf16[394,640]{1,0:T(8,128)(2,1)S(1)}, bf16[394,640]{1,0:T(8,128)(2,1)}, u32[]{:S(2)}, u32[]{:S(2)}) %collective-permute-start.2) | collective-permute-done | bytes 504352 | tf_op jit(solution)/shard_map/ppermute | solution.py:69
  117.7 5.4 %gather_fusion.4 = f32[384,5120]{1,0:T(8,128)} fusion(f32[8,5120]{1,0:T(8,128)S(1)} %get-tuple-element.22, s32[1024]{0:T(1024)S(1)} %pad_clamp_fusion), kind=kCustom, calls=%fused_computation.clone | custom fusion | bytes 15730176 | tf_op jit(solution)/shard_map/jit(_take)/gather | solution.py:147
  123.1 5.5 %gather_fusion.5 = f32[384,5120]{1,0:T(8,128)} fusion(f32[8,5120]{1,0:T(8,128)S(1)} %get-tuple-element.21, s32[1024]{0:T(1024)S(1)} %pad_clamp_fusion), kind=kCustom, calls=%fused_computation.1.clone | custom fusion | bytes 15730176 | tf_op jit(solution)/shard_map/jit(_take)/gather | solution.py:146
  129.7 2.1 collective-permute-start.6
  133.1 10.3 %select_add_fusion = (f32[384,5120]{1,0:T(8,128)}, f32[384,5120]{1,0:T(8,128)}) fusion(f32[384,5120]{1,0:T(8,128)} %gather_fusion.4, pred[384]{0:T(512)(128)(4,1)S(1)} %compare_and_fusion.1, f32[384,5120]{1,0:T(8,128)} %gather_fusion.5), kind=kLoop, calls=%fused_computation.16 | loop fusion | flops 5898240 | bytes 31457664 | tf_op jit(solution)/shard_map/add | solution.py:192
  143.5 9.9 %collective-permute-done.5 = bf16[2,384,640]{2,1,0:T(8,128)(2,1)} collective-permute-done((bf16[2,384,640]{2,1,0:T(8,128)(2,1)S(1)}, bf16[2,384,640]{2,1,0:T(8,128)(2,1)}, u32[]{:S(2)}, u32[]{:S(2)}) %collective-permute-start.5) | collective-permute-done | bytes 983072 | tf_op jit(solution)/shard_map/ppermute | solution.py:69
  153.4 21.4 %collective-permute-done.6 = bf16[2,384,640]{2,1,0:T(8,128)(2,1)} collective-permute-done((bf16[2,384,640]{2,1,0:T(8,128)(2,1)S(1)}, bf16[2,384,640]{2,1,0:T(8,128)(2,1)}, u32[]{:S(2)}, u32[]{:S(2)}) %collective-permute-start.6) | collective-permute-done | bytes 983072 | tf_op jit(solution)/shard_map/ppermute | solution.py:69
  174.8 3.6 %pad_maximum_fusion = bf16[4,2,384,640]{3,2,1,0:T(8,128)(2,1)} fusion(bf16[1,2,384,640]{3,2,1,0:T(8,128)(2,1)} %bitcast.26, bf16[1,2,384,640]{3,2,1,0:T(8,128)(2,1)} %bitcast.25, bf16[1,2,384,640]{3,2,1,0:T(8,128)(2,1)} %bitcast.24, bf16[1,2,384,640]{3,2,1,0:T(8,128)(2,1)S(1)} %get-tuple-element.18), kind=kLoop, calls=%fused_computation.20 | loop fusion | flops 5898240 | bytes 7864320 | tf_op jit(solution)/shard_map/stack | solution.py:98
  178.4 5.0 %gather_fusion.3 = bf16[8,384,640]{2,1,0:T(8,128)(2,1)} fusion(bf16[8,384,640]{2,1,0:T(8,128)(2,1)} %bitcast.157, s32[1024]{0:T(1024)S(1)} %pad_clamp_fusion.1), kind=kCustom, calls=%fused_computation.5 | custom fusion | bytes 7864352 | tf_op jit(solution)/shard_map/jit(_take)/gather | solution.py:101
  183.4 3.7 %convert_reduce_fusion = (f32[384]{0:T(512)S(1)}, f32[384]{0:T(512)S(1)}) fusion(bf16[8,384,640]{2,1,0:T(8,128)(2,1)} %gather_fusion.3, pred[8]{0:T(512)(128)(4,1)S(1)} %compare_and_fusion), kind=kLoop, calls=%fused_computation.8 | loop fusion | flops 9829632 | bytes 3935240 | tf_op jit(solution)/shard_map/reduce_sum | solution.py:189
  187.2 6.7 %fusion.3 = bf16[8,384,640]{2,1,0:T(8,128)(2,1)S(1)} fusion(f32[48,8,8,640]{3,2,1,0:T(8,128)} %bitcast.154, f32[48,8,8,640]{3,2,1,0:T(8,128)} %bitcast.153, f32[384]{0:T(512)S(1)} %get-tuple-element.24, f32[384]{0:T(512)S(1)} %get-tuple-element.23, bf16[8,384,640]{2,1,0:T(8,128)(2,1)S(1)} %copy-done.1, pred[8]{0:T(512)(128)(4,1)S(1)} %compare_and_fusion), kind=kLoop, calls=%fused_computation.12 | loop fusion | flops 13762560 | bytes 23596040 | tf_op jit(solution)/shard_map/convert_element_type | solution.py:196
  203.9 2.2 collective-permute-done.10
  206.1 9.8 %convolution_bitcast_fusion.1 = f32[384,864]{0,1:T(8,128)S(1)} fusion(bf16[8,384,640]{2,1,0:T(8,128)(2,1)} %copy-done.4, bf16[8,640,864]{2,1,0:T(8,128)(2,1)} %bitcast.166), kind=kOutput, calls=%fused_computation.37 | convolution fusion | flops 3397386240 | bytes 14106624 | tf_op jit(solution)/shard_map/mtc,mch->th/dot_general | solution.py:208
  215.9 10.5 %all-gather.8.cloned.1.call-done = bf16[864,5120]{0,1:T(8,128)(2,1)} async-done(((bf16[864,320]{0,1:T(8,128)(2,1)}), bf16[864,5120]{0,1:T(8,128)(2,1)}) %all-gather.8.cloned.1.call-update) | async-done | bytes 8847376 | tf_op jit(solution)/shard_map/all_gather | solution.py:128
  226.4 9.2 %convolution_convert_fusion = bf16[384,8,640]{2,0,1:T(8,128)(2,1)} fusion(bf16[864,8,640]{0,2,1:T(8,128)(2,1)} %bitcast.167, f32[384,864]{0,1:T(8,128)S(1)} %convolution_bitcast_fusion.1, bf16[16,16,864]{2,1,0:T(8,128)(2,1)S(1)} %copy-done, bf16[384,16]{0,1:T(8,128)(2,1)S(1)} %add_convert_fusion, bf16[384,16]{0,1:T(8,128)(2,1)S(1)} %get-tuple-element.25), kind=kOutput, calls=%fused_computation.26 | convolution fusion | flops 3572637696 | bytes 14573568 | tf_op jit(solution)/shard_map/th,hmc->mtc/dot_general | solution.py:220
  238.4 3.6 %collective-permute-done.11 = bf16[4,384,640]{2,1,0:T(8,128)(2,1)S(1)} collective-permute-done((bf16[4,384,640]{2,1,0:T(8,128)(2,1)S(1)}, bf16[4,384,640]{2,1,0:T(8,128)(2,1)S(1)}, u32[]{:S(2)}, u32[]{:S(2)}) %collective-permute-start.11) | collective-permute-done | bytes 1966112 | tf_op jit(solution)/shard_map/ppermute | solution.py:69
  242.0 2.4 fusion.83
  246.6 2.4 collective-permute-start.13
  252.9 6.4 %collective-permute-done.12 = bf16[384,640]{1,0:T(8,128)(2,1)S(1)} collective-permute-done((bf16[384,640]{1,0:T(8,128)(2,1)}, bf16[384,640]{1,0:T(8,128)(2,1)S(1)}, u32[]{:S(2)}, u32[]{:S(2)}) %collective-permute-start.12) | collective-permute-done | bytes 491552 | tf_op jit(solution)/shard_map/ppermute | solution.py:69
  259.3 11.5 %collective-permute-done.13 = bf16[384,640]{1,0:T(8,128)(2,1)S(1)} collective-permute-done((bf16[384,640]{1,0:T(8,128)(2,1)}, bf16[384,640]{1,0:T(8,128)(2,1)S(1)}, u32[]{:S(2)}, u32[]{:S(2)}) %collective-permute-start.13) | collective-permute-done | bytes 491552 | tf_op jit(solution)/shard_map/ppermute | solution.py:69
  270.8 2.5 fusion.35
  (114 shorter events, 40.7 us)
Async XLA Ops:
  6.5 219.9 %copy-start = (bf16[16,16,864]{2,1,0:T(8,128)(2,1)S(1)}, bf16[16,16,864]{2,1,0:T(8,128)(2,1)}, u32[]{:S(2)}) copy-start(bf16[16,16,864]{2,1,0:T(8,128)(2,1)} %param.25) | copy-start | bytes 1327108
  6.5 16.4 %copy-start.8 = (s32[16,4]{0,1:T(4,128)S(1)}, s32[16,4]{0,1:T(4,128)}, u32[]{:S(2)}) copy-start(s32[16,4]{0,1:T(4,128)} %param.17) | copy-start | bytes 772
  6.5 17.1 %copy-start.9 = (s32[64]{0:T(128)S(1)}, s32[64]{0:T(128)}, u32[]{:S(2)}) copy-start(s32[64]{0:T(128)} %param.18) | copy-start | bytes 772
  6.5 17.2 %copy-start.10 = (s32[8]{0:T(128)S(1)}, s32[8]{0:T(128)}, u32[]{:S(2)}) copy-start(s32[8]{0:T(128)} %param.19) | copy-start | bytes 100
  6.5 59.5 %all-gather.4.cloned.1.call-start = ((), (), s32[]{:S(2)}) async-start(), calls=%async_computation.2 | async-start | bytes 4177920 | tf_op jit(solution)/shard_map/all_gather | solution.py:126
  7.3 31.5 %copy-start.12 = (bf16[384,16,16]{0,2,1:T(8,128)(2,1)S(1)}, bf16[384,16,16]{0,2,1:T(8,128)(2,1)}, u32[]{:S(2)}) copy-start(bf16[384,16,16]{0,2,1:T(8,128)(2,1)} %param.21) | copy-start | bytes 589828
  7.3 198.8 %all-gather.6.cloned.1.call-start = ((), (), s32[]{:S(2)}) async-start(), calls=%async_computation.3 | async-start | bytes 9748480 | tf_op jit(solution)/shard_map/all_gather | solution.py:127
  8.0 218.4 %all-gather.8.cloned.1.call-start = ((), (), s32[]{:S(2)}) async-start(), calls=%async_computation.4 | async-start | bytes 9748480 | tf_op jit(solution)/shard_map/all_gather | solution.py:128
  14.5 22.1 %all-to-all-start.1 = ((bf16[36,16,384]{2,0,1:T(8,128)(2,1)}), bf16[36,16,384]{2,0,1:T(8,128)(2,1)S(1)}, u32[]{:S(2)}, u32[]{:S(2)}) async-start(bf16[36,16,384]{2,0,1:T(8,128)(2,1)} %copy.91), calls=%async_computation.1 | async-start | bytes 983040 | tf_op jit(solution)/shard_map/all_to_all | solution.py:136
  70.4 2.6 copy-start.2
  70.4 3.6 %copy-start.5 = (bf16[576,640]{1,0:T(8,128)(2,1)S(1)}, bf16[576,640]{1,0:T(8,128)(2,1)}, u32[]{:S(2)}) copy-start(bf16[576,640]{1,0:T(8,128)(2,1)} %param.15) | copy-start | bytes 2211844
  73.0 7.5 %collective-permute-start = (bf16[4,394,640]{2,0,1:T(4,128)(2,1)}, bf16[4,394,640]{2,0,1:T(4,128)(2,1)}, u32[]{:S(2)}, u32[]{:S(2)}) collective-permute-start(bf16[4,394,640]{2,0,1:T(4,128)(2,1)} %copy.98), channel_id=1, source_target_pairs={{0,1},{1,0},{2,3},{3,2},{4,5},{5,4},{6,7},{7,6},{8,9},{9,8},{10,11... | collective-permute-start | bytes 6051848 | tf_op jit(solution)/shard_map/ppermute | solution.py:69
  75.7 26.5 %all-to-all-start = ((bf16[36,16,640]{2,0,1:T(8,128)(2,1)}), bf16[36,16,640]{2,0,1:T(8,128)(2,1)S(1)}, u32[]{:S(2)}, u32[]{:S(2)}) async-start(bf16[36,16,640]{2,0,1:T(8,128)(2,1)} %copy.89), calls=%async_computation | async-start | bytes 1638400 | tf_op jit(solution)/shard_map/all_to_all | solution.py:140
  80.5 10.7 %copy-start.6 = (f32[8,3,5120]{2,0,1:T(8,128)S(1)}, f32[8,3,5120]{2,0,1:T(8,128)}, u32[]{:S(2)}) copy-start(f32[8,3,5120]{2,0,1:T(8,128)} %param.23) | copy-start | bytes 1474564
  86.4 18.4 %collective-permute-start.1 = (bf16[394,640]{1,0:T(8,128)(2,1)}, bf16[394,640]{1,0:T(8,128)(2,1)}, u32[]{:S(2)}, u32[]{:S(2)}) collective-permute-start(bf16[394,640]{1,0:T(8,128)(2,1)} %get-tuple-element.12), channel_id=1, source_target_pairs={{0,2},{1,3},{2,4},{3,5},{4,6},{5,7},{6,0},{7,1},{8,10},{9,11},{10,... | collective-permute-start | bytes 1512968 | tf_op jit(solution)/shard_map/ppermute | solution.py:69
  87.6 25.2 %collective-permute-start.2 = (bf16[394,640]{1,0:T(8,128)(2,1)S(1)}, bf16[394,640]{1,0:T(8,128)(2,1)}, u32[]{:S(2)}, u32[]{:S(2)}) collective-permute-start(bf16[394,640]{1,0:T(8,128)(2,1)S(1)} %get-tuple-element.14), channel_id=1, source_target_pairs={{0,4},{1,5},{2,6},{3,7},{4,0},{5,1},{6,2},{7,3},{8,12},{9,13},{10,... | collective-permute-start | bytes 1512968 | tf_op jit(solution)/shard_map/ppermute | solution.py:69
  90.0 22.8 %collective-permute-start.3 = (bf16[394,640]{1,0:T(8,128)(2,1)S(1)}, bf16[394,640]{1,0:T(8,128)(2,1)}, u32[]{:S(2)}, u32[]{:S(2)}) collective-permute-start(bf16[394,640]{1,0:T(8,128)(2,1)S(1)} %get-tuple-element.13), channel_id=1, source_target_pairs={{0,6},{1,7},{2,0},{3,1},{4,2},{5,3},{6,4},{7,5},{8,14},{9,15},{10,... | collective-permute-start | bytes 1512968 | tf_op jit(solution)/shard_map/ppermute | solution.py:69
  104.8 10.1 %copy-start.7 = (bf16[384,640]{1,0:T(8,128)(2,1)S(1)}, bf16[384,640]{1,0:T(8,128)(2,1)}, u32[]{:S(2)}) copy-start(bf16[384,640]{1,0:T(8,128)(2,1)} %gather_fusion) | copy-start | bytes 1474564
  116.3 12.3 %collective-permute-start.4 = (bf16[384,640]{1,0:T(8,128)(2,1)S(1)}, bf16[384,640]{1,0:T(8,128)(2,1)S(1)}, u32[]{:S(2)}, u32[]{:S(2)}) collective-permute-start(bf16[384,640]{1,0:T(8,128)(2,1)S(1)} %fusion.24), channel_id=1, source_target_pairs={{0,1},{1,0},{2,3},{3,2},{4,5},{5,4},{6,7},{7,6},{8,9},{9,8},{10,11... | collective-permute-start | bytes 1474568 | tf_op jit(solution)/shard_map/ppermute | solution.py:69
  128.8 24.6 %collective-permute-start.5 = (bf16[2,384,640]{2,1,0:T(8,128)(2,1)S(1)}, bf16[2,384,640]{2,1,0:T(8,128)(2,1)}, u32[]{:S(2)}, u32[]{:S(2)}) collective-permute-start(bf16[2,384,640]{2,1,0:T(8,128)(2,1)S(1)} %get-tuple-element.19), channel_id=1, source_target_pairs={{0,2},{1,3},{2,4},{3,5},{4,6},{5,7},{6,0},{7,1},{8,10},{9,11},{10,... | collective-permute-start | bytes 2949128 | tf_op jit(solution)/shard_map/ppermute | solution.py:69
  129.7 45.1 %collective-permute-start.6 = (bf16[2,384,640]{2,1,0:T(8,128)(2,1)S(1)}, bf16[2,384,640]{2,1,0:T(8,128)(2,1)}, u32[]{:S(2)}, u32[]{:S(2)}) collective-permute-start(bf16[2,384,640]{2,1,0:T(8,128)(2,1)S(1)} %get-tuple-element.19), channel_id=1, source_target_pairs={{0,4},{1,5},{2,6},{3,7},{4,0},{5,1},{6,2},{7,3},{8,12},{9,13},{10,... | collective-permute-start | bytes 2949128 | tf_op jit(solution)/shard_map/ppermute | solution.py:69
  131.8 43.0 %collective-permute-start.7 = (bf16[2,384,640]{2,1,0:T(8,128)(2,1)S(1)}, bf16[2,384,640]{2,1,0:T(8,128)(2,1)}, u32[]{:S(2)}, u32[]{:S(2)}) collective-permute-start(bf16[2,384,640]{2,1,0:T(8,128)(2,1)S(1)} %get-tuple-element.19), channel_id=1, source_target_pairs={{0,6},{1,7},{2,0},{3,1},{4,2},{5,3},{6,4},{7,5},{8,14},{9,15},{10,... | collective-permute-start | bytes 2949128 | tf_op jit(solution)/shard_map/ppermute | solution.py:69
  183.4 3.7 %copy-start.1 = (bf16[8,384,640]{2,1,0:T(8,128)(2,1)S(1)}, bf16[8,384,640]{2,1,0:T(8,128)(2,1)}, u32[]{:S(2)}) copy-start(bf16[8,384,640]{2,1,0:T(8,128)(2,1)} %gather_fusion.3) | copy-start | bytes 11796484
  187.2 8.7 %copy-start.11 = (bf16[640,16,16]{0,2,1:T(8,128)(2,1)S(1)}, bf16[640,16,16]{0,2,1:T(8,128)(2,1)}, u32[]{:S(2)}) copy-start(bf16[640,16,16]{0,2,1:T(8,128)(2,1)} %param.24) | copy-start | bytes 983044
  196.2 2.5 collective-permute-start.8
  198.7 3.1 %collective-permute-start.9 = (f32[384,16]{0,1:T(8,128)S(1)}, f32[384,16]{0,1:T(8,128)S(1)}, u32[]{:S(2)}, u32[]{:S(2)}) collective-permute-start(f32[384,16]{0,1:T(8,128)S(1)} %fusion.74), channel_id=1, source_target_pairs={{0,2},{1,3},{2,0},{3,1},{4,6},{5,7},{6,4},{7,5},{8,10},{9,11},{10,... | collective-permute-start | bytes 73736 | tf_op jit(solution)/shard_map/ppermute | solution.py:62
  201.8 4.2 %collective-permute-start.10 = (f32[384,16]{0,1:T(8,128)S(1)}, f32[384,16]{0,1:T(8,128)S(1)}, u32[]{:S(2)}, u32[]{:S(2)}) collective-permute-start(f32[384,16]{0,1:T(8,128)S(1)} %add.383), channel_id=1, source_target_pairs={{0,4},{1,5},{2,6},{3,7},{4,0},{5,1},{6,2},{7,3},{8,12},{9,13},{10,... | collective-permute-start | bytes 73736 | tf_op jit(solution)/shard_map/ppermute | solution.py:62
  235.6 6.4 %copy-start.3 = (bf16[384,8,640]{2,0,1:T(8,128)(2,1)S(1)}, bf16[384,8,640]{2,0,1:T(8,128)(2,1)}, u32[]{:S(2)}) copy-start(bf16[384,8,640]{2,0,1:T(8,128)(2,1)} %convolution_convert_fusion) | copy-start | bytes 11796484
  237.4 4.5 %collective-permute-start.11 = (bf16[4,384,640]{2,1,0:T(8,128)(2,1)S(1)}, bf16[4,384,640]{2,1,0:T(8,128)(2,1)S(1)}, u32[]{:S(2)}, u32[]{:S(2)}) collective-permute-start(bf16[4,384,640]{2,1,0:T(8,128)(2,1)S(1)} %dynamic-slice_bitcast_fusion), channel_id=1, source_target_pairs={{0,1},{1,0},{2,3},{3,2},{4,5},{5,4},{6,7},{7,6},{8,9},{9,8},{10,11... | collective-permute-start | bytes 5898248 | tf_op jit(solution)/shard_map/ppermute | solution.py:69
  245.4 13.8 %collective-permute-start.12 = (bf16[384,640]{1,0:T(8,128)(2,1)}, bf16[384,640]{1,0:T(8,128)(2,1)S(1)}, u32[]{:S(2)}, u32[]{:S(2)}) collective-permute-start(bf16[384,640]{1,0:T(8,128)(2,1)} %get-tuple-element.15), channel_id=1, source_target_pairs={{0,2},{1,3},{2,4},{3,5},{4,6},{5,7},{6,0},{7,1},{8,10},{9,11},{10,... | collective-permute-start | bytes 1474568 | tf_op jit(solution)/shard_map/ppermute | solution.py:69
  246.6 24.1 %collective-permute-start.13 = (bf16[384,640]{1,0:T(8,128)(2,1)}, bf16[384,640]{1,0:T(8,128)(2,1)S(1)}, u32[]{:S(2)}, u32[]{:S(2)}) collective-permute-start(bf16[384,640]{1,0:T(8,128)(2,1)} %get-tuple-element.17), channel_id=1, source_target_pairs={{0,4},{1,5},{2,6},{3,7},{4,0},{5,1},{6,2},{7,3},{8,12},{9,13},{10,... | collective-permute-start | bytes 1474568 | tf_op jit(solution)/shard_map/ppermute | solution.py:69
  249.1 21.7 %collective-permute-start.14 = (bf16[384,640]{1,0:T(8,128)(2,1)S(1)}, bf16[384,640]{1,0:T(8,128)(2,1)}, u32[]{:S(2)}, u32[]{:S(2)}) collective-permute-start(bf16[384,640]{1,0:T(8,128)(2,1)S(1)} %get-tuple-element.16), channel_id=1, source_target_pairs={{0,6},{1,7},{2,0},{3,1},{4,2},{5,3},{6,4},{7,5},{8,14},{9,15},{10,... | collective-permute-start | bytes 1474568 | tf_op jit(solution)/shard_map/ppermute | solution.py:69
  (1 other events, 1.9 us)
Sparse Core Ops, SparseCore 0:
  9.5 56.4 all-gather.3
  68.2 81.9 all-gather.5
  152.3 74.0 all-gather.7
where the time goes:
time: 280 us
  waiting for transfers between devices  127 us (45%)
  other arithmetic  40.1 us (14%)
  starting transfers between devices  35.7 us (13%)
  local copies, waits for them, and re-layouts  35.6 us (13%)
  matrix products  25.4 us (9%)
  between operations  15.5 us (6%)
    ppermute x12, waiting for transfers between devices, mlp_move(): return lax.ppermute(block, 'mlp', [(i, target(i)) for i in range(n)])  60.8 us
    all_gather x1, waiting for transfers between devices, local(): out_w = lax.all_gather(output_weight, 'req', axis=1, tiled=True)  26.5 us
    ppermute x12, starting transfers between devices, mlp_move(): return lax.ppermute(block, 'mlp', [(i, target(i)) for i in range(n)])  17.4 us
    all_to_all x1, waiting for transfers between devices, local(): lax.all_to_all(send_layout(attention_output, offset, req_count), 'req', s...  12.7 us
    all_gather x1, waiting for transfers between devices, local(): down_w = lax.all_gather(down_weight, 'req', axis=1, tiled=True)  10.5 us
    add x1, other arithmetic, local(): 1.0 + scale_rows  10.3 us
    all_to_all x1, waiting for transfers between devices, local(): lax.all_to_all(send_layout(residual_input, offset, req_count), 'req', spl...  10.2 us
    dot_general x1, matrix products, local(): jnp.einsum('mtc,mch->th', normalized, up_w.reshape(mlp_count, width, hidd...  9.79 us
  transfers between devices with their start and end apart: 20, of which 13 were waited for; matrix products, arithmetic and copies ran while one was open for 29% of the time, Pallas kernels for 0%

commit v1 on v0

--- a/solution.py
+++ b/solution.py
@@ -125,7 +125,11 @@
 
     out_w = lax.all_gather(output_weight, "req", axis=1, tiled=True)
     up_w = lax.all_gather(up_weight, "req", axis=0, tiled=True)
-    down_w = lax.all_gather(down_weight, "req", axis=1, tiled=True)
+    split = down_weight.shape[1] // 2
+    down_halves = [
+        lax.all_gather(down_weight[:, :split], "req", axis=1, tiled=True),
+        lax.all_gather(down_weight[:, split:], "req", axis=1, tiled=True),
+    ]
 
     live_rows = jnp.sum(request_length, axis=1)
     dev_ends = jnp.cumsum(live_rows)
@@ -217,15 +221,21 @@
         preferred_element_type=jnp.float32,
     )
     hidden = jax.nn.gelu(hidden_total, approximate=True).astype(jnp.bfloat16)
-    down_terms = jnp.einsum(
-        "th,hmc->mtc",
-        hidden,
-        down_w.reshape(hidden_units, mlp_count, width),
-        preferred_element_type=jnp.float32,
-    ).astype(jnp.bfloat16)
-    down_sum = scatter_mlp(
-        down_terms.reshape((Y_COUNT, mlp_count // Y_COUNT) + down_terms.shape[1:])
-    )
+    sums = []
+    for index in range(len(down_halves)):
+        down_half = down_halves[index]
+        if sums:
+            sums[-1], down_half = lax.optimization_barrier((sums[-1], down_half))
+        down_terms = jnp.einsum(
+            "th,hmjc->mtjc",
+            hidden,
+            down_half.reshape(hidden_units, mlp_count, 2, split),
+            preferred_element_type=jnp.float32,
+        ).astype(jnp.bfloat16)
+        sums.append(
+            scatter_mlp(down_terms.reshape((Y_COUNT, mlp_count // Y_COUNT) + down_terms.shape[1:]))
+        )
+    down_sum = jnp.concatenate(sums, axis=-1).reshape(tok_dev, width)
     result = (values + gate_rows * down_sum).astype(jnp.bfloat16)
     return result.reshape(tok_dev, 1, width)
 

time: 280 us -> 297 us (1.061)
  waiting for transfers between devices: 127 us -> 134 us
  starting transfers between devices: 35.7 us -> 42.1 us
    all_gather x1 -> x2, waiting for transfers between devices: 10.5 us -> 17.8 us  [the longest x1 17.8 us: local(): lax.all_gather(down_weight[:, split:], 'req', axis=1, tiled=True)]
    ppermute x12 -> x16, starting transfers between devices: 17.4 us -> 24 us  [mlp_move(): return lax.ppermute(block, 'mlp', [(i, target(i)) for i in range(n)])]
    unnamed x0 -> x1, matrix products: none -> 4.65 us
    dot_general x1 -> x2, matrix products: 9.15 us -> 5.71 us  [the longest x1 5.01 us: local(): jnp.einsum('th,hmjc->mtjc', hidden, down_half.reshape(hidden_units, mlp_c...]
    ppermute x12 -> x16, waiting for transfers between devices: 60.8 us -> 62.4 us  [mlp_move(): return lax.ppermute(block, 'mlp', [(i, target(i)) for i in range(n)])]
  transfers between devices with their start and end apart: 20 -> 25, of which waited for: 13 -> 17; matrix products, arithmetic and copies ran while one was open for 29% -> 31% of each run, Pallas kernels for 0% -> 0%
where the time goes in v1:
time: 297 us; the launch traced here: 296 us
  waiting for transfers between devices  134 us (45%)
  starting transfers between devices  42.1 us (14%)
  other arithmetic  41.8 us (14%)
  local copies, waits for them, and re-layouts  36 us (12%)
  matrix products  26.4 us (9%)
  between operations  15.7 us (5%)
    ppermute x16, waiting for transfers between devices, mlp_move(): return lax.ppermute(block, 'mlp', [(i, target(i)) for i in range(n)])  62.4 us
    all_gather x1, waiting for transfers between devices, local(): out_w = lax.all_gather(output_weight, 'req', axis=1, tiled=True)  26.8 us
    ppermute x16, starting transfers between devices, mlp_move(): return lax.ppermute(block, 'mlp', [(i, target(i)) for i in range(n)])  24 us
    all_gather x1, waiting for transfers between devices, local(): lax.all_gather(down_weight[:, split:], 'req', axis=1, tiled=True)  17.8 us
    all_to_all x1, waiting for transfers between devices, local(): lax.all_to_all(send_layout(attention_output, offset, req_count), 'req', s...  11.3 us
    add x1, other arithmetic, local(): 1.0 + scale_rows  10.3 us
    dot_general x1, matrix products, local(): jnp.einsum('mtc,mch->th', normalized, up_w.reshape(mlp_count, width, hidd...  9.57 us
    all_to_all x1, waiting for transfers between devices, local(): lax.all_to_all(send_layout(residual_input, offset, req_count), 'req', spl...  9.35 us
  transfers between devices with their start and end apart: 25, of which 17 were waited for; matrix products, arithmetic and copies ran while one was open for 31% of the time, Pallas kernels for 0%

profile of v1, /device:TPU:1, one launch (start us, length us, event | category | flops | bytes accessed | tf_op | source)
XLA Modules:
  0.0 296.2 jit_solution(5655402778367014517)
XLA Ops:
  15.8 8.4 %all-to-all-start.1 = ((bf16[36,16,384]{2,0,1:T(8,128)(2,1)}), bf16[36,16,384]{2,0,1:T(8,128)(2,1)S(1)}, u32[]{:S(2)}, u32[]{:S(2)}) async-start(bf16[36,16,384]{2,0,1:T(8,128)(2,1)} %copy.90), calls=%async_computation.1 | async-start | bytes 983040 | tf_op jit(solution)/shard_map/all_to_all | solution.py:140
  25.2 11.3 %all-to-all-done.1 = bf16[36,16,384]{2,0,1:T(8,128)(2,1)S(1)} async-done(((bf16[36,16,384]{2,0,1:T(8,128)(2,1)}), bf16[36,16,384]{2,0,1:T(8,128)(2,1)S(1)}, u32[]{:S(2)}, u32[]{:S(2)}) %all-to-all-start.1) | async-done | bytes 442400 | tf_op jit(solution)/shard_map/all_to_all | solution.py:140
  39.4 26.8 %all-gather.5.cloned.1.call-done = bf16[384,5120]{0,1:T(8,128)(2,1)} async-done(((bf16[384,320]{0,1:T(8,128)(2,1)}), bf16[384,5120]{0,1:T(8,128)(2,1)}) %all-gather.5.cloned.1.call-update) | async-done | bytes 3932176 | tf_op jit(solution)/shard_map/all_gather | solution.py:126
  66.2 4.4 %convolution_convert_fusion = bf16[384,8,640]{2,0,1:T(8,128)(2,1)S(1)} fusion(bf16[384,8,640]{0,2,1:T(8,128)(2,1)} %bitcast.175, bf16[384,384]{1,0:T(8,128)(2,1)S(1)} %gather_fusion.1, pred[384]{0:T(512)(128)(4,1)S(1)} %compare_and_fusion.2), kind=kOutput, calls=%fused_computation.25 | convolution fusion | flops 1512062976 | bytes 8159616 | tf_op jit(solution)/shard_map/tk,kmc->mtc/dot_general | solution.py:155
  70.8 2.2 copy.97
  75.8 4.7 %all-to-all-start = ((bf16[36,16,640]{2,0,1:T(8,128)(2,1)}), bf16[36,16,640]{2,0,1:T(8,128)(2,1)S(1)}, u32[]{:S(2)}, u32[]{:S(2)}) async-start(bf16[36,16,640]{2,0,1:T(8,128)(2,1)} %copy.88), calls=%async_computation | async-start | bytes 1638400 | tf_op jit(solution)/shard_map/all_to_all | solution.py:144
  81.2 5.1 %convert_add_fusion = (f32[4,394,640]{2,1,0:T(8,128)}, bf16[4,394,640]{2,1,0:T(8,128)(2,1)S(1)}) fusion(s32[]{:T(128)S(6)} %select_n.268, bf16[4,2,10,640]{3,2,0,1:T(8,128)(2,1)S(1)} %broadcast_in_dim.135, bf16[4,394,640]{2,0,1:T(4,128)(2,1)} %collective-permute-done, bf16[4,2,384,640]{3,2,1,0:T(8,128)(2,1)} %bitcast.167), kind=kLoop, calls=%fused_computation.19 | loop fusion | flops 14120960 | bytes 12103684 | tf_op jit(solution)/shard_map/add | solution.py:83
  88.4 2.4 collective-permute-start.2
  92.7 9.3 %all-to-all-done = bf16[36,16,640]{2,0,1:T(8,128)(2,1)S(1)} async-done(((bf16[36,16,640]{2,0,1:T(8,128)(2,1)}), bf16[36,16,640]{2,0,1:T(8,128)(2,1)S(1)}, u32[]{:S(2)}, u32[]{:S(2)}) %all-to-all-start) | async-done | bytes 737312 | tf_op jit(solution)/shard_map/all_to_all | solution.py:144
  102.2 2.6 gather_fusion
  104.8 8.9 %collective-permute-done.2 = bf16[394,640]{1,0:T(8,128)(2,1)} collective-permute-done((bf16[394,640]{1,0:T(8,128)(2,1)S(1)}, bf16[394,640]{1,0:T(8,128)(2,1)}, u32[]{:S(2)}, u32[]{:S(2)}) %collective-permute-start.2) | collective-permute-done | bytes 504352 | tf_op jit(solution)/shard_map/ppermute | solution.py:69
  118.6 5.4 %gather_fusion.4 = f32[384,5120]{1,0:T(8,128)} fusion(f32[8,5120]{1,0:T(8,128)S(1)} %get-tuple-element.33, s32[1024]{0:T(1024)S(1)} %pad_clamp_fusion), kind=kCustom, calls=%fused_computation.clone | custom fusion | bytes 15730176 | tf_op jit(solution)/shard_map/jit(_take)/gather | solution.py:151
  124.0 5.4 %gather_fusion.5 = f32[384,5120]{1,0:T(8,128)} fusion(f32[8,5120]{1,0:T(8,128)S(1)} %get-tuple-element.32, s32[1024]{0:T(1024)S(1)} %pad_clamp_fusion), kind=kCustom, calls=%fused_computation.1.clone | custom fusion | bytes 15730176 | tf_op jit(solution)/shard_map/jit(_take)/gather | solution.py:150
  133.9 10.3 %select_add_fusion = (f32[384,5120]{1,0:T(8,128)}, f32[384,5120]{1,0:T(8,128)}) fusion(f32[384,5120]{1,0:T(8,128)} %gather_fusion.4, pred[384]{0:T(512)(128)(4,1)S(1)} %compare_and_fusion.1, f32[384,5120]{1,0:T(8,128)} %gather_fusion.5), kind=kLoop, calls=%fused_computation.16 | loop fusion | flops 5898240 | bytes 31457664 | tf_op jit(solution)/shard_map/add | solution.py:196
  144.2 10.0 %collective-permute-done.5 = bf16[2,384,640]{2,1,0:T(8,128)(2,1)} collective-permute-done((bf16[2,384,640]{2,1,0:T(8,128)(2,1)S(1)}, bf16[2,384,640]{2,1,0:T(8,128)(2,1)}, u32[]{:S(2)}, u32[]{:S(2)}) %collective-permute-start.5) | collective-permute-done | bytes 983072 | tf_op jit(solution)/shard_map/ppermute | solution.py:69
  154.3 21.3 %collective-permute-done.6 = bf16[2,384,640]{2,1,0:T(8,128)(2,1)} collective-permute-done((bf16[2,384,640]{2,1,0:T(8,128)(2,1)S(1)}, bf16[2,384,640]{2,1,0:T(8,128)(2,1)}, u32[]{:S(2)}, u32[]{:S(2)}) %collective-permute-start.6) | collective-permute-done | bytes 983072 | tf_op jit(solution)/shard_map/ppermute | solution.py:69
  175.7 3.6 %pad_maximum_fusion = bf16[4,2,384,640]{3,2,1,0:T(8,128)(2,1)} fusion(bf16[1,2,384,640]{3,2,1,0:T(8,128)(2,1)} %bitcast.26, bf16[1,2,384,640]{3,2,1,0:T(8,128)(2,1)} %bitcast.25, bf16[1,2,384,640]{3,2,1,0:T(8,128)(2,1)} %bitcast.24, bf16[1,2,384,640]{3,2,1,0:T(8,128)(2,1)S(1)} %get-tuple-element.27), kind=kLoop, calls=%fused_computation.20 | loop fusion | flops 5898240 | bytes 7864320 | tf_op jit(solution)/shard_map/stack | solution.py:98
  179.3 5.0 %gather_fusion.3 = bf16[8,384,640]{2,1,0:T(8,128)(2,1)} fusion(bf16[8,384,640]{2,1,0:T(8,128)(2,1)} %bitcast.172, s32[1024]{0:T(1024)S(1)} %pad_clamp_fusion.1), kind=kCustom, calls=%fused_computation.5 | custom fusion | bytes 7864352 | tf_op jit(solution)/shard_map/jit(_take)/gather | solution.py:101
  184.3 3.7 %convert_reduce_fusion = (f32[384]{0:T(512)S(1)}, f32[384]{0:T(512)S(1)}) fusion(bf16[8,384,640]{2,1,0:T(8,128)(2,1)} %gather_fusion.3, pred[8]{0:T(512)(128)(4,1)S(1)} %compare_and_fusion), kind=kLoop, calls=%fused_computation.8 | loop fusion | flops 9829632 | bytes 3935240 | tf_op jit(solution)/shard_map/reduce_sum | solution.py:193
  188.0 7.0 %fusion.3 = bf16[8,384,640]{2,1,0:T(8,128)(2,1)S(1)} fusion(f32[48,8,8,640]{3,2,1,0:T(8,128)} %bitcast.169, f32[48,8,8,640]{3,2,1,0:T(8,128)} %bitcast.168, f32[384]{0:T(512)S(1)} %get-tuple-element.35, f32[384]{0:T(512)S(1)} %get-tuple-element.34, bf16[8,384,640]{2,1,0:T(8,128)(2,1)S(1)} %copy-done.1, pred[8]{0:T(512)(128)(4,1)S(1)} %compare_and_fusion), kind=kLoop, calls=%fused_computation.12 | loop fusion | flops 13762560 | bytes 23596040 | tf_op jit(solution)/shard_map/convert_element_type | solution.py:200
  202.6 2.2 collective-permute-start.10
  206.8 9.6 %convolution_bitcast_fusion.1 = f32[384,864]{0,1:T(8,128)S(1)} fusion(bf16[8,384,640]{2,1,0:T(8,128)(2,1)} %copy-done.3, bf16[8,640,864]{2,1,0:T(8,128)(2,1)} %bitcast.185), kind=kOutput, calls=%fused_computation.37 | convolution fusion | flops 3397386240 | bytes 14106624 | tf_op jit(solution)/shard_map/mtc,mch->th/dot_general | solution.py:212
  217.1 4.7 %fusion.75 = f32[384,2560]{0,1:S(1)} fusion(bf16[864,2560]{0,1:T(8,128)(2,1)} %all-gather.9.cloned.1.call-done, bf16[384,864]{0,1:T(8,128)(2,1)S(1)} %fusion.17), kind=kOutput, calls=%fused_computation.184 | convolution fusion | flops 1698693120 | bytes 9019392
  222.2 2.2 collective-permute-start.11
  224.4 2.2 collective-permute-done.11
  231.3 4.1 %collective-permute-done.12 = bf16[384,2,160]{0,2,1:T(8,128)(2,1)S(1)} collective-permute-done((bf16[384,2,160]{0,2,1:T(8,128)(2,1)S(1)}, bf16[384,2,160]{0,2,1:T(8,128)(2,1)S(1)}, u32[]{:S(2)}, u32[]{:S(2)}) %collective-permute-start.12) | collective-permute-done | bytes 245792 | tf_op jit(solution)/shard_map/ppermute | solution.py:69
  235.4 6.1 %collective-permute-done.13 = bf16[384,2,160]{0,2,1:T(8,128)(2,1)S(1)} collective-permute-done((bf16[384,2,160]{0,2,1:T(8,128)(2,1)S(1)}, bf16[384,2,160]{0,2,1:T(8,128)(2,1)S(1)}, u32[]{:S(2)}, u32[]{:S(2)}) %collective-permute-start.13) | collective-permute-done | bytes 245792 | tf_op jit(solution)/shard_map/ppermute | solution.py:69
  242.4 17.8 %all-gather.11.cloned.1.call-done = bf16[864,2560]{0,1:T(8,128)(2,1)} async-done(((bf16[864,160]{0,1:T(8,128)(2,1)}), bf16[864,2560]{0,1:T(8,128)(2,1)}) %all-gather.11.cloned.1.call-update) | async-done | bytes 4423696 | tf_op jit(solution)/shard_map/all_gather | solution.py:131
  260.2 5.0 %convolution_convert_fusion.1 = bf16[8,2,160,384]{3,2,1,0:T(8,128)(2,1)S(1)} fusion(bf16[864,8,2,160]{0,3,2,1:T(8,128)(2,1)} %bitcast.186, bf16[384,864]{0,1:T(8,128)(2,1)S(1)} %fusion.17), kind=kOutput, calls=%fused_computation.33 | convolution fusion | flops 1699676160 | bytes 7053312 | tf_op jit(solution)/shard_map/th,hmjc->mtjc/dot_general | solution.py:229
  266.5 2.2 collective-permute-done.15
  271.1 2.4 collective-permute-start.17
  278.6 6.2 %collective-permute-done.17 = bf16[384,2,160]{0,2,1:T(8,128)(2,1)} collective-permute-done((bf16[384,2,160]{0,2,1:T(8,128)(2,1)}, bf16[384,2,160]{0,2,1:T(8,128)(2,1)}, u32[]{:S(2)}, u32[]{:S(2)}) %collective-permute-start.17) | collective-permute-done | bytes 245792 | tf_op jit(solution)/shard_map/ppermute | solution.py:69
  (136 shorter events, 57.7 us)
Async XLA Ops:
  6.5 209.8 %copy-start = (bf16[16,16,864]{2,1,0:T(8,128)(2,1)S(1)}, bf16[16,16,864]{2,1,0:T(8,128)(2,1)}, u32[]{:S(2)}) copy-start(bf16[16,16,864]{2,1,0:T(8,128)(2,1)} %param.25) | copy-start | bytes 1327108
  6.5 17.7 %copy-start.8 = (s32[16,4]{0,1:T(4,128)S(1)}, s32[16,4]{0,1:T(4,128)}, u32[]{:S(2)}) copy-start(s32[16,4]{0,1:T(4,128)} %param.17) | copy-start | bytes 772
  6.5 18.4 %copy-start.9 = (s32[64]{0:T(128)S(1)}, s32[64]{0:T(128)}, u32[]{:S(2)}) copy-start(s32[64]{0:T(128)} %param.18) | copy-start | bytes 772
  6.5 18.5 %copy-start.10 = (s32[8]{0:T(128)S(1)}, s32[8]{0:T(128)}, u32[]{:S(2)}) copy-start(s32[8]{0:T(128)} %param.19) | copy-start | bytes 100
  6.5 59.7 %all-gather.5.cloned.1.call-start = ((), (), s32[]{:S(2)}) async-start(), calls=%async_computation.2 | async-start | bytes 4177920 | tf_op jit(solution)/shard_map/all_gather | solution.py:126
  7.3 199.5 %all-gather.7.cloned.1.call-start = ((), (), s32[]{:S(2)}) async-start(), calls=%async_computation.3 | async-start | bytes 9748480 | tf_op jit(solution)/shard_map/all_gather | solution.py:127
  8.0 30.7 %copy-start.12 = (bf16[384,16,16]{0,2,1:T(8,128)(2,1)S(1)}, bf16[384,16,16]{0,2,1:T(8,128)(2,1)}, u32[]{:S(2)}) copy-start(bf16[384,16,16]{0,2,1:T(8,128)(2,1)} %param.21) | copy-start | bytes 589828
  8.0 209.1 %all-gather.9.cloned.1.call-start = ((), (), s32[]{:S(2)}) async-start(), calls=%async_computation.4 | async-start | bytes 4874240 | tf_op jit(solution)/shard_map/all_gather | solution.py:130
  15.8 20.7 %all-to-all-start.1 = ((bf16[36,16,384]{2,0,1:T(8,128)(2,1)}), bf16[36,16,384]{2,0,1:T(8,128)(2,1)S(1)}, u32[]{:S(2)}, u32[]{:S(2)}) async-start(bf16[36,16,384]{2,0,1:T(8,128)(2,1)} %copy.90), calls=%async_computation.1 | async-start | bytes 983040 | tf_op jit(solution)/shard_map/all_to_all | solution.py:140
  73.1 8.1 %collective-permute-start = (bf16[4,394,640]{2,0,1:T(4,128)(2,1)}, bf16[4,394,640]{2,0,1:T(4,128)(2,1)}, u32[]{:S(2)}, u32[]{:S(2)}) collective-permute-start(bf16[4,394,640]{2,0,1:T(4,128)(2,1)} %copy.97), channel_id=1, source_target_pairs={{0,1},{1,0},{2,3},{3,2},{4,5},{5,4},{6,7},{7,6},{8,9},{9,8},{10,11... | collective-permute-start | bytes 6051848 | tf_op jit(solution)/shard_map/ppermute | solution.py:69
  75.8 26.3 %all-to-all-start = ((bf16[36,16,640]{2,0,1:T(8,128)(2,1)}), bf16[36,16,640]{2,0,1:T(8,128)(2,1)S(1)}, u32[]{:S(2)}, u32[]{:S(2)}) async-start(bf16[36,16,640]{2,0,1:T(8,128)(2,1)} %copy.88), calls=%async_computation | async-start | bytes 1638400 | tf_op jit(solution)/shard_map/all_to_all | solution.py:144
  80.5 179.7 %all-gather.11.cloned.1.call-start = ((), (), s32[]{:S(2)}) async-start(), calls=%async_computation.5 | async-start | bytes 4874240 | tf_op jit(solution)/shard_map/all_gather | solution.py:131
  87.2 17.6 %collective-permute-start.1 = (bf16[394,640]{1,0:T(8,128)(2,1)}, bf16[394,640]{1,0:T(8,128)(2,1)}, u32[]{:S(2)}, u32[]{:S(2)}) collective-permute-start(bf16[394,640]{1,0:T(8,128)(2,1)} %get-tuple-element.18), channel_id=1, source_target_pairs={{0,2},{1,3},{2,4},{3,5},{4,6},{5,7},{6,0},{7,1},{8,10},{9,11},{10,... | collective-permute-start | bytes 1512968 | tf_op jit(solution)/shard_map/ppermute | solution.py:69
  88.4 25.3 %collective-permute-start.2 = (bf16[394,640]{1,0:T(8,128)(2,1)S(1)}, bf16[394,640]{1,0:T(8,128)(2,1)}, u32[]{:S(2)}, u32[]{:S(2)}) collective-permute-start(bf16[394,640]{1,0:T(8,128)(2,1)S(1)} %get-tuple-element.20), channel_id=1, source_target_pairs={{0,4},{1,5},{2,6},{3,7},{4,0},{5,1},{6,2},{7,3},{8,12},{9,13},{10,... | collective-permute-start | bytes 1512968 | tf_op jit(solution)/shard_map/ppermute | solution.py:69
  90.9 22.8 %collective-permute-start.3 = (bf16[394,640]{1,0:T(8,128)(2,1)S(1)}, bf16[394,640]{1,0:T(8,128)(2,1)}, u32[]{:S(2)}, u32[]{:S(2)}) collective-permute-start(bf16[394,640]{1,0:T(8,128)(2,1)S(1)} %get-tuple-element.19), channel_id=1, source_target_pairs={{0,6},{1,7},{2,0},{3,1},{4,2},{5,3},{6,4},{7,5},{8,14},{9,15},{10,... | collective-permute-start | bytes 1512968 | tf_op jit(solution)/shard_map/ppermute | solution.py:69
  104.8 11.1 %copy-start.7 = (bf16[384,640]{1,0:T(8,128)(2,1)S(1)}, bf16[384,640]{1,0:T(8,128)(2,1)}, u32[]{:S(2)}) copy-start(bf16[384,640]{1,0:T(8,128)(2,1)} %gather_fusion) | copy-start | bytes 1474564
  117.2 12.2 %copy-start.4 = (bf16[384,640]{1,0:T(8,128)(2,1)}, bf16[384,640]{1,0:T(8,128)(2,1)S(1)}, u32[]{:S(2)}) copy-start(bf16[384,640]{1,0:T(8,128)(2,1)S(1)} %fusion.23) | copy-start | bytes 1474564
  117.2 12.2 %collective-permute-start.4 = (bf16[384,640]{1,0:T(8,128)(2,1)S(1)}, bf16[384,640]{1,0:T(8,128)(2,1)S(1)}, u32[]{:S(2)}, u32[]{:S(2)}) collective-permute-start(bf16[384,640]{1,0:T(8,128)(2,1)S(1)} %fusion.23), channel_id=1, source_target_pairs={{0,1},{1,0},{2,3},{3,2},{4,5},{5,4},{6,7},{7,6},{8,9},{9,8},{10,11... | collective-permute-start | bytes 1474568 | tf_op jit(solution)/shard_map/ppermute | solution.py:69
  129.6 24.7 %collective-permute-start.5 = (bf16[2,384,640]{2,1,0:T(8,128)(2,1)S(1)}, bf16[2,384,640]{2,1,0:T(8,128)(2,1)}, u32[]{:S(2)}, u32[]{:S(2)}) collective-permute-start(bf16[2,384,640]{2,1,0:T(8,128)(2,1)S(1)} %get-tuple-element.28), channel_id=1, source_target_pairs={{0,2},{1,3},{2,4},{3,5},{4,6},{5,7},{6,0},{7,1},{8,10},{9,11},{10,... | collective-permute-start | bytes 2949128 | tf_op jit(solution)/shard_map/ppermute | solution.py:69
  130.5 45.0 %collective-permute-start.6 = (bf16[2,384,640]{2,1,0:T(8,128)(2,1)S(1)}, bf16[2,384,640]{2,1,0:T(8,128)(2,1)}, u32[]{:S(2)}, u32[]{:S(2)}) collective-permute-start(bf16[2,384,640]{2,1,0:T(8,128)(2,1)S(1)} %get-tuple-element.28), channel_id=1, source_target_pairs={{0,4},{1,5},{2,6},{3,7},{4,0},{5,1},{6,2},{7,3},{8,12},{9,13},{10,... | collective-permute-start | bytes 2949128 | tf_op jit(solution)/shard_map/ppermute | solution.py:69
  132.6 43.1 %collective-permute-start.7 = (bf16[2,384,640]{2,1,0:T(8,128)(2,1)S(1)}, bf16[2,384,640]{2,1,0:T(8,128)(2,1)}, u32[]{:S(2)}, u32[]{:S(2)}) collective-permute-start(bf16[2,384,640]{2,1,0:T(8,128)(2,1)S(1)} %get-tuple-element.28), channel_id=1, source_target_pairs={{0,6},{1,7},{2,0},{3,1},{4,2},{5,3},{6,4},{7,5},{8,14},{9,15},{10,... | collective-permute-start | bytes 2949128 | tf_op jit(solution)/shard_map/ppermute | solution.py:69
  197.4 2.1 collective-permute-start.8
  199.5 3.1 %collective-permute-start.9 = (f32[384,16]{0,1:T(8,128)S(1)}, f32[384,16]{0,1:T(8,128)S(1)}, u32[]{:S(2)}, u32[]{:S(2)}) collective-permute-start(f32[384,16]{0,1:T(8,128)S(1)} %fusion.66), channel_id=1, source_target_pairs={{0,2},{1,3},{2,0},{3,1},{4,6},{5,7},{6,4},{7,5},{8,10},{9,11},{10,... | collective-permute-start | bytes 73736 | tf_op jit(solution)/shard_map/ppermute | solution.py:62
  202.6 4.2 %collective-permute-start.10 = (f32[384,16]{0,1:T(8,128)S(1)}, f32[384,16]{0,1:T(8,128)S(1)}, u32[]{:S(2)}, u32[]{:S(2)}) collective-permute-start(f32[384,16]{0,1:T(8,128)S(1)} %add.408), channel_id=1, source_target_pairs={{0,4},{1,5},{2,6},{3,7},{4,0},{5,1},{6,2},{7,3},{8,12},{9,13},{10,... | collective-permute-start | bytes 73736 | tf_op jit(solution)/shard_map/ppermute | solution.py:62
  222.2 4.4 %collective-permute-start.11 = (bf16[4,384,2,160]{1,3,2,0:T(8,128)(2,1)S(1)}, bf16[4,384,2,160]{1,3,2,0:T(8,128)(2,1)S(1)}, u32[]{:S(2)}, u32[]{:S(2)}) collective-permute-start(bf16[4,384,2,160]{1,3,2,0:T(8,128)(2,1)S(1)} %dynamic-slice_bitcast_fusion.1), channel_id=1, source_target_pairs={{0,1},{1,0},{2,3},{3,2},{4,5},{5,4},{6,7},{7,6},{8,9},{9,8},{10,11... | collective-permute-start | bytes 2949128 | tf_op jit(solution)/shard_map/ppermute | solution.py:69
  227.0 8.4 %collective-permute-start.12 = (bf16[384,2,160]{0,2,1:T(8,128)(2,1)S(1)}, bf16[384,2,160]{0,2,1:T(8,128)(2,1)S(1)}, u32[]{:S(2)}, u32[]{:S(2)}) collective-permute-start(bf16[384,2,160]{0,2,1:T(8,128)(2,1)S(1)} %get-tuple-element.24), channel_id=1, source_target_pairs={{0,2},{1,3},{2,4},{3,5},{4,6},{5,7},{6,0},{7,1},{8,10},{9,11},{10,... | collective-permute-start | bytes 737288 | tf_op jit(solution)/shard_map/ppermute | solution.py:69
  228.5 13.0 %collective-permute-start.13 = (bf16[384,2,160]{0,2,1:T(8,128)(2,1)S(1)}, bf16[384,2,160]{0,2,1:T(8,128)(2,1)S(1)}, u32[]{:S(2)}, u32[]{:S(2)}) collective-permute-start(bf16[384,2,160]{0,2,1:T(8,128)(2,1)S(1)} %get-tuple-element.26), channel_id=1, source_target_pairs={{0,4},{1,5},{2,6},{3,7},{4,0},{5,1},{6,2},{7,3},{8,12},{9,13},{10,... | collective-permute-start | bytes 737288 | tf_op jit(solution)/shard_map/ppermute | solution.py:69
  230.6 10.9 %collective-permute-start.14 = (bf16[384,2,160]{0,2,1:T(8,128)(2,1)S(1)}, bf16[384,2,160]{0,2,1:T(8,128)(2,1)S(1)}, u32[]{:S(2)}, u32[]{:S(2)}) collective-permute-start(bf16[384,2,160]{0,2,1:T(8,128)(2,1)S(1)} %get-tuple-element.25), channel_id=1, source_target_pairs={{0,6},{1,7},{2,0},{3,1},{4,2},{5,3},{6,4},{7,5},{8,14},{9,15},{10,... | collective-permute-start | bytes 737288 | tf_op jit(solution)/shard_map/ppermute | solution.py:69
  265.4 3.4 %collective-permute-start.15 = (bf16[4,384,2,160]{1,3,2,0:T(8,128)(2,1)S(1)}, bf16[4,384,2,160]{1,3,2,0:T(8,128)(2,1)S(1)}, u32[]{:S(2)}, u32[]{:S(2)}) collective-permute-start(bf16[4,384,2,160]{1,3,2,0:T(8,128)(2,1)S(1)} %dynamic-slice_bitcast_fusion), channel_id=1, source_target_pairs={{0,1},{1,0},{2,3},{3,2},{4,5},{5,4},{6,7},{7,6},{8,9},{9,8},{10,11... | collective-permute-start | bytes 2949128 | tf_op jit(solution)/shard_map/ppermute | solution.py:69
  269.9 8.7 %collective-permute-start.16 = (bf16[384,2,160]{0,2,1:T(8,128)(2,1)}, bf16[384,2,160]{0,2,1:T(8,128)(2,1)}, u32[]{:S(2)}, u32[]{:S(2)}) collective-permute-start(bf16[384,2,160]{0,2,1:T(8,128)(2,1)} %get-tuple-element.21), channel_id=1, source_target_pairs={{0,2},{1,3},{2,4},{3,5},{4,6},{5,7},{6,0},{7,1},{8,10},{9,11},{10,... | collective-permute-start | bytes 737288 | tf_op jit(solution)/shard_map/ppermute | solution.py:69
  271.1 13.7 %collective-permute-start.17 = (bf16[384,2,160]{0,2,1:T(8,128)(2,1)}, bf16[384,2,160]{0,2,1:T(8,128)(2,1)}, u32[]{:S(2)}, u32[]{:S(2)}) collective-permute-start(bf16[384,2,160]{0,2,1:T(8,128)(2,1)} %get-tuple-element.23), channel_id=1, source_target_pairs={{0,4},{1,5},{2,6},{3,7},{4,0},{5,1},{6,2},{7,3},{8,12},{9,13},{10,... | collective-permute-start | bytes 737288 | tf_op jit(solution)/shard_map/ppermute | solution.py:69
  273.6 11.3 %collective-permute-start.18 = (bf16[384,2,160]{0,2,1:T(8,128)(2,1)}, bf16[384,2,160]{0,2,1:T(8,128)(2,1)}, u32[]{:S(2)}, u32[]{:S(2)}) collective-permute-start(bf16[384,2,160]{0,2,1:T(8,128)(2,1)} %get-tuple-element.22), channel_id=1, source_target_pairs={{0,6},{1,7},{2,0},{3,1},{4,2},{5,3},{6,4},{7,5},{8,14},{9,15},{10,... | collective-permute-start | bytes 737288 | tf_op jit(solution)/shard_map/ppermute | solution.py:69
  (6 other events, 31.6 us)
Sparse Core Ops, SparseCore 0:
  9.5 56.7 all-gather.4
  68.4 81.9 all-gather.6
  152.5 52.7 all-gather.8
  207.3 52.8 all-gather.10

commit v2 on v0

--- a/solution.py
+++ b/solution.py
@@ -124,8 +124,10 @@
     head_width = attention_output.shape[1]
 
     out_w = lax.all_gather(output_weight, "req", axis=1, tiled=True)
-    up_w = lax.all_gather(up_weight, "req", axis=0, tiled=True)
-    down_w = lax.all_gather(down_weight, "req", axis=1, tiled=True)
+    both = jnp.stack([up_weight, down_weight.T], axis=0)
+    both = lax.all_gather(both, "req", axis=1, tiled=True)
+    up_w = both[0]
+    down_t = both[1]
 
     live_rows = jnp.sum(request_length, axis=1)
     dev_ends = jnp.cumsum(live_rows)
@@ -218,9 +220,9 @@
     )
     hidden = jax.nn.gelu(hidden_total, approximate=True).astype(jnp.bfloat16)
     down_terms = jnp.einsum(
-        "th,hmc->mtc",
+        "th,mch->mtc",
         hidden,
-        down_w.reshape(hidden_units, mlp_count, width),
+        down_t.reshape(mlp_count, width, hidden_units),
         preferred_element_type=jnp.float32,
     ).astype(jnp.bfloat16)
     down_sum = scatter_mlp(

time: 280 us -> 285 us (1.018)
  local copies, waits for them, and re-layouts: 35.6 us -> 53.9 us
  waiting for transfers between devices: 127 us -> 113 us
  matrix products: 25.4 us -> 21.4 us
  other arithmetic: 40.1 us -> 43.4 us
    slice x0 -> x1, local copies, waits for them, and re-layouts: none -> 11.6 us  [local(): up_w = both[0]]
    all_gather x2 -> x1, waiting for transfers between devices: 10.5 us -> 0.01 us  [local(): both = lax.all_gather(both, 'req', axis=1, tiled=True)]
    dynamic_slice x0 -> x2, local copies, waits for them, and re-layouts: none -> 6.29 us  [the longest x1 3.86 us: scatter_mlp(): mine = lax.dynamic_index_in_dim(payload, core, 1, keepdims=False)]
    dot_general x1, matrix products: 9.79 us -> 4.77 us  [local(): jnp.einsum('mtc,mch->th', normalized, up_w.reshape(mlp_count, width, hidd...]
    ppermute x12, waiting for transfers between devices: 60.8 us -> 56.4 us  [mlp_move(): return lax.ppermute(block, 'mlp', [(i, target(i)) for i in range(n)])]
    add x1 -> x2, other arithmetic: 4.92 us -> 8.77 us  [scatter_mlp(): mine.astype(jnp.float32)]
  transfers between devices with their start and end apart: 20 -> 19, of which waited for: 13 -> 12; matrix products, arithmetic and copies ran while one was open for 29% -> 27% of each run, Pallas kernels for 0% -> 0%
where the time goes in v2:
time: 285 us
  waiting for transfers between devices  113 us (40%)
  local copies, waits for them, and re-layouts  53.9 us (19%)
  other arithmetic  43.4 us (15%)
  starting transfers between devices  37.4 us (13%)
  matrix products  21.4 us (8%)
  between operations  15.9 us (6%)
    ppermute x12, waiting for transfers between devices, mlp_move(): return lax.ppermute(block, 'mlp', [(i, target(i)) for i in range(n)])  56.4 us
    all_gather x1, waiting for transfers between devices, local(): out_w = lax.all_gather(output_weight, 'req', axis=1, tiled=True)  26.6 us
    ppermute x12, starting transfers between devices, mlp_move(): return lax.ppermute(block, 'mlp', [(i, target(i)) for i in range(n)])  19.2 us
    all_to_all x1, waiting for transfers between devices, local(): lax.all_to_all(send_layout(attention_output, offset, req_count), 'req', s...  12.7 us
    all_to_all x1, waiting for transfers between devices, local(): lax.all_to_all(send_layout(residual_input, offset, req_count), 'req', spl...  12.3 us
    slice x1, local copies, waits for them, and re-layouts, local(): up_w = both[0]  11.6 us
    add x1, other arithmetic, local(): 1.0 + scale_rows  10.6 us
    dot_general x1, matrix products, local(): jnp.einsum('th,mch->mtc', hidden, down_t.reshape(mlp_count, width, hidden...  10.1 us
  transfers between devices with their start and end apart: 19, of which 12 were waited for; matrix products, arithmetic and copies ran while one was open for 27% of the time, Pallas kernels for 0%

profile of v2, /device:TPU:1, one launch (start us, length us, event | category | flops | bytes accessed | tf_op | source)
XLA Modules:
  0.0 284.5 jit_solution(4044587420654296451)
XLA Ops:
  7.3 2.4 pad_maximum_fusion.1
  14.5 8.4 %all-to-all-start.1 = ((bf16[36,16,384]{2,0,1:T(8,128)(2,1)}), bf16[36,16,384]{2,0,1:T(8,128)(2,1)S(1)}, u32[]{:S(2)}, u32[]{:S(2)}) async-start(bf16[36,16,384]{2,0,1:T(8,128)(2,1)} %copy.96), calls=%async_computation.1 | async-start | bytes 983040 | tf_op jit(solution)/shard_map/all_to_all | solution.py:138
  23.9 12.7 %all-to-all-done.1 = bf16[36,16,384]{2,0,1:T(8,128)(2,1)S(1)} async-done(((bf16[36,16,384]{2,0,1:T(8,128)(2,1)}), bf16[36,16,384]{2,0,1:T(8,128)(2,1)S(1)}, u32[]{:S(2)}, u32[]{:S(2)}) %all-to-all-start.1) | async-done | bytes 442400 | tf_op jit(solution)/shard_map/all_to_all | solution.py:138
  39.5 26.6 %all-gather.3.cloned.1.call-done = bf16[384,5120]{0,1:T(8,128)(2,1)} async-done(((bf16[384,320]{0,1:T(8,128)(2,1)}), bf16[384,5120]{0,1:T(8,128)(2,1)}) %all-gather.3.cloned.1.call-update) | async-done | bytes 3932176 | tf_op jit(solution)/shard_map/all_gather | solution.py:126
  66.1 4.4 %convolution_convert_fusion.1 = bf16[384,8,640]{2,0,1:T(8,128)(2,1)S(1)} fusion(bf16[384,8,640]{0,2,1:T(8,128)(2,1)} %bitcast.162, bf16[384,384]{1,0:T(8,128)(2,1)S(1)} %gather_fusion.1, pred[384]{0:T(512)(128)(4,1)S(1)} %compare_and_fusion.2), kind=kOutput, calls=%fused_computation.27 | convolution fusion | flops 1512062976 | bytes 8159616 | tf_op jit(solution)/shard_map/tk,kmc->mtc/dot_general | solution.py:153
  70.7 2.3 copy.103
  75.7 4.7 %all-to-all-start = ((bf16[36,16,640]{2,0,1:T(8,128)(2,1)}), bf16[36,16,640]{2,0,1:T(8,128)(2,1)S(1)}, u32[]{:S(2)}, u32[]{:S(2)}) async-start(bf16[36,16,640]{2,0,1:T(8,128)(2,1)} %copy.94), calls=%async_computation | async-start | bytes 1638400 | tf_op jit(solution)/shard_map/all_to_all | solution.py:142
  80.5 4.9 %convert_add_fusion = (f32[4,394,640]{2,1,0:T(8,128)}, bf16[4,394,640]{2,1,0:T(8,128)(2,1)S(1)}) fusion(s32[]{:T(128)S(6)} %select_n.253, bf16[4,2,10,640]{3,2,0,1:T(8,128)(2,1)S(1)} %broadcast_in_dim.135, bf16[4,394,640]{2,0,1:T(4,128)(2,1)} %collective-permute-done, bf16[4,2,384,640]{3,2,1,0:T(8,128)(2,1)} %bitcast.154), kind=kLoop, calls=%fused_computation.19 | loop fusion | flops 14120960 | bytes 12103684 | tf_op jit(solution)/shard_map/add | solution.py:83
  87.7 2.4 collective-permute-start.2
  91.9 12.3 %all-to-all-done = bf16[36,16,640]{2,0,1:T(8,128)(2,1)S(1)} async-done(((bf16[36,16,640]{2,0,1:T(8,128)(2,1)}), bf16[36,16,640]{2,0,1:T(8,128)(2,1)S(1)}, u32[]{:S(2)}, u32[]{:S(2)}) %all-to-all-start) | async-done | bytes 737312 | tf_op jit(solution)/shard_map/all_to_all | solution.py:142
  106.5 6.3 %collective-permute-done.2 = bf16[394,640]{1,0:T(8,128)(2,1)} collective-permute-done((bf16[394,640]{1,0:T(8,128)(2,1)S(1)}, bf16[394,640]{1,0:T(8,128)(2,1)}, u32[]{:S(2)}, u32[]{:S(2)}) %collective-permute-start.2) | collective-permute-done | bytes 504352 | tf_op jit(solution)/shard_map/ppermute | solution.py:69
  117.8 5.4 %gather_fusion.4 = f32[384,5120]{1,0:T(8,128)} fusion(f32[8,5120]{1,0:T(8,128)S(1)} %get-tuple-element.26, s32[1024]{0:T(1024)S(1)} %pad_clamp_fusion), kind=kCustom, calls=%fused_computation.clone | custom fusion | bytes 15730176 | tf_op jit(solution)/shard_map/jit(_take)/gather | solution.py:149
  123.2 5.5 %gather_fusion.5 = f32[384,5120]{1,0:T(8,128)} fusion(f32[8,5120]{1,0:T(8,128)S(1)} %get-tuple-element.25, s32[1024]{0:T(1024)S(1)} %pad_clamp_fusion), kind=kCustom, calls=%fused_computation.1.clone | custom fusion | bytes 15730176 | tf_op jit(solution)/shard_map/jit(_take)/gather | solution.py:148
  133.5 10.6 %select_add_fusion = (f32[384,5120]{1,0:T(8,128)}, f32[384,5120]{1,0:T(8,128)}) fusion(f32[384,5120]{1,0:T(8,128)} %gather_fusion.4, pred[384]{0:T(512)(128)(4,1)S(1)} %compare_and_fusion.1, f32[384,5120]{1,0:T(8,128)} %gather_fusion.5), kind=kLoop, calls=%fused_computation.16 | loop fusion | flops 5898240 | bytes 31457664 | tf_op jit(solution)/shard_map/add | solution.py:194
  144.2 9.1 %collective-permute-done.5 = bf16[2,384,640]{2,1,0:T(8,128)(2,1)} collective-permute-done((bf16[2,384,640]{2,1,0:T(8,128)(2,1)S(1)}, bf16[2,384,640]{2,1,0:T(8,128)(2,1)}, u32[]{:S(2)}, u32[]{:S(2)}) %collective-permute-start.5) | collective-permute-done | bytes 983072 | tf_op jit(solution)/shard_map/ppermute | solution.py:69
  153.3 21.8 %collective-permute-done.6 = bf16[2,384,640]{2,1,0:T(8,128)(2,1)} collective-permute-done((bf16[2,384,640]{2,1,0:T(8,128)(2,1)S(1)}, bf16[2,384,640]{2,1,0:T(8,128)(2,1)}, u32[]{:S(2)}, u32[]{:S(2)}) %collective-permute-start.6) | collective-permute-done | bytes 983072 | tf_op jit(solution)/shard_map/ppermute | solution.py:69
  175.1 3.6 %pad_maximum_fusion = bf16[4,2,384,640]{3,2,1,0:T(8,128)(2,1)} fusion(bf16[1,2,384,640]{3,2,1,0:T(8,128)(2,1)} %bitcast.30, bf16[1,2,384,640]{3,2,1,0:T(8,128)(2,1)} %bitcast.29, bf16[1,2,384,640]{3,2,1,0:T(8,128)(2,1)} %bitcast.28, bf16[1,2,384,640]{3,2,1,0:T(8,128)(2,1)S(1)} %get-tuple-element.22), kind=kLoop, calls=%fused_computation.20 | loop fusion | flops 5898240 | bytes 7864320 | tf_op jit(solution)/shard_map/stack | solution.py:98
  178.7 5.0 %gather_fusion.3 = bf16[8,384,640]{2,1,0:T(8,128)(2,1)} fusion(bf16[8,384,640]{2,1,0:T(8,128)(2,1)} %bitcast.159, s32[1024]{0:T(1024)S(1)} %pad_clamp_fusion.1), kind=kCustom, calls=%fused_computation.5 | custom fusion | bytes 7864352 | tf_op jit(solution)/shard_map/jit(_take)/gather | solution.py:101
  183.7 3.7 %convert_reduce_fusion = (f32[384]{0:T(512)S(1)}, f32[384]{0:T(512)S(1)}) fusion(bf16[8,384,640]{2,1,0:T(8,128)(2,1)} %gather_fusion.3, pred[8]{0:T(512)(128)(4,1)S(1)} %compare_and_fusion), kind=kLoop, calls=%fused_computation.8 | loop fusion | flops 9829632 | bytes 3935240 | tf_op jit(solution)/shard_map/reduce_sum | solution.py:191
  187.5 6.7 %fusion.3 = bf16[8,384,640]{2,1,0:T(8,128)(2,1)S(1)} fusion(f32[48,8,8,640]{3,2,1,0:T(8,128)} %bitcast.156, f32[48,8,8,640]{3,2,1,0:T(8,128)} %bitcast.155, f32[384]{0:T(512)S(1)} %get-tuple-element.28, f32[384]{0:T(512)S(1)} %get-tuple-element.27, bf16[8,384,640]{2,1,0:T(8,128)(2,1)S(1)} %copy-done.1, pred[8]{0:T(512)(128)(4,1)S(1)} %compare_and_fusion), kind=kLoop, calls=%fused_computation.12 | loop fusion | flops 13762560 | bytes 23596040 | tf_op jit(solution)/shard_map/convert_element_type | solution.py:198
  201.3 2.5 collective-permute-start.10
  205.5 11.6 %fusion.84 = (bf16[1,5120,864]{2,1,0:T(8,128)(2,1)S(1)}, bf16[1,5120,864]{2,1,0:T(8,128)(2,1)}) fusion(bf16[2,5120,864]{2,1,0:T(8,128)(2,1)} %all-gather.5.cloned.1.call-done), kind=kLoop, calls=%fused_computation.184 | loop fusion | bytes 35389440 | tf_op jit(solution)/shard_map/slice | solution.py:129
  217.0 4.8 %convolution_bitcast_fusion.1 = f32[384,864]{0,1:T(8,128)S(1)} fusion(bf16[8,384,640]{2,1,0:T(8,128)(2,1)S(1)} %copy-done.4, bf16[8,640,864]{2,1,0:T(8,128)(2,1)S(1)} %bitcast.161), kind=kOutput, calls=%fused_computation.36 | convolution fusion | flops 3397386240 | bytes 14106624 | tf_op jit(solution)/shard_map/mtc,mch->th/dot_general | solution.py:210
  221.8 10.1 %convolution_convert_fusion = bf16[8,640,384]{2,1,0:T(8,128)(2,1)} fusion(bf16[8,640,864]{2,1,0:T(8,128)(2,1)} %bitcast.160, f32[384,864]{0,1:T(8,128)S(1)} %convolution_bitcast_fusion.1, bf16[16,16,864]{2,1,0:T(8,128)(2,1)S(1)} %copy-done, bf16[384,16]{0,1:T(8,128)(2,1)S(1)} %add_convert_fusion, bf16[384,16]{0,1:T(8,128)(2,1)S(1)} %get-tuple-element.29), kind=kOutput, calls=%fused_computation.26 | convolution fusion | flops 3572637696 | bytes 14573568 | tf_op jit(solution)/shard_map/th,mch->mtc/dot_general | solution.py:222
  232.0 3.9 %constant_dynamic-slice_fusion.1 = (bf16[4,1,384,640]{2,3,1,0:T(8,128)(2,1)}, bf16[4,1,384,640]{2,3,1,0:T(8,128)(2,1)S(1)}) fusion(bf16[4,2,384,640]{2,3,1,0:T(8,128)(2,1)} %bitcast.163, s32[]{:T(128)S(6)} %select_n.253, s32[]{:T(128)S(6)} %select_n.254), kind=kLoop, calls=%fused_computation.118 | loop fusion | bytes 7864328 | tf_op jit(solution)/shard_map/jit(dynamic_index_in_dim)/dynamic_slice | solution.py:81
  235.8 2.4 copy.113
  238.3 2.6 collective-permute-start.11
  240.9 2.8 copy.119
  244.8 3.9 %convert_add_fusion.1 = (f32[4,384,640]{2,1,0:T(8,128)}, bf16[4,384,640]{2,1,0:T(8,128)(2,1)S(1)}) fusion(bf16[4,384,640]{2,1,0:T(8,128)(2,1)} %collective-permute-done.11, bf16[4,1,384,640]{3,2,0,1:T(8,128)(2,1)S(1)} %copy.119), kind=kLoop, calls=%fused_computation.21 | loop fusion | flops 3932160 | bytes 9830400 | tf_op jit(solution)/shard_map/add | solution.py:83
  257.0 6.6 %collective-permute-done.12 = bf16[384,640]{1,0:T(8,128)(2,1)S(1)} collective-permute-done((bf16[384,640]{1,0:T(8,128)(2,1)}, bf16[384,640]{1,0:T(8,128)(2,1)S(1)}, u32[]{:S(2)}, u32[]{:S(2)}) %collective-permute-start.12) | collective-permute-done | bytes 491552 | tf_op jit(solution)/shard_map/ppermute | solution.py:69
  263.6 11.4 %collective-permute-done.13 = bf16[384,640]{1,0:T(8,128)(2,1)} collective-permute-done((bf16[384,640]{1,0:T(8,128)(2,1)}, bf16[384,640]{1,0:T(8,128)(2,1)}, u32[]{:S(2)}, u32[]{:S(2)}) %collective-permute-start.13) | collective-permute-done | bytes 491552 | tf_op jit(solution)/shard_map/ppermute | solution.py:69
  275.0 2.7 fusion.35
  (115 shorter events, 44.6 us)
Async XLA Ops:
  6.5 215.3 %copy-start = (bf16[16,16,864]{2,1,0:T(8,128)(2,1)S(1)}, bf16[16,16,864]{2,1,0:T(8,128)(2,1)}, u32[]{:S(2)}) copy-start(bf16[16,16,864]{2,1,0:T(8,128)(2,1)} %param.25) | copy-start | bytes 1327108
  6.5 16.4 %copy-start.8 = (s32[16,4]{0,1:T(4,128)S(1)}, s32[16,4]{0,1:T(4,128)}, u32[]{:S(2)}) copy-start(s32[16,4]{0,1:T(4,128)} %param.17) | copy-start | bytes 772
  6.5 6.8 %copy-start.7 = (bf16[576,384]{1,0:T(8,128)(2,1)S(1)}, bf16[576,384]{1,0:T(8,128)(2,1)}, u32[]{:S(2)}) copy-start(bf16[576,384]{1,0:T(8,128)(2,1)} %param.16) | copy-start | bytes 1327108
  6.5 17.1 %copy-start.9 = (s32[64]{0:T(128)S(1)}, s32[64]{0:T(128)}, u32[]{:S(2)}) copy-start(s32[64]{0:T(128)} %param.18) | copy-start | bytes 772
  6.5 17.2 %copy-start.10 = (s32[8]{0:T(128)S(1)}, s32[8]{0:T(128)}, u32[]{:S(2)}) copy-start(s32[8]{0:T(128)} %param.19) | copy-start | bytes 100
  6.5 59.5 %all-gather.3.cloned.1.call-start = ((), (), s32[]{:S(2)}) async-start(), calls=%async_computation.2 | async-start | bytes 4177920 | tf_op jit(solution)/shard_map/all_gather | solution.py:126
  7.3 198.2 %all-gather.5.cloned.1.call-start = ((), (), s32[]{:S(2)}) async-start(), calls=%async_computation.3 | async-start | bytes 19496960 | tf_op jit(solution)/shard_map/all_gather | solution.py:128
  9.7 29.1 %copy-start.12 = (bf16[384,16,16]{0,2,1:T(8,128)(2,1)S(1)}, bf16[384,16,16]{0,2,1:T(8,128)(2,1)}, u32[]{:S(2)}) copy-start(bf16[384,16,16]{0,2,1:T(8,128)(2,1)} %param.21) | copy-start | bytes 589828
  14.5 22.1 %all-to-all-start.1 = ((bf16[36,16,384]{2,0,1:T(8,128)(2,1)}), bf16[36,16,384]{2,0,1:T(8,128)(2,1)S(1)}, u32[]{:S(2)}, u32[]{:S(2)}) async-start(bf16[36,16,384]{2,0,1:T(8,128)(2,1)} %copy.96), calls=%async_computation.1 | async-start | bytes 983040 | tf_op jit(solution)/shard_map/all_to_all | solution.py:138
  70.5 2.6 copy-start.2
  70.5 3.6 %copy-start.5 = (bf16[576,640]{1,0:T(8,128)(2,1)S(1)}, bf16[576,640]{1,0:T(8,128)(2,1)}, u32[]{:S(2)}) copy-start(bf16[576,640]{1,0:T(8,128)(2,1)} %param.15) | copy-start | bytes 2211844
  73.0 7.5 %collective-permute-start = (bf16[4,394,640]{2,0,1:T(4,128)(2,1)}, bf16[4,394,640]{2,0,1:T(4,128)(2,1)}, u32[]{:S(2)}, u32[]{:S(2)}) collective-permute-start(bf16[4,394,640]{2,0,1:T(4,128)(2,1)} %copy.103), channel_id=1, source_target_pairs={{0,1},{1,0},{2,3},{3,2},{4,5},{5,4},{6,7},{7,6},{8,9},{9,8},{10,11... | collective-permute-start | bytes 6051848 | tf_op jit(solution)/shard_map/ppermute | solution.py:69
  75.7 28.5 %all-to-all-start = ((bf16[36,16,640]{2,0,1:T(8,128)(2,1)}), bf16[36,16,640]{2,0,1:T(8,128)(2,1)S(1)}, u32[]{:S(2)}, u32[]{:S(2)}) async-start(bf16[36,16,640]{2,0,1:T(8,128)(2,1)} %copy.94), calls=%async_computation | async-start | bytes 1638400 | tf_op jit(solution)/shard_map/all_to_all | solution.py:142
  80.5 10.7 %copy-start.6 = (f32[8,3,5120]{2,0,1:T(8,128)S(1)}, f32[8,3,5120]{2,0,1:T(8,128)}, u32[]{:S(2)}) copy-start(f32[8,3,5120]{2,0,1:T(8,128)} %param.23) | copy-start | bytes 1474564
  86.4 20.1 %collective-permute-start.1 = (bf16[394,640]{1,0:T(8,128)(2,1)}, bf16[394,640]{1,0:T(8,128)(2,1)}, u32[]{:S(2)}, u32[]{:S(2)}) collective-permute-start(bf16[394,640]{1,0:T(8,128)(2,1)} %get-tuple-element.16), channel_id=1, source_target_pairs={{0,2},{1,3},{2,4},{3,5},{4,6},{5,7},{6,0},{7,1},{8,10},{9,11},{10,... | collective-permute-start | bytes 1512968 | tf_op jit(solution)/shard_map/ppermute | solution.py:69
  87.7 25.2 %collective-permute-start.2 = (bf16[394,640]{1,0:T(8,128)(2,1)S(1)}, bf16[394,640]{1,0:T(8,128)(2,1)}, u32[]{:S(2)}, u32[]{:S(2)}) collective-permute-start(bf16[394,640]{1,0:T(8,128)(2,1)S(1)} %get-tuple-element.18), channel_id=1, source_target_pairs={{0,4},{1,5},{2,6},{3,7},{4,0},{5,1},{6,2},{7,3},{8,12},{9,13},{10,... | collective-permute-start | bytes 1512968 | tf_op jit(solution)/shard_map/ppermute | solution.py:69
  90.1 22.7 %collective-permute-start.3 = (bf16[394,640]{1,0:T(8,128)(2,1)S(1)}, bf16[394,640]{1,0:T(8,128)(2,1)}, u32[]{:S(2)}, u32[]{:S(2)}) collective-permute-start(bf16[394,640]{1,0:T(8,128)(2,1)S(1)} %get-tuple-element.17), channel_id=1, source_target_pairs={{0,6},{1,7},{2,0},{3,1},{4,2},{5,3},{6,4},{7,5},{8,14},{9,15},{10,... | collective-permute-start | bytes 1512968 | tf_op jit(solution)/shard_map/ppermute | solution.py:69
  116.3 12.3 %collective-permute-start.4 = (bf16[384,640]{1,0:T(8,128)(2,1)S(1)}, bf16[384,640]{1,0:T(8,128)(2,1)S(1)}, u32[]{:S(2)}, u32[]{:S(2)}) collective-permute-start(bf16[384,640]{1,0:T(8,128)(2,1)S(1)} %fusion.24), channel_id=1, source_target_pairs={{0,1},{1,0},{2,3},{3,2},{4,5},{5,4},{6,7},{7,6},{8,9},{9,8},{10,11... | collective-permute-start | bytes 1474568 | tf_op jit(solution)/shard_map/ppermute | solution.py:69
  128.8 24.5 %collective-permute-start.5 = (bf16[2,384,640]{2,1,0:T(8,128)(2,1)S(1)}, bf16[2,384,640]{2,1,0:T(8,128)(2,1)}, u32[]{:S(2)}, u32[]{:S(2)}) collective-permute-start(bf16[2,384,640]{2,1,0:T(8,128)(2,1)S(1)} %get-tuple-element.23), channel_id=1, source_target_pairs={{0,2},{1,3},{2,4},{3,5},{4,6},{5,7},{6,0},{7,1},{8,10},{9,11},{10,... | collective-permute-start | bytes 2949128 | tf_op jit(solution)/shard_map/ppermute | solution.py:69
  130.0 45.1 %collective-permute-start.6 = (bf16[2,384,640]{2,1,0:T(8,128)(2,1)S(1)}, bf16[2,384,640]{2,1,0:T(8,128)(2,1)}, u32[]{:S(2)}, u32[]{:S(2)}) collective-permute-start(bf16[2,384,640]{2,1,0:T(8,128)(2,1)S(1)} %get-tuple-element.23), channel_id=1, source_target_pairs={{0,4},{1,5},{2,6},{3,7},{4,0},{5,1},{6,2},{7,3},{8,12},{9,13},{10,... | collective-permute-start | bytes 2949128 | tf_op jit(solution)/shard_map/ppermute | solution.py:69
  132.3 42.8 %collective-permute-start.7 = (bf16[2,384,640]{2,1,0:T(8,128)(2,1)S(1)}, bf16[2,384,640]{2,1,0:T(8,128)(2,1)}, u32[]{:S(2)}, u32[]{:S(2)}) collective-permute-start(bf16[2,384,640]{2,1,0:T(8,128)(2,1)S(1)} %get-tuple-element.23), channel_id=1, source_target_pairs={{0,6},{1,7},{2,0},{3,1},{4,2},{5,3},{6,4},{7,5},{8,14},{9,15},{10,... | collective-permute-start | bytes 2949128 | tf_op jit(solution)/shard_map/ppermute | solution.py:69
  183.7 3.7 %copy-start.1 = (bf16[8,384,640]{2,1,0:T(8,128)(2,1)S(1)}, bf16[8,384,640]{2,1,0:T(8,128)(2,1)}, u32[]{:S(2)}) copy-start(bf16[8,384,640]{2,1,0:T(8,128)(2,1)} %gather_fusion.3) | copy-start | bytes 11796484
  187.5 8.7 %copy-start.11 = (bf16[640,16,16]{0,2,1:T(8,128)(2,1)S(1)}, bf16[640,16,16]{0,2,1:T(8,128)(2,1)}, u32[]{:S(2)}) copy-start(bf16[640,16,16]{0,2,1:T(8,128)(2,1)} %param.24) | copy-start | bytes 983044
  194.2 2.0 copy-start.3
  196.6 2.0 collective-permute-start.8
  198.6 2.7 collective-permute-start.9
  201.3 4.2 %collective-permute-start.10 = (f32[384,16]{0,1:T(8,128)S(1)}, f32[384,16]{0,1:T(8,128)S(1)}, u32[]{:S(2)}, u32[]{:S(2)}) collective-permute-start(f32[384,16]{0,1:T(8,128)S(1)} %add.383), channel_id=1, source_target_pairs={{0,4},{1,5},{2,6},{3,7},{4,0},{5,1},{6,2},{7,3},{8,12},{9,13},{10,... | collective-permute-start | bytes 73736 | tf_op jit(solution)/shard_map/ppermute | solution.py:62
  205.4 11.6 %copy-start.4 = (bf16[8,384,640]{2,1,0:T(8,128)(2,1)S(1)}, bf16[8,384,640]{2,1,0:T(8,128)(2,1)}, u32[]{:S(2)}) copy-start(bf16[8,384,640]{2,1,0:T(8,128)(2,1)} %copy-done.3) | copy-start | bytes 11796484
  238.3 6.6 %collective-permute-start.11 = (bf16[4,384,640]{2,1,0:T(8,128)(2,1)}, bf16[4,384,640]{2,1,0:T(8,128)(2,1)}, u32[]{:S(2)}, u32[]{:S(2)}) collective-permute-start(bf16[4,384,640]{2,1,0:T(8,128)(2,1)} %bitcast.164), channel_id=1, source_target_pairs={{0,1},{1,0},{2,3},{3,2},{4,5},{5,4},{6,7},{7,6},{8,9},{9,8},{10,11... | collective-permute-start | bytes 5898248 | tf_op jit(solution)/shard_map/ppermute | solution.py:69
  249.8 13.8 %collective-permute-start.12 = (bf16[384,640]{1,0:T(8,128)(2,1)}, bf16[384,640]{1,0:T(8,128)(2,1)S(1)}, u32[]{:S(2)}, u32[]{:S(2)}) collective-permute-start(bf16[384,640]{1,0:T(8,128)(2,1)} %get-tuple-element.19), channel_id=1, source_target_pairs={{0,2},{1,3},{2,4},{3,5},{4,6},{5,7},{6,0},{7,1},{8,10},{9,11},{10,... | collective-permute-start | bytes 1474568 | tf_op jit(solution)/shard_map/ppermute | solution.py:69
  251.1 23.9 %collective-permute-start.13 = (bf16[384,640]{1,0:T(8,128)(2,1)}, bf16[384,640]{1,0:T(8,128)(2,1)}, u32[]{:S(2)}, u32[]{:S(2)}) collective-permute-start(bf16[384,640]{1,0:T(8,128)(2,1)} %get-tuple-element.21), channel_id=1, source_target_pairs={{0,4},{1,5},{2,6},{3,7},{4,0},{5,1},{6,2},{7,3},{8,12},{9,13},{10,... | collective-permute-start | bytes 1474568 | tf_op jit(solution)/shard_map/ppermute | solution.py:69
  253.2 21.8 %collective-permute-start.14 = (bf16[384,640]{1,0:T(8,128)(2,1)S(1)}, bf16[384,640]{1,0:T(8,128)(2,1)}, u32[]{:S(2)}, u32[]{:S(2)}) collective-permute-start(bf16[384,640]{1,0:T(8,128)(2,1)S(1)} %get-tuple-element.20), channel_id=1, source_target_pairs={{0,6},{1,7},{2,0},{3,1},{4,2},{5,3},{6,4},{7,5},{8,14},{9,15},{10,... | collective-permute-start | bytes 1474568 | tf_op jit(solution)/shard_map/ppermute | solution.py:69
Sparse Core Ops, SparseCore 0:
  9.5 56.5 all-gather.2
  68.2 127.7 all-gather.4

commit v3 on v2

--- a/solution.py
+++ b/solution.py
@@ -81,11 +81,21 @@
     mine = lax.dynamic_index_in_dim(payload, core, 1, keepdims=False)
     other = lax.dynamic_index_in_dim(payload, 1 - core, 1, keepdims=False)
     pair = mine.astype(jnp.float32) + mlp_move(other, lambda i: i ^ 1).astype(jnp.float32)
-    pair_b = pair.astype(jnp.bfloat16)
-    total = lax.dynamic_index_in_dim(pair, y_here, 0, keepdims=False)
-    for step in range(1, y_count):
-        send = lax.dynamic_index_in_dim(pair_b, (y_here + step) % y_count, 0, keepdims=False)
-        total = total + mlp_move(send, y_shift(step, y_count)).astype(jnp.float32)
+
+    def chunk(step):
+        return lax.dynamic_index_in_dim(pair, (y_here + step) % y_count, 0, keepdims=False)
+
+    far = chunk(2)
+    cut = far.shape[0] // 2
+    via_right = mlp_move(far[:cut].astype(jnp.bfloat16), y_shift(1, y_count))
+    via_left = mlp_move(far[cut:].astype(jnp.bfloat16), y_shift(-1, y_count))
+    right = chunk(1)
+    right = jnp.concatenate([right[:cut] + via_right.astype(jnp.float32), right[cut:]], axis=0)
+    left = chunk(-1)
+    left = jnp.concatenate([left[:cut], left[cut:] + via_left.astype(jnp.float32)], axis=0)
+    total = chunk(0)
+    total = total + mlp_move(right.astype(jnp.bfloat16), y_shift(1, y_count)).astype(jnp.float32)
+    total = total + mlp_move(left.astype(jnp.bfloat16), y_shift(-1, y_count)).astype(jnp.float32)
     return total
 
 
@@ -94,8 +104,13 @@
     y_here = m // 2
     core = m % 2
     pair = jnp.stack([block, mlp_move(block, lambda i: i ^ 1)], axis=0)
-    rows = [pair] + [mlp_move(pair, y_shift(step, y_count)) for step in range(1, y_count)]
-    held = jnp.stack(rows, axis=0).reshape((2 * y_count,) + block.shape)
+    from_left = mlp_move(pair, y_shift(1, y_count))
+    from_right = mlp_move(pair, y_shift(-1, y_count))
+    far = jnp.concatenate(
+        [mlp_move(from_left[:1], y_shift(1, y_count)), mlp_move(from_right[1:], y_shift(-1, y_count))],
+        axis=0,
+    )
+    held = jnp.stack([pair, from_left, far, from_right], axis=0).reshape((2 * y_count,) + block.shape)
     target = jnp.arange(2 * y_count, dtype=jnp.int32)
     slot = ((y_here - target // 2) % y_count) * 2 + (target % 2) ^ core
     return jnp.take(held, slot, axis=0)

time: 285 us -> 264 us (0.926)
  waiting for transfers between devices: 113 us -> 92.8 us
    ppermute x12 -> x15, waiting for transfers between devices: 56.4 us -> 31.8 us  [mlp_move(): return lax.ppermute(block, 'mlp', [(i, target(i)) for i in range(n)])]
    add x2, other arithmetic: 8.77 us -> 2.46 us  [scatter_mlp(): mine.astype(jnp.float32)]
    dynamic_slice x2 -> x0, local copies, waits for them, and re-layouts: 6.29 us -> none  [the longest x1 3.86 us: scatter_mlp(): mine = lax.dynamic_index_in_dim(payload, core, 1, keepdims=False)]
    slice x0 -> x4, local copies, waits for them, and re-layouts: none -> 5.24 us  [the longest x2 2.53 us: scatter_mlp(): right[cut:]]
    another operation x6 -> x9, other arithmetic: 4.13 us -> 8.77 us  [the longest x3 5.76 us: gather_mlp(): jnp.stack([pair, from_left, far, from_right], axis=0)]
    unnamed x28 -> x43, local copies, waits for them, and re-layouts: 4.89 us -> 5.93 us
    ppermute x12 -> x15, starting transfers between devices: 19.2 us -> 19.3 us  [mlp_move(): return lax.ppermute(block, 'mlp', [(i, target(i)) for i in range(n)])]
  transfers between devices with their start and end apart: 19 -> 22, of which waited for: 12 -> 14; matrix products, arithmetic and copies ran while one was open for 27% -> 30% of each run, Pallas kernels for 0% -> 0%
where the time goes in v3:
time: 264 us; the launch traced here: 262 us
  waiting for transfers between devices  92.8 us (35%)
  local copies, waits for them, and re-layouts  53 us (20%)
  other arithmetic  43.7 us (17%)
  starting transfers between devices  36.5 us (14%)
  matrix products  20.4 us (8%)
  between operations  16 us (6%)
    ppermute x15, waiting for transfers between devices, mlp_move(): return lax.ppermute(block, 'mlp', [(i, target(i)) for i in range(n)])  31.8 us
    all_gather x1, waiting for transfers between devices, local(): out_w = lax.all_gather(output_weight, 'req', axis=1, tiled=True)  26.6 us
    ppermute x15, starting transfers between devices, mlp_move(): return lax.ppermute(block, 'mlp', [(i, target(i)) for i in range(n)])  19.3 us
    all_to_all x1, waiting for transfers between devices, local(): lax.all_to_all(send_layout(residual_input, offset, req_count), 'req', spl...  14.5 us
    all_to_all x1, waiting for transfers between devices, local(): lax.all_to_all(send_layout(attention_output, offset, req_count), 'req', s...  12.1 us
    slice x1, local copies, waits for them, and re-layouts, local(): up_w = both[0]  11.6 us
    add x1, other arithmetic, local(): 1.0 + scale_rows  10.7 us
    dot_general x1, matrix products, local(): jnp.einsum('th,mch->mtc', hidden, down_t.reshape(mlp_count, width, hidden...  9.05 us
  transfers between devices with their start and end apart: 22, of which 14 were waited for; matrix products, arithmetic and copies ran while one was open for 30% of the time, Pallas kernels for 0%

profile of v3, /device:TPU:1, one launch (start us, length us, event | category | flops | bytes accessed | tf_op | source)
XLA Modules:
  0.0 262.3 jit_solution(17826676789579446520)
XLA Ops:
  7.3 2.4 pad_maximum_fusion.1
  14.5 8.4 %all-to-all-start.1 = ((bf16[36,16,384]{2,0,1:T(8,128)(2,1)}), bf16[36,16,384]{2,0,1:T(8,128)(2,1)S(1)}, u32[]{:S(2)}, u32[]{:S(2)}) async-start(bf16[36,16,384]{2,0,1:T(8,128)(2,1)} %copy.74), calls=%async_computation.1 | async-start | bytes 983040 | tf_op jit(solution)/shard_map/all_to_all | solution.py:153
  24.5 12.1 %all-to-all-done.1 = bf16[36,16,384]{2,0,1:T(8,128)(2,1)S(1)} async-done(((bf16[36,16,384]{2,0,1:T(8,128)(2,1)}), bf16[36,16,384]{2,0,1:T(8,128)(2,1)S(1)}, u32[]{:S(2)}, u32[]{:S(2)}) %all-to-all-start.1) | async-done | bytes 442400 | tf_op jit(solution)/shard_map/all_to_all | solution.py:153
  36.7 2.1 gather_fusion.1
  39.5 26.6 %all-gather.3.cloned.1.call-done = bf16[384,5120]{0,1:T(8,128)(2,1)} async-done(((bf16[384,320]{0,1:T(8,128)(2,1)}), bf16[384,5120]{0,1:T(8,128)(2,1)}) %all-gather.3.cloned.1.call-update) | async-done | bytes 3932176 | tf_op jit(solution)/shard_map/all_gather | solution.py:141
  66.1 4.4 %convolution_convert_fusion.1 = bf16[384,8,640]{2,0,1:T(8,128)(2,1)S(1)} fusion(bf16[384,8,640]{0,2,1:T(8,128)(2,1)} %bitcast.186, bf16[384,384]{1,0:T(8,128)(2,1)S(1)} %gather_fusion.1, pred[384]{0:T(512)(128)(4,1)S(1)} %compare_and_fusion.2), kind=kOutput, calls=%fused_computation.27 | convolution fusion | flops 1512062976 | bytes 8159616 | tf_op jit(solution)/shard_map/tk,kmc->mtc/dot_general | solution.py:168
  70.7 2.3 copy.81
  74.1 3.9 %collective-permute-done = bf16[4,394,640]{2,0,1:T(4,128)(2,1)S(1)} collective-permute-done((bf16[4,394,640]{2,0,1:T(4,128)(2,1)}, bf16[4,394,640]{2,0,1:T(4,128)(2,1)S(1)}, u32[]{:S(2)}, u32[]{:S(2)}) %collective-permute-start) | collective-permute-done | bytes 2017312 | tf_op jit(solution)/shard_map/ppermute | solution.py:69
  78.0 2.1 convert_add_fusion
  86.6 4.5 %all-to-all-start = ((bf16[36,16,640]{2,0,1:T(8,128)(2,1)}), bf16[36,16,640]{2,0,1:T(8,128)(2,1)S(1)}, u32[]{:S(2)}, u32[]{:S(2)}) async-start(bf16[36,16,640]{2,0,1:T(8,128)(2,1)} %copy.72), calls=%async_computation | async-start | bytes 1638400 | tf_op jit(solution)/shard_map/all_to_all | solution.py:157
  94.8 2.7 %collective-permute-start.4 = (bf16[394,640]{1,0:T(8,128)(2,1)}, bf16[394,640]{1,0:T(8,128)(2,1)S(1)}, u32[]{:S(2)}, u32[]{:S(2)}) collective-permute-start(bf16[394,640]{1,0:T(8,128)(2,1)} %pad_maximum_fusion.4), channel_id=1, source_target_pairs={{0,6},{1,7},{2,0},{3,1},{4,2},{5,3},{6,4},{7,5},{8,14},{9,15},{10,... | collective-permute-start | bytes 1512968 | tf_op jit(solution)/shard_map/ppermute | solution.py:69
  97.5 14.5 %all-to-all-done = bf16[36,16,640]{2,0,1:T(8,128)(2,1)S(1)} async-done(((bf16[36,16,640]{2,0,1:T(8,128)(2,1)}), bf16[36,16,640]{2,0,1:T(8,128)(2,1)S(1)}, u32[]{:S(2)}, u32[]{:S(2)}) %all-to-all-start) | async-done | bytes 737312 | tf_op jit(solution)/shard_map/all_to_all | solution.py:157
  112.1 2.3 gather_fusion
  123.8 5.5 %gather_fusion.4 = f32[384,5120]{1,0:T(8,128)} fusion(f32[8,5120]{1,0:T(8,128)S(1)} %get-tuple-element.24, s32[1024]{0:T(1024)S(1)} %pad_clamp_fusion), kind=kCustom, calls=%fused_computation.clone | custom fusion | bytes 15730176 | tf_op jit(solution)/shard_map/jit(_take)/gather | solution.py:164
  129.3 5.5 %gather_fusion.5 = f32[384,5120]{1,0:T(8,128)} fusion(f32[8,5120]{1,0:T(8,128)S(1)} %get-tuple-element.23, s32[1024]{0:T(1024)S(1)} %pad_clamp_fusion), kind=kCustom, calls=%fused_computation.1.clone | custom fusion | bytes 15730176 | tf_op jit(solution)/shard_map/jit(_take)/gather | solution.py:163
  134.8 10.8 %collective-permute-done.6 = bf16[2,384,640]{2,1,0:T(8,128)(2,1)S(1)} collective-permute-done((bf16[2,384,640]{2,1,0:T(8,128)(2,1)}, bf16[2,384,640]{2,1,0:T(8,128)(2,1)S(1)}, u32[]{:S(2)}, u32[]{:S(2)}) %collective-permute-start.6) | collective-permute-done | bytes 983072 | tf_op jit(solution)/shard_map/ppermute | solution.py:69
  148.3 2.7 %collective-permute-start.9 = (bf16[1,384,640]{2,1,0:T(8,128)(2,1)}, bf16[1,384,640]{2,1,0:T(8,128)(2,1)}, u32[]{:S(2)}, u32[]{:S(2)}) collective-permute-start(bf16[1,384,640]{2,1,0:T(8,128)(2,1)} %slice.157), channel_id=1, source_target_pairs={{0,6},{1,7},{2,0},{3,1},{4,2},{5,3},{6,4},{7,5},{8,14},{9,15},{10,... | collective-permute-start | bytes 1474568 | tf_op jit(solution)/shard_map/ppermute | solution.py:69
  151.0 10.7 %select_add_fusion = (f32[384,5120]{1,0:T(8,128)}, f32[384,5120]{1,0:T(8,128)}) fusion(f32[384,5120]{1,0:T(8,128)} %gather_fusion.4, pred[384]{0:T(512)(128)(4,1)S(1)} %compare_and_fusion.1, f32[384,5120]{1,0:T(8,128)} %gather_fusion.5), kind=kLoop, calls=%fused_computation.16 | loop fusion | flops 5898240 | bytes 31457664 | tf_op jit(solution)/shard_map/add | solution.py:209
  163.1 3.3 %pad_maximum_fusion = bf16[4,2,384,640]{3,2,1,0:T(8,128)(2,1)} fusion(bf16[1,2,384,640]{3,2,1,0:T(8,128)(2,1)} %bitcast.33, bf16[1,2,384,640]{3,2,1,0:T(8,128)(2,1)S(1)} %maximum_bitcast_fusion, bf16[1,2,384,640]{3,2,1,0:T(8,128)(2,1)S(1)} %bitcast.189, bf16[1,2,384,640]{3,2,1,0:T(8,128)(2,1)S(1)} %get-tuple-element.18), kind=kLoop, calls=%fused_computation.20 | loop fusion | flops 5898240 | bytes 7864320 | tf_op jit(solution)/shard_map/stack | solution.py:113
  166.4 5.2 %gather_fusion.3 = bf16[8,384,640]{2,1,0:T(8,128)(2,1)} fusion(bf16[8,384,640]{2,1,0:T(8,128)(2,1)} %bitcast.183, s32[1024]{0:T(1024)S(1)} %pad_clamp_fusion.1), kind=kCustom, calls=%fused_computation.5 | custom fusion | bytes 7864352 | tf_op jit(solution)/shard_map/jit(_take)/gather | solution.py:116
  171.6 3.9 %convert_reduce_fusion = (f32[384]{0:T(512)S(1)}, f32[384]{0:T(512)S(1)}) fusion(bf16[8,384,640]{2,1,0:T(8,128)(2,1)} %gather_fusion.3, pred[8]{0:T(512)(128)(4,1)S(1)} %compare_and_fusion), kind=kLoop, calls=%fused_computation.8 | loop fusion | flops 9829632 | bytes 3935240 | tf_op jit(solution)/shard_map/reduce_sum | solution.py:206
  175.5 6.7 %fusion.3 = bf16[8,384,640]{2,1,0:T(8,128)(2,1)S(1)} fusion(f32[48,8,8,640]{3,2,1,0:T(8,128)} %bitcast.180, f32[48,8,8,640]{3,2,1,0:T(8,128)} %bitcast.179, f32[384]{0:T(512)S(1)} %get-tuple-element.28, f32[384]{0:T(512)S(1)} %get-tuple-element.27, bf16[8,384,640]{2,1,0:T(8,128)(2,1)S(1)} %copy-done.2, pred[8]{0:T(512)(128)(4,1)S(1)} %compare_and_fusion), kind=kLoop, calls=%fused_computation.12 | loop fusion | flops 13762560 | bytes 23596040 | tf_op jit(solution)/shard_map/convert_element_type | solution.py:213
  182.3 2.0 copy-done.5
  187.2 3.0 %collective-permute-done.11 = f32[384,16]{0,1:T(8,128)S(1)} collective-permute-done((f32[384,16]{0,1:T(8,128)S(1)}, f32[384,16]{0,1:T(8,128)S(1)}, u32[]{:S(2)}, u32[]{:S(2)}) %collective-permute-start.11) | collective-permute-done | bytes 24608 | tf_op jit(solution)/shard_map/ppermute | solution.py:62
  190.2 2.5 collective-permute-start.12
  196.0 11.6 %fusion.92 = (bf16[1,5120,864]{2,1,0:T(8,128)(2,1)S(1)}, bf16[1,5120,864]{2,1,0:T(8,128)(2,1)}) fusion(bf16[2,5120,864]{2,1,0:T(8,128)(2,1)} %all-gather.5.cloned.1.call-done), kind=kLoop, calls=%fused_computation.204 | loop fusion | bytes 35389440 | tf_op jit(solution)/shard_map/slice | solution.py:144
  207.6 4.8 %convolution_bitcast_fusion.1 = f32[384,864]{0,1:T(8,128)S(1)} fusion(bf16[8,384,640]{2,1,0:T(8,128)(2,1)S(1)} %copy-done.6, bf16[8,640,864]{2,1,0:T(8,128)(2,1)S(1)} %bitcast.185), kind=kOutput, calls=%fused_computation.37 | convolution fusion | flops 3397386240 | bytes 14106624 | tf_op jit(solution)/shard_map/mtc,mch->th/dot_general | solution.py:225
  212.4 9.1 %convolution_convert_fusion = bf16[8,640,384]{1,2,0:T(8,128)(2,1)} fusion(bf16[8,640,864]{2,1,0:T(8,128)(2,1)} %bitcast.184, f32[384,864]{0,1:T(8,128)S(1)} %convolution_bitcast_fusion.1, bf16[16,16,864]{2,1,0:T(8,128)(2,1)S(1)} %copy-done, bf16[384,16]{0,1:T(8,128)(2,1)S(1)} %add_convert_fusion, bf16[384,16]{0,1:T(8,128)(2,1)S(1)} %copy-done.14), kind=kOutput, calls=%fused_computation.26 | convolution fusion | flops 3572637696 | bytes 14573568 | tf_op jit(solution)/shard_map/th,mch->mtc/dot_general | solution.py:237
  224.2 3.6 %collective-permute-done.13 = bf16[4,384,640]{2,1,0:T(8,128)(2,1)S(1)} collective-permute-done((bf16[4,384,640]{2,1,0:T(8,128)(2,1)S(1)}, bf16[4,384,640]{2,1,0:T(8,128)(2,1)S(1)}, u32[]{:S(2)}, u32[]{:S(2)}) %collective-permute-start.13) | collective-permute-done | bytes 1966112 | tf_op jit(solution)/shard_map/ppermute | solution.py:69
  234.2 4.4 %collective-permute-done.14 = bf16[192,640]{1,0:T(8,128)(2,1)S(1)} collective-permute-done((bf16[192,640]{1,0:T(8,128)(2,1)S(1)}, bf16[192,640]{1,0:T(8,128)(2,1)S(1)}, u32[]{:S(2)}, u32[]{:S(2)}) %collective-permute-start.14) | collective-permute-done | bytes 245792 | tf_op jit(solution)/shard_map/ppermute | solution.py:69
  245.4 7.3 %collective-permute-done.15 = bf16[384,640]{1,0:T(8,128)(2,1)S(1)} collective-permute-done((bf16[384,640]{1,0:T(8,128)(2,1)S(1)}, bf16[384,640]{1,0:T(8,128)(2,1)S(1)}, u32[]{:S(2)}, u32[]{:S(2)}) %collective-permute-start.15) | collective-permute-done | bytes 491552 | tf_op jit(solution)/shard_map/ppermute | solution.py:69
  253.0 2.5 fusion.37
  (148 shorter events, 53.2 us)
Async XLA Ops:
  6.5 205.8 %copy-start = (bf16[16,16,864]{2,1,0:T(8,128)(2,1)S(1)}, bf16[16,16,864]{2,1,0:T(8,128)(2,1)}, u32[]{:S(2)}) copy-start(bf16[16,16,864]{2,1,0:T(8,128)(2,1)} %param.25) | copy-start | bytes 1327108
  6.5 16.4 %copy-start.15 = (s32[16,4]{0,1:T(4,128)S(1)}, s32[16,4]{0,1:T(4,128)}, u32[]{:S(2)}) copy-start(s32[16,4]{0,1:T(4,128)} %param.17) | copy-start | bytes 772
  6.5 17.2 %copy-start.17 = (s32[64]{0:T(128)S(1)}, s32[64]{0:T(128)}, u32[]{:S(2)}) copy-start(s32[64]{0:T(128)} %param.18) | copy-start | bytes 772
  6.5 17.3 %copy-start.18 = (s32[8]{0:T(128)S(1)}, s32[8]{0:T(128)}, u32[]{:S(2)}) copy-start(s32[8]{0:T(128)} %param.19) | copy-start | bytes 100
  6.5 59.6 %all-gather.3.cloned.1.call-start = ((), (), s32[]{:S(2)}) async-start(), calls=%async_computation.2 | async-start | bytes 4177920 | tf_op jit(solution)/shard_map/all_gather | solution.py:141
  7.3 188.7 %all-gather.5.cloned.1.call-start = ((), (), s32[]{:S(2)}) async-start(), calls=%async_computation.3 | async-start | bytes 19496960 | tf_op jit(solution)/shard_map/all_gather | solution.py:143
  9.7 29.1 %copy-start.20 = (bf16[384,16,16]{0,2,1:T(8,128)(2,1)S(1)}, bf16[384,16,16]{0,2,1:T(8,128)(2,1)}, u32[]{:S(2)}) copy-start(bf16[384,16,16]{0,2,1:T(8,128)(2,1)} %param.21) | copy-start | bytes 589828
  14.5 22.1 %all-to-all-start.1 = ((bf16[36,16,384]{2,0,1:T(8,128)(2,1)}), bf16[36,16,384]{2,0,1:T(8,128)(2,1)S(1)}, u32[]{:S(2)}, u32[]{:S(2)}) async-start(bf16[36,16,384]{2,0,1:T(8,128)(2,1)} %copy.74), calls=%async_computation.1 | async-start | bytes 983040 | tf_op jit(solution)/shard_map/all_to_all | solution.py:153
  23.6 46.9 %copy-start.13 = (s32[1024]{0:T(1024)}, s32[1024]{0:T(1024)S(1)}, u32[]{:S(2)}) copy-start(s32[1024]{0:T(1024)S(1)} %pad_clamp_fusion.3) | copy-start | bytes 12292
  23.9 46.6 %copy-start.16 = (pred[384]{0:T(512)(128)(4,1)}, pred[384]{0:T(512)(128)(4,1)S(1)}, u32[]{:S(2)}) copy-start(pred[384]{0:T(512)(128)(4,1)S(1)} %compare_and_fusion.2) | copy-start | bytes 1156
  24.5 46.0 %copy-start.11 = (f32[384,16]{0,1:T(8,128)}, f32[384,16]{0,1:T(8,128)S(1)}, u32[]{:S(2)}) copy-start(f32[384,16]{0,1:T(8,128)S(1)} %get-tuple-element.30) | copy-start | bytes 73732
  73.0 5.0 %collective-permute-start = (bf16[4,394,640]{2,0,1:T(4,128)(2,1)}, bf16[4,394,640]{2,0,1:T(4,128)(2,1)S(1)}, u32[]{:S(2)}, u32[]{:S(2)}) collective-permute-start(bf16[4,394,640]{2,0,1:T(4,128)(2,1)} %copy.81), channel_id=1, source_target_pairs={{0,1},{1,0},{2,3},{3,2},{4,5},{5,4},{6,7},{7,6},{8,9},{9,8},{10,11... | collective-permute-start | bytes 6051848 | tf_op jit(solution)/shard_map/ppermute | solution.py:69
  74.1 10.8 %copy-start.8 = (bf16[576,640]{1,0:T(8,128)(2,1)S(1)}, bf16[576,640]{1,0:T(8,128)(2,1)}, u32[]{:S(2)}) copy-start(bf16[576,640]{1,0:T(8,128)(2,1)} %param.15) | copy-start | bytes 2211844
  82.2 10.2 %collective-permute-start.1 = (bf16[197,640]{1,0:T(8,128)(2,1)S(1)}, bf16[197,640]{1,0:T(8,128)(2,1)S(1)}, u32[]{:S(2)}, u32[]{:S(2)}) collective-permute-start(bf16[197,640]{1,0:T(8,128)(2,1)S(1)} %get-tuple-element.20), channel_id=1, source_target_pairs={{0,2},{1,3},{2,4},{3,5},{4,6},{5,7},{6,0},{7,1},{8,10},{9,11},{10,... | collective-permute-start | bytes 756488 | tf_op jit(solution)/shard_map/ppermute | solution.py:69
  83.5 8.9 %collective-permute-start.3 = (bf16[197,640]{1,0:T(8,128)(2,1)S(1)}, bf16[197,640]{1,0:T(8,128)(2,1)S(1)}, u32[]{:S(2)}, u32[]{:S(2)}) collective-permute-start(bf16[197,640]{1,0:T(8,128)(2,1)S(1)} %get-tuple-element.21), channel_id=1, source_target_pairs={{0,6},{1,7},{2,0},{3,1},{4,2},{5,3},{6,4},{7,5},{8,14},{9,15},{10,... | collective-permute-start | bytes 756488 | tf_op jit(solution)/shard_map/ppermute | solution.py:69
  86.6 25.4 %all-to-all-start = ((bf16[36,16,640]{2,0,1:T(8,128)(2,1)}), bf16[36,16,640]{2,0,1:T(8,128)(2,1)S(1)}, u32[]{:S(2)}, u32[]{:S(2)}) async-start(bf16[36,16,640]{2,0,1:T(8,128)(2,1)} %copy.72), calls=%async_computation | async-start | bytes 1638400 | tf_op jit(solution)/shard_map/all_to_all | solution.py:157
  93.9 20.6 %collective-permute-start.2 = (bf16[394,640]{1,0:T(8,128)(2,1)S(1)}, bf16[394,640]{1,0:T(8,128)(2,1)S(1)}, u32[]{:S(2)}, u32[]{:S(2)}) collective-permute-start(bf16[394,640]{1,0:T(8,128)(2,1)S(1)} %pad_maximum_fusion.3), channel_id=1, source_target_pairs={{0,2},{1,3},{2,4},{3,5},{4,6},{5,7},{6,0},{7,1},{8,10},{9,11},{10,... | collective-permute-start | bytes 1512968 | tf_op jit(solution)/shard_map/ppermute | solution.py:69
  94.8 19.6 %collective-permute-start.4 = (bf16[394,640]{1,0:T(8,128)(2,1)}, bf16[394,640]{1,0:T(8,128)(2,1)S(1)}, u32[]{:S(2)}, u32[]{:S(2)}) collective-permute-start(bf16[394,640]{1,0:T(8,128)(2,1)} %pad_maximum_fusion.4), channel_id=1, source_target_pairs={{0,6},{1,7},{2,0},{3,1},{4,2},{5,3},{6,4},{7,5},{8,14},{9,15},{10,... | collective-permute-start | bytes 1512968 | tf_op jit(solution)/shard_map/ppermute | solution.py:69
  117.5 2.5 collective-permute-start.5
  121.1 24.5 %collective-permute-start.6 = (bf16[2,384,640]{2,1,0:T(8,128)(2,1)}, bf16[2,384,640]{2,1,0:T(8,128)(2,1)S(1)}, u32[]{:S(2)}, u32[]{:S(2)}) collective-permute-start(bf16[2,384,640]{2,1,0:T(8,128)(2,1)} %get-tuple-element.19), channel_id=1, source_target_pairs={{0,2},{1,3},{2,4},{3,5},{4,6},{5,7},{6,0},{7,1},{8,10},{9,11},{10,... | collective-permute-start | bytes 2949128 | tf_op jit(solution)/shard_map/ppermute | solution.py:69
  122.3 24.1 %collective-permute-start.8 = (bf16[2,384,640]{2,1,0:T(8,128)(2,1)}, bf16[2,384,640]{2,1,0:T(8,128)(2,1)}, u32[]{:S(2)}, u32[]{:S(2)}) collective-permute-start(bf16[2,384,640]{2,1,0:T(8,128)(2,1)} %get-tuple-element.19), channel_id=1, source_target_pairs={{0,6},{1,7},{2,0},{3,1},{4,2},{5,3},{6,4},{7,5},{8,14},{9,15},{10,... | collective-permute-start | bytes 2949128 | tf_op jit(solution)/shard_map/ppermute | solution.py:69
  146.4 15.3 %collective-permute-start.7 = (bf16[1,384,640]{2,1,0:T(8,128)(2,1)}, bf16[1,384,640]{2,1,0:T(8,128)(2,1)}, u32[]{:S(2)}, u32[]{:S(2)}) collective-permute-start(bf16[1,384,640]{2,1,0:T(8,128)(2,1)} %slice.156), channel_id=1, source_target_pairs={{0,2},{1,3},{2,4},{3,5},{4,6},{5,7},{6,0},{7,1},{8,10},{9,11},{10,... | collective-permute-start | bytes 1474568 | tf_op jit(solution)/shard_map/ppermute | solution.py:69
  148.3 13.4 %collective-permute-start.9 = (bf16[1,384,640]{2,1,0:T(8,128)(2,1)}, bf16[1,384,640]{2,1,0:T(8,128)(2,1)}, u32[]{:S(2)}, u32[]{:S(2)}) collective-permute-start(bf16[1,384,640]{2,1,0:T(8,128)(2,1)} %slice.157), channel_id=1, source_target_pairs={{0,6},{1,7},{2,0},{3,1},{4,2},{5,3},{6,4},{7,5},{8,14},{9,15},{10,... | collective-permute-start | bytes 1474568 | tf_op jit(solution)/shard_map/ppermute | solution.py:69
  184.6 2.5 collective-permute-start.10
  187.2 3.1 %collective-permute-start.11 = (f32[384,16]{0,1:T(8,128)S(1)}, f32[384,16]{0,1:T(8,128)S(1)}, u32[]{:S(2)}, u32[]{:S(2)}) collective-permute-start(f32[384,16]{0,1:T(8,128)S(1)} %fusion.84), channel_id=1, source_target_pairs={{0,2},{1,3},{2,0},{3,1},{4,6},{5,7},{6,4},{7,5},{8,10},{9,11},{10,... | collective-permute-start | bytes 73736 | tf_op jit(solution)/shard_map/ppermute | solution.py:62
  190.2 4.2 %collective-permute-start.12 = (f32[384,16]{0,1:T(8,128)S(1)}, f32[384,16]{0,1:T(8,128)S(1)}, u32[]{:S(2)}, u32[]{:S(2)}) collective-permute-start(f32[384,16]{0,1:T(8,128)S(1)} %add.393), channel_id=1, source_target_pairs={{0,4},{1,5},{2,6},{3,7},{4,0},{5,1},{6,2},{7,3},{8,12},{9,13},{10,... | collective-permute-start | bytes 73736 | tf_op jit(solution)/shard_map/ppermute | solution.py:62
  196.0 11.6 %copy-start.6 = (bf16[8,384,640]{2,1,0:T(8,128)(2,1)S(1)}, bf16[8,384,640]{2,1,0:T(8,128)(2,1)}, u32[]{:S(2)}) copy-start(bf16[8,384,640]{2,1,0:T(8,128)(2,1)} %copy-done.5) | copy-start | bytes 11796484
  223.3 4.5 %collective-permute-start.13 = (bf16[4,384,640]{2,1,0:T(8,128)(2,1)S(1)}, bf16[4,384,640]{2,1,0:T(8,128)(2,1)S(1)}, u32[]{:S(2)}, u32[]{:S(2)}) collective-permute-start(bf16[4,384,640]{2,1,0:T(8,128)(2,1)S(1)} %dynamic-slice_bitcast_fusion), channel_id=1, source_target_pairs={{0,1},{1,0},{2,3},{3,2},{4,5},{5,4},{6,7},{7,6},{8,9},{9,8},{10,11... | collective-permute-start | bytes 5898248 | tf_op jit(solution)/shard_map/ppermute | solution.py:69
  230.2 8.4 %collective-permute-start.14 = (bf16[192,640]{1,0:T(8,128)(2,1)S(1)}, bf16[192,640]{1,0:T(8,128)(2,1)S(1)}, u32[]{:S(2)}, u32[]{:S(2)}) collective-permute-start(bf16[192,640]{1,0:T(8,128)(2,1)S(1)} %get-tuple-element.25), channel_id=1, source_target_pairs={{0,2},{1,3},{2,4},{3,5},{4,6},{5,7},{6,0},{7,1},{8,10},{9,11},{10,... | collective-permute-start | bytes 737288 | tf_op jit(solution)/shard_map/ppermute | solution.py:69
  231.4 7.1 %collective-permute-start.16 = (bf16[192,640]{1,0:T(8,128)(2,1)S(1)}, bf16[192,640]{1,0:T(8,128)(2,1)S(1)}, u32[]{:S(2)}, u32[]{:S(2)}) collective-permute-start(bf16[192,640]{1,0:T(8,128)(2,1)S(1)} %get-tuple-element.26), channel_id=1, source_target_pairs={{0,6},{1,7},{2,0},{3,1},{4,2},{5,3},{6,4},{7,5},{8,14},{9,15},{10,... | collective-permute-start | bytes 737288 | tf_op jit(solution)/shard_map/ppermute | solution.py:69
  239.9 12.8 %collective-permute-start.15 = (bf16[384,640]{1,0:T(8,128)(2,1)S(1)}, bf16[384,640]{1,0:T(8,128)(2,1)S(1)}, u32[]{:S(2)}, u32[]{:S(2)}) collective-permute-start(bf16[384,640]{1,0:T(8,128)(2,1)S(1)} %pad_maximum_fusion.5), channel_id=1, source_target_pairs={{0,2},{1,3},{2,4},{3,5},{4,6},{5,7},{6,0},{7,1},{8,10},{9,11},{10,... | collective-permute-start | bytes 1474568 | tf_op jit(solution)/shard_map/ppermute | solution.py:69
  241.7 11.3 %collective-permute-start.17 = (bf16[384,640]{1,0:T(8,128)(2,1)}, bf16[384,640]{1,0:T(8,128)(2,1)}, u32[]{:S(2)}, u32[]{:S(2)}) collective-permute-start(bf16[384,640]{1,0:T(8,128)(2,1)} %pad_maximum_fusion.6), channel_id=1, source_target_pairs={{0,6},{1,7},{2,0},{3,1},{4,2},{5,3},{6,4},{7,5},{8,14},{9,15},{10,... | collective-permute-start | bytes 1474568 | tf_op jit(solution)/shard_map/ppermute | solution.py:69
  (11 other events, 55.4 us)
Sparse Core Ops, SparseCore 0:
  9.5 56.5 all-gather.2
  68.2 127.7 all-gather.4

commit v4 on v3

--- a/solution.py
+++ b/solution.py
@@ -74,12 +74,15 @@
 
 
 def scatter_mlp(payload):
-    y_count = payload.shape[0]
-    m = lax.axis_index("mlp")
-    y_here = m // 2
-    core = m % 2
+    core = lax.axis_index("mlp") % 2
     mine = lax.dynamic_index_in_dim(payload, core, 1, keepdims=False)
     other = lax.dynamic_index_in_dim(payload, 1 - core, 1, keepdims=False)
+    return scatter_pair(mine, other)
+
+
+def scatter_pair(mine, other):
+    y_count = mine.shape[0]
+    y_here = lax.axis_index("mlp") // 2
     pair = mine.astype(jnp.float32) + mlp_move(other, lambda i: i ^ 1).astype(jnp.float32)
 
     def chunk(step):
@@ -234,15 +237,18 @@
         preferred_element_type=jnp.float32,
     )
     hidden = jax.nn.gelu(hidden_total, approximate=True).astype(jnp.bfloat16)
-    down_terms = jnp.einsum(
-        "th,mch->mtc",
-        hidden,
-        down_t.reshape(mlp_count, width, hidden_units),
-        preferred_element_type=jnp.float32,
-    ).astype(jnp.bfloat16)
-    down_sum = scatter_mlp(
-        down_terms.reshape((Y_COUNT, mlp_count // Y_COUNT) + down_terms.shape[1:])
-    )
+    core = column_index % 2
+    down_by_core = down_t.reshape(Y_COUNT, mlp_count // Y_COUNT, width, hidden_units)
+    down_parts = [
+        jnp.einsum(
+            "th,ych->ytc",
+            hidden,
+            lax.dynamic_index_in_dim(down_by_core, pick, 1, keepdims=False),
+            preferred_element_type=jnp.float32,
+        ).astype(jnp.bfloat16)
+        for pick in (1 - core, core)
+    ]
+    down_sum = scatter_pair(lax.optimization_barrier(down_parts[1]), down_parts[0])
     result = (values + gate_rows * down_sum).astype(jnp.bfloat16)
     return result.reshape(tok_dev, 1, width)
 

time: 264 us -> 259 us (0.981)
    dot_general x1 -> x3, matrix products: 9.05 us -> 5.31 us  [the longest x2 4.61 us: local(): jnp.einsum('th,ych->ytc', hidden, lax.dynamic_index_in_dim(down_by_core,...]
    unnamed x43 -> x41, local copies, waits for them, and re-layouts: 5.93 us -> 5.93 us
  transfers between devices with their start and end apart: 22 -> 22, of which waited for: 14 -> 14; matrix products, arithmetic and copies ran while one was open for 30% -> 32% of each run, Pallas kernels for 0% -> 0%
where the time goes in v4:
time: 259 us; the launch traced here: 257 us
  waiting for transfers between devices  90.6 us (35%)
  local copies, waits for them, and re-layouts  51 us (20%)
  other arithmetic  43.7 us (17%)
  starting transfers between devices  36.5 us (14%)
  matrix products  19.2 us (7%)
  between operations  16 us (6%)
    ppermute x15, waiting for transfers between devices, mlp_move(): return lax.ppermute(block, 'mlp', [(i, target(i)) for i in range(n)])  29.5 us
    all_gather x1, waiting for transfers between devices, local(): out_w = lax.all_gather(output_weight, 'req', axis=1, tiled=True)  26.6 us
    ppermute x15, starting transfers between devices, mlp_move(): return lax.ppermute(block, 'mlp', [(i, target(i)) for i in range(n)])  19.3 us
    all_to_all x1, waiting for transfers between devices, local(): lax.all_to_all(send_layout(residual_input, offset, req_count), 'req', spl...  14.5 us
    all_to_all x1, waiting for transfers between devices, local(): lax.all_to_all(send_layout(attention_output, offset, req_count), 'req', s...  12.1 us
    slice x1, local copies, waits for them, and re-layouts, local(): down_t = both[1]  11.5 us
    add x1, other arithmetic, local(): 1.0 + scale_rows  10.7 us
    all_to_all x1, starting transfers between devices, local(): lax.all_to_all(send_layout(attention_output, offset, req_count), 'req', s...  8.42 us
  transfers between devices with their start and end apart: 22, of which 14 were waited for; matrix products, arithmetic and copies ran while one was open for 32% of the time, Pallas kernels for 0%

profile of v4, /device:TPU:1, one launch (start us, length us, event | category | flops | bytes accessed | tf_op | source)
XLA Modules:
  0.0 257.0 jit_solution(16246950426900237865)
XLA Ops:
  7.3 2.4 pad_maximum_fusion.1
  14.5 8.4 %all-to-all-start.1 = ((bf16[36,16,384]{2,0,1:T(8,128)(2,1)}), bf16[36,16,384]{2,0,1:T(8,128)(2,1)S(1)}, u32[]{:S(2)}, u32[]{:S(2)}) async-start(bf16[36,16,384]{2,0,1:T(8,128)(2,1)} %copy.81), calls=%async_computation.1 | async-start | bytes 983040 | tf_op jit(solution)/shard_map/all_to_all | solution.py:156
  24.5 12.1 %all-to-all-done.1 = bf16[36,16,384]{2,0,1:T(8,128)(2,1)S(1)} async-done(((bf16[36,16,384]{2,0,1:T(8,128)(2,1)}), bf16[36,16,384]{2,0,1:T(8,128)(2,1)S(1)}, u32[]{:S(2)}, u32[]{:S(2)}) %all-to-all-start.1) | async-done | bytes 442400 | tf_op jit(solution)/shard_map/all_to_all | solution.py:156
  36.6 2.1 gather_fusion.1
  39.5 26.6 %all-gather.3.cloned.1.call-done = bf16[384,5120]{0,1:T(8,128)(2,1)} async-done(((bf16[384,320]{0,1:T(8,128)(2,1)}), bf16[384,5120]{0,1:T(8,128)(2,1)}) %all-gather.3.cloned.1.call-update) | async-done | bytes 3932176 | tf_op jit(solution)/shard_map/all_gather | solution.py:144
  66.1 4.4 %convolution_convert_fusion = bf16[384,8,640]{2,0,1:T(8,128)(2,1)S(1)} fusion(bf16[384,8,640]{0,2,1:T(8,128)(2,1)} %bitcast.190, bf16[384,384]{1,0:T(8,128)(2,1)S(1)} %gather_fusion.1, pred[384]{0:T(512)(128)(4,1)S(1)} %compare_and_fusion.2), kind=kOutput, calls=%fused_computation.32 | convolution fusion | flops 1512062976 | bytes 8159616 | tf_op jit(solution)/shard_map/tk,kmc->mtc/dot_general | solution.py:171
  70.7 2.3 copy.88
  74.1 3.9 %collective-permute-done = bf16[4,394,640]{2,0,1:T(4,128)(2,1)S(1)} collective-permute-done((bf16[4,394,640]{2,0,1:T(4,128)(2,1)}, bf16[4,394,640]{2,0,1:T(4,128)(2,1)S(1)}, u32[]{:S(2)}, u32[]{:S(2)}) %collective-permute-start) | collective-permute-done | bytes 2017312 | tf_op jit(solution)/shard_map/ppermute | solution.py:69
  78.0 2.1 convert_add_fusion
  80.1 2.0 copy-done.3
  86.5 4.5 %all-to-all-start = ((bf16[36,16,640]{2,0,1:T(8,128)(2,1)}), bf16[36,16,640]{2,0,1:T(8,128)(2,1)S(1)}, u32[]{:S(2)}, u32[]{:S(2)}) async-start(bf16[36,16,640]{2,0,1:T(8,128)(2,1)} %copy.79), calls=%async_computation | async-start | bytes 1638400 | tf_op jit(solution)/shard_map/all_to_all | solution.py:160
  94.8 2.7 %collective-permute-start.4 = (bf16[394,640]{1,0:T(8,128)(2,1)}, bf16[394,640]{1,0:T(8,128)(2,1)S(1)}, u32[]{:S(2)}, u32[]{:S(2)}) collective-permute-start(bf16[394,640]{1,0:T(8,128)(2,1)} %pad_maximum_fusion.4), channel_id=1, source_target_pairs={{0,6},{1,7},{2,0},{3,1},{4,2},{5,3},{6,4},{7,5},{8,14},{9,15},{10,... | collective-permute-start | bytes 1512968 | tf_op jit(solution)/shard_map/ppermute | solution.py:69
  97.4 14.5 %all-to-all-done = bf16[36,16,640]{2,0,1:T(8,128)(2,1)S(1)} async-done(((bf16[36,16,640]{2,0,1:T(8,128)(2,1)}), bf16[36,16,640]{2,0,1:T(8,128)(2,1)S(1)}, u32[]{:S(2)}, u32[]{:S(2)}) %all-to-all-start) | async-done | bytes 737312 | tf_op jit(solution)/shard_map/all_to_all | solution.py:160
  112.1 2.3 gather_fusion
  123.8 5.4 %gather_fusion.4 = f32[384,5120]{1,0:T(8,128)} fusion(f32[8,5120]{1,0:T(8,128)S(1)} %get-tuple-element.24, s32[1024]{0:T(1024)S(1)} %pad_clamp_fusion), kind=kCustom, calls=%fused_computation.clone | custom fusion | bytes 15730176 | tf_op jit(solution)/shard_map/jit(_take)/gather | solution.py:167
  129.2 5.5 %gather_fusion.5 = f32[384,5120]{1,0:T(8,128)} fusion(f32[8,5120]{1,0:T(8,128)S(1)} %get-tuple-element.23, s32[1024]{0:T(1024)S(1)} %pad_clamp_fusion), kind=kCustom, calls=%fused_computation.1.clone | custom fusion | bytes 15730176 | tf_op jit(solution)/shard_map/jit(_take)/gather | solution.py:166
  134.7 10.8 %collective-permute-done.6 = bf16[2,384,640]{2,1,0:T(8,128)(2,1)S(1)} collective-permute-done((bf16[2,384,640]{2,1,0:T(8,128)(2,1)}, bf16[2,384,640]{2,1,0:T(8,128)(2,1)S(1)}, u32[]{:S(2)}, u32[]{:S(2)}) %collective-permute-start.6) | collective-permute-done | bytes 983072 | tf_op jit(solution)/shard_map/ppermute | solution.py:69
  148.3 2.7 %collective-permute-start.9 = (bf16[1,384,640]{2,1,0:T(8,128)(2,1)}, bf16[1,384,640]{2,1,0:T(8,128)(2,1)}, u32[]{:S(2)}, u32[]{:S(2)}) collective-permute-start(bf16[1,384,640]{2,1,0:T(8,128)(2,1)} %slice.157), channel_id=1, source_target_pairs={{0,6},{1,7},{2,0},{3,1},{4,2},{5,3},{6,4},{7,5},{8,14},{9,15},{10,... | collective-permute-start | bytes 1474568 | tf_op jit(solution)/shard_map/ppermute | solution.py:69
  151.0 10.7 %select_add_fusion = (f32[384,5120]{1,0:T(8,128)}, f32[384,5120]{1,0:T(8,128)}) fusion(f32[384,5120]{1,0:T(8,128)} %gather_fusion.4, pred[384]{0:T(512)(128)(4,1)S(1)} %compare_and_fusion.1, f32[384,5120]{1,0:T(8,128)} %gather_fusion.5), kind=kLoop, calls=%fused_computation.16 | loop fusion | flops 5898240 | bytes 31457664 | tf_op jit(solution)/shard_map/add | solution.py:212
  163.1 3.3 %pad_maximum_fusion = bf16[4,2,384,640]{3,2,1,0:T(8,128)(2,1)} fusion(bf16[1,2,384,640]{3,2,1,0:T(8,128)(2,1)} %bitcast.34, bf16[1,2,384,640]{3,2,1,0:T(8,128)(2,1)S(1)} %maximum_bitcast_fusion, bf16[1,2,384,640]{3,2,1,0:T(8,128)(2,1)S(1)} %bitcast.191, bf16[1,2,384,640]{3,2,1,0:T(8,128)(2,1)S(1)} %get-tuple-element.18), kind=kLoop, calls=%fused_computation.26 | loop fusion | flops 5898240 | bytes 7864320 | tf_op jit(solution)/shard_map/stack | solution.py:116
  166.4 5.2 %gather_fusion.3 = bf16[8,384,640]{2,1,0:T(8,128)(2,1)} fusion(bf16[8,384,640]{2,1,0:T(8,128)(2,1)} %bitcast.186, s32[1024]{0:T(1024)S(1)} %pad_clamp_fusion.1), kind=kCustom, calls=%fused_computation.5 | custom fusion | bytes 7864352 | tf_op jit(solution)/shard_map/jit(_take)/gather | solution.py:119
  171.6 3.9 %convert_reduce_fusion = (f32[384]{0:T(512)S(1)}, f32[384]{0:T(512)S(1)}) fusion(bf16[8,384,640]{2,1,0:T(8,128)(2,1)} %gather_fusion.3, pred[8]{0:T(512)(128)(4,1)S(1)} %compare_and_fusion), kind=kLoop, calls=%fused_computation.8 | loop fusion | flops 9829632 | bytes 3935240 | tf_op jit(solution)/shard_map/reduce_sum | solution.py:209
  175.5 6.7 %fusion.3 = bf16[8,384,640]{2,1,0:T(8,128)(2,1)S(1)} fusion(f32[48,8,8,640]{3,2,1,0:T(8,128)} %bitcast.183, f32[48,8,8,640]{3,2,1,0:T(8,128)} %bitcast.182, f32[384]{0:T(512)S(1)} %get-tuple-element.28, f32[384]{0:T(512)S(1)} %get-tuple-element.27, bf16[8,384,640]{2,1,0:T(8,128)(2,1)S(1)} %copy-done.2, pred[8]{0:T(512)(128)(4,1)S(1)} %compare_and_fusion), kind=kLoop, calls=%fused_computation.12 | loop fusion | flops 13762560 | bytes 23596040 | tf_op jit(solution)/shard_map/convert_element_type | solution.py:216
  187.2 3.0 %collective-permute-done.11 = f32[384,16]{0,1:T(8,128)S(1)} collective-permute-done((f32[384,16]{0,1:T(8,128)S(1)}, f32[384,16]{0,1:T(8,128)S(1)}, u32[]{:S(2)}, u32[]{:S(2)}) %collective-permute-start.11) | collective-permute-done | bytes 24608 | tf_op jit(solution)/shard_map/ppermute | solution.py:62
  190.2 2.5 collective-permute-start.12
  196.0 11.5 %fusion.93 = (bf16[1,5120,864]{2,1,0:T(8,128)(2,1)S(1)}, bf16[1,5120,864]{2,1,0:T(8,128)(2,1)}) fusion(bf16[2,5120,864]{2,1,0:T(8,128)(2,1)} %all-gather.5.cloned.1.call-done), kind=kLoop, calls=%fused_computation.204 | loop fusion | bytes 35389440 | tf_op jit(solution)/shard_map/slice | solution.py:148
  207.5 7.4 %convolution_bitcast_fusion.1 = f32[384,864]{0,1:T(8,128)S(1)} fusion(bf16[8,384,640]{2,1,0:T(8,128)(2,1)S(1)} %copy-done.6, bf16[8,640,864]{2,1,0:T(8,128)(2,1)} %bitcast.189), kind=kOutput, calls=%fused_computation.43 | convolution fusion | flops 3397386240 | bytes 14106624 | tf_op jit(solution)/shard_map/mtc,mch->th/dot_general | solution.py:228
  215.6 2.3 convert_bitcast_fusion
  218.9 2.3 convert_bitcast_fusion.1
  228.8 4.4 %collective-permute-done.14 = bf16[192,640]{1,0:T(8,128)(2,1)S(1)} collective-permute-done((bf16[192,640]{1,0:T(8,128)(2,1)S(1)}, bf16[192,640]{1,0:T(8,128)(2,1)S(1)}, u32[]{:S(2)}, u32[]{:S(2)}) %collective-permute-start.14) | collective-permute-done | bytes 245792 | tf_op jit(solution)/shard_map/ppermute | solution.py:69
  240.1 7.3 %collective-permute-done.15 = bf16[384,640]{1,0:T(8,128)(2,1)S(1)} collective-permute-done((bf16[384,640]{1,0:T(8,128)(2,1)S(1)}, bf16[384,640]{1,0:T(8,128)(2,1)S(1)}, u32[]{:S(2)}, u32[]{:S(2)}) %collective-permute-start.15) | collective-permute-done | bytes 491552 | tf_op jit(solution)/shard_map/ppermute | solution.py:69
  247.7 2.5 fusion.43
  (147 shorter events, 53.3 us)
Async XLA Ops:
  6.5 208.4 %copy-start = (bf16[16,16,864]{2,1,0:T(8,128)(2,1)S(1)}, bf16[16,16,864]{2,1,0:T(8,128)(2,1)}, u32[]{:S(2)}) copy-start(bf16[16,16,864]{2,1,0:T(8,128)(2,1)} %param.25) | copy-start | bytes 1327108
  6.5 16.4 %copy-start.14 = (s32[16,4]{0,1:T(4,128)S(1)}, s32[16,4]{0,1:T(4,128)}, u32[]{:S(2)}) copy-start(s32[16,4]{0,1:T(4,128)} %param.17) | copy-start | bytes 772
  6.5 17.2 %copy-start.16 = (s32[64]{0:T(128)S(1)}, s32[64]{0:T(128)}, u32[]{:S(2)}) copy-start(s32[64]{0:T(128)} %param.18) | copy-start | bytes 772
  6.5 17.3 %copy-start.17 = (s32[8]{0:T(128)S(1)}, s32[8]{0:T(128)}, u32[]{:S(2)}) copy-start(s32[8]{0:T(128)} %param.19) | copy-start | bytes 100
  6.5 59.5 %all-gather.3.cloned.1.call-start = ((), (), s32[]{:S(2)}) async-start(), calls=%async_computation.2 | async-start | bytes 4177920 | tf_op jit(solution)/shard_map/all_gather | solution.py:144
  7.3 188.7 %all-gather.5.cloned.1.call-start = ((), (), s32[]{:S(2)}) async-start(), calls=%async_computation.3 | async-start | bytes 19496960 | tf_op jit(solution)/shard_map/all_gather | solution.py:146
  9.7 29.1 %copy-start.19 = (bf16[384,16,16]{0,2,1:T(8,128)(2,1)S(1)}, bf16[384,16,16]{0,2,1:T(8,128)(2,1)}, u32[]{:S(2)}) copy-start(bf16[384,16,16]{0,2,1:T(8,128)(2,1)} %param.21) | copy-start | bytes 589828
  14.5 22.1 %all-to-all-start.1 = ((bf16[36,16,384]{2,0,1:T(8,128)(2,1)}), bf16[36,16,384]{2,0,1:T(8,128)(2,1)S(1)}, u32[]{:S(2)}, u32[]{:S(2)}) async-start(bf16[36,16,384]{2,0,1:T(8,128)(2,1)} %copy.81), calls=%async_computation.1 | async-start | bytes 983040 | tf_op jit(solution)/shard_map/all_to_all | solution.py:156
  23.6 46.9 %copy-start.12 = (s32[1024]{0:T(1024)}, s32[1024]{0:T(1024)S(1)}, u32[]{:S(2)}) copy-start(s32[1024]{0:T(1024)S(1)} %pad_clamp_fusion.3) | copy-start | bytes 12292
  23.9 46.6 %copy-start.15 = (pred[384]{0:T(512)(128)(4,1)}, pred[384]{0:T(512)(128)(4,1)S(1)}, u32[]{:S(2)}) copy-start(pred[384]{0:T(512)(128)(4,1)S(1)} %compare_and_fusion.2) | copy-start | bytes 1156
  24.5 46.0 %copy-start.10 = (f32[384,16]{0,1:T(8,128)}, f32[384,16]{0,1:T(8,128)S(1)}, u32[]{:S(2)}) copy-start(f32[384,16]{0,1:T(8,128)S(1)} %get-tuple-element.30) | copy-start | bytes 73732
  73.0 5.0 %collective-permute-start = (bf16[4,394,640]{2,0,1:T(4,128)(2,1)}, bf16[4,394,640]{2,0,1:T(4,128)(2,1)S(1)}, u32[]{:S(2)}, u32[]{:S(2)}) collective-permute-start(bf16[4,394,640]{2,0,1:T(4,128)(2,1)} %copy.88), channel_id=1, source_target_pairs={{0,1},{1,0},{2,3},{3,2},{4,5},{5,4},{6,7},{7,6},{8,9},{9,8},{10,11... | collective-permute-start | bytes 6051848 | tf_op jit(solution)/shard_map/ppermute | solution.py:69
  74.1 10.8 %copy-start.7 = (bf16[576,640]{1,0:T(8,128)(2,1)S(1)}, bf16[576,640]{1,0:T(8,128)(2,1)}, u32[]{:S(2)}) copy-start(bf16[576,640]{1,0:T(8,128)(2,1)} %param.15) | copy-start | bytes 2211844
  82.2 10.2 %collective-permute-start.1 = (bf16[197,640]{1,0:T(8,128)(2,1)S(1)}, bf16[197,640]{1,0:T(8,128)(2,1)S(1)}, u32[]{:S(2)}, u32[]{:S(2)}) collective-permute-start(bf16[197,640]{1,0:T(8,128)(2,1)S(1)} %get-tuple-element.20), channel_id=1, source_target_pairs={{0,2},{1,3},{2,4},{3,5},{4,6},{5,7},{6,0},{7,1},{8,10},{9,11},{10,... | collective-permute-start | bytes 756488 | tf_op jit(solution)/shard_map/ppermute | solution.py:69
  83.5 8.9 %collective-permute-start.3 = (bf16[197,640]{1,0:T(8,128)(2,1)S(1)}, bf16[197,640]{1,0:T(8,128)(2,1)S(1)}, u32[]{:S(2)}, u32[]{:S(2)}) collective-permute-start(bf16[197,640]{1,0:T(8,128)(2,1)S(1)} %get-tuple-element.21), channel_id=1, source_target_pairs={{0,6},{1,7},{2,0},{3,1},{4,2},{5,3},{6,4},{7,5},{8,14},{9,15},{10,... | collective-permute-start | bytes 756488 | tf_op jit(solution)/shard_map/ppermute | solution.py:69
  86.5 25.4 %all-to-all-start = ((bf16[36,16,640]{2,0,1:T(8,128)(2,1)}), bf16[36,16,640]{2,0,1:T(8,128)(2,1)S(1)}, u32[]{:S(2)}, u32[]{:S(2)}) async-start(bf16[36,16,640]{2,0,1:T(8,128)(2,1)} %copy.79), calls=%async_computation | async-start | bytes 1638400 | tf_op jit(solution)/shard_map/all_to_all | solution.py:160
  93.8 20.6 %collective-permute-start.2 = (bf16[394,640]{1,0:T(8,128)(2,1)S(1)}, bf16[394,640]{1,0:T(8,128)(2,1)S(1)}, u32[]{:S(2)}, u32[]{:S(2)}) collective-permute-start(bf16[394,640]{1,0:T(8,128)(2,1)S(1)} %pad_maximum_fusion.3), channel_id=1, source_target_pairs={{0,2},{1,3},{2,4},{3,5},{4,6},{5,7},{6,0},{7,1},{8,10},{9,11},{10,... | collective-permute-start | bytes 1512968 | tf_op jit(solution)/shard_map/ppermute | solution.py:69
  94.8 19.6 %collective-permute-start.4 = (bf16[394,640]{1,0:T(8,128)(2,1)}, bf16[394,640]{1,0:T(8,128)(2,1)S(1)}, u32[]{:S(2)}, u32[]{:S(2)}) collective-permute-start(bf16[394,640]{1,0:T(8,128)(2,1)} %pad_maximum_fusion.4), channel_id=1, source_target_pairs={{0,6},{1,7},{2,0},{3,1},{4,2},{5,3},{6,4},{7,5},{8,14},{9,15},{10,... | collective-permute-start | bytes 1512968 | tf_op jit(solution)/shard_map/ppermute | solution.py:69
  117.5 2.5 collective-permute-start.5
  121.1 24.5 %collective-permute-start.6 = (bf16[2,384,640]{2,1,0:T(8,128)(2,1)}, bf16[2,384,640]{2,1,0:T(8,128)(2,1)S(1)}, u32[]{:S(2)}, u32[]{:S(2)}) collective-permute-start(bf16[2,384,640]{2,1,0:T(8,128)(2,1)} %get-tuple-element.19), channel_id=1, source_target_pairs={{0,2},{1,3},{2,4},{3,5},{4,6},{5,7},{6,0},{7,1},{8,10},{9,11},{10,... | collective-permute-start | bytes 2949128 | tf_op jit(solution)/shard_map/ppermute | solution.py:69
  122.3 24.1 %collective-permute-start.8 = (bf16[2,384,640]{2,1,0:T(8,128)(2,1)}, bf16[2,384,640]{2,1,0:T(8,128)(2,1)}, u32[]{:S(2)}, u32[]{:S(2)}) collective-permute-start(bf16[2,384,640]{2,1,0:T(8,128)(2,1)} %get-tuple-element.19), channel_id=1, source_target_pairs={{0,6},{1,7},{2,0},{3,1},{4,2},{5,3},{6,4},{7,5},{8,14},{9,15},{10,... | collective-permute-start | bytes 2949128 | tf_op jit(solution)/shard_map/ppermute | solution.py:69
  146.4 15.3 %collective-permute-start.7 = (bf16[1,384,640]{2,1,0:T(8,128)(2,1)}, bf16[1,384,640]{2,1,0:T(8,128)(2,1)}, u32[]{:S(2)}, u32[]{:S(2)}) collective-permute-start(bf16[1,384,640]{2,1,0:T(8,128)(2,1)} %slice.156), channel_id=1, source_target_pairs={{0,2},{1,3},{2,4},{3,5},{4,6},{5,7},{6,0},{7,1},{8,10},{9,11},{10,... | collective-permute-start | bytes 1474568 | tf_op jit(solution)/shard_map/ppermute | solution.py:69
  148.3 13.4 %collective-permute-start.9 = (bf16[1,384,640]{2,1,0:T(8,128)(2,1)}, bf16[1,384,640]{2,1,0:T(8,128)(2,1)}, u32[]{:S(2)}, u32[]{:S(2)}) collective-permute-start(bf16[1,384,640]{2,1,0:T(8,128)(2,1)} %slice.157), channel_id=1, source_target_pairs={{0,6},{1,7},{2,0},{3,1},{4,2},{5,3},{6,4},{7,5},{8,14},{9,15},{10,... | collective-permute-start | bytes 1474568 | tf_op jit(solution)/shard_map/ppermute | solution.py:69
  184.6 2.5 collective-permute-start.10
  187.1 3.1 %collective-permute-start.11 = (f32[384,16]{0,1:T(8,128)S(1)}, f32[384,16]{0,1:T(8,128)S(1)}, u32[]{:S(2)}, u32[]{:S(2)}) collective-permute-start(f32[384,16]{0,1:T(8,128)S(1)} %fusion.89), channel_id=1, source_target_pairs={{0,2},{1,3},{2,0},{3,1},{4,6},{5,7},{6,4},{7,5},{8,10},{9,11},{10,... | collective-permute-start | bytes 73736 | tf_op jit(solution)/shard_map/ppermute | solution.py:62
  190.2 4.2 %collective-permute-start.12 = (f32[384,16]{0,1:T(8,128)S(1)}, f32[384,16]{0,1:T(8,128)S(1)}, u32[]{:S(2)}, u32[]{:S(2)}) collective-permute-start(f32[384,16]{0,1:T(8,128)S(1)} %add.393), channel_id=1, source_target_pairs={{0,4},{1,5},{2,6},{3,7},{4,0},{5,1},{6,2},{7,3},{8,12},{9,13},{10,... | collective-permute-start | bytes 73736 | tf_op jit(solution)/shard_map/ppermute | solution.py:62
  196.0 11.5 %copy-start.6 = (bf16[8,384,640]{2,1,0:T(8,128)(2,1)S(1)}, bf16[8,384,640]{2,1,0:T(8,128)(2,1)}, u32[]{:S(2)}) copy-start(bf16[8,384,640]{2,1,0:T(8,128)(2,1)} %copy-done.5) | copy-start | bytes 11796484
  217.9 4.5 %collective-permute-start.13 = (bf16[4,384,640]{2,1,0:T(8,128)(2,1)S(1)}, bf16[4,384,640]{2,1,0:T(8,128)(2,1)S(1)}, u32[]{:S(2)}, u32[]{:S(2)}) collective-permute-start(bf16[4,384,640]{2,1,0:T(8,128)(2,1)S(1)} %convert_bitcast_fusion), channel_id=1, source_target_pairs={{0,1},{1,0},{2,3},{3,2},{4,5},{5,4},{6,7},{7,6},{8,9},{9,8},{10,11... | collective-permute-start | bytes 5898248 | tf_op jit(solution)/shard_map/ppermute | solution.py:69
  224.8 8.4 %collective-permute-start.14 = (bf16[192,640]{1,0:T(8,128)(2,1)S(1)}, bf16[192,640]{1,0:T(8,128)(2,1)S(1)}, u32[]{:S(2)}, u32[]{:S(2)}) collective-permute-start(bf16[192,640]{1,0:T(8,128)(2,1)S(1)} %get-tuple-element.25), channel_id=1, source_target_pairs={{0,2},{1,3},{2,4},{3,5},{4,6},{5,7},{6,0},{7,1},{8,10},{9,11},{10,... | collective-permute-start | bytes 737288 | tf_op jit(solution)/shard_map/ppermute | solution.py:69
  226.1 7.2 %collective-permute-start.16 = (bf16[192,640]{1,0:T(8,128)(2,1)S(1)}, bf16[192,640]{1,0:T(8,128)(2,1)S(1)}, u32[]{:S(2)}, u32[]{:S(2)}) collective-permute-start(bf16[192,640]{1,0:T(8,128)(2,1)S(1)} %get-tuple-element.26), channel_id=1, source_target_pairs={{0,6},{1,7},{2,0},{3,1},{4,2},{5,3},{6,4},{7,5},{8,14},{9,15},{10,... | collective-permute-start | bytes 737288 | tf_op jit(solution)/shard_map/ppermute | solution.py:69
  234.6 12.8 %collective-permute-start.15 = (bf16[384,640]{1,0:T(8,128)(2,1)S(1)}, bf16[384,640]{1,0:T(8,128)(2,1)S(1)}, u32[]{:S(2)}, u32[]{:S(2)}) collective-permute-start(bf16[384,640]{1,0:T(8,128)(2,1)S(1)} %pad_maximum_fusion.5), channel_id=1, source_target_pairs={{0,2},{1,3},{2,4},{3,5},{4,6},{5,7},{6,0},{7,1},{8,10},{9,11},{10,... | collective-permute-start | bytes 1474568 | tf_op jit(solution)/shard_map/ppermute | solution.py:69
  236.4 11.3 %collective-permute-start.17 = (bf16[384,640]{1,0:T(8,128)(2,1)}, bf16[384,640]{1,0:T(8,128)(2,1)}, u32[]{:S(2)}, u32[]{:S(2)}) collective-permute-start(bf16[384,640]{1,0:T(8,128)(2,1)} %pad_maximum_fusion.6), channel_id=1, source_target_pairs={{0,6},{1,7},{2,0},{3,1},{4,2},{5,3},{6,4},{7,5},{8,14},{9,15},{10,... | collective-permute-start | bytes 1474568 | tf_op jit(solution)/shard_map/ppermute | solution.py:69
  (10 other events, 51.5 us)
Sparse Core Ops, SparseCore 0:
  9.5 56.5 all-gather.2
  68.2 127.7 all-gather.4

commit v5 on v4

--- a/solution.py
+++ b/solution.py
@@ -156,10 +156,11 @@
     moved_attn = lax.all_to_all(
         send_layout(attention_output, offset, req_count), "req", split_axis=1, concat_axis=1, tiled=True
     )
-    attention_rows = compact(moved_attn, dev_starts, dev_ends, req_count, token_rank)
     moved_res = lax.all_to_all(
         send_layout(residual_input, offset, req_count), "req", split_axis=1, concat_axis=1, tiled=True
     )
+    moved_attn, moved_res = lax.optimization_barrier((moved_attn, moved_res))
+    attention_rows = compact(moved_attn, dev_starts, dev_ends, req_count, token_rank)
     residual_rows = compact(moved_res, dev_starts, dev_ends, req_count, token_rank)
 
     group_ids, adapter_hot = token_groups(token_rank, request_length, request_group, adapter_per_group)

time: 259 us -> 258 us (level)
  waiting for transfers between devices: 90.6 us -> 85.6 us
  starting transfers between devices: 36.5 us -> 39.9 us
    all_gather x1, waiting for transfers between devices: 26.6 us -> 13 us  [local(): out_w = lax.all_gather(output_weight, 'req', axis=1, tiled=True)]
    ppermute x15, waiting for transfers between devices: 29.5 us -> 43 us  [mlp_move(): return lax.ppermute(block, 'mlp', [(i, target(i)) for i in range(n)])]
    ppermute x15, starting transfers between devices: 19.3 us -> 23.2 us  [mlp_move(): return lax.ppermute(block, 'mlp', [(i, target(i)) for i in range(n)])]
    unnamed x41 -> x43, local copies, waits for them, and re-layouts: 5.93 us -> 5.92 us
  transfers between devices with their start and end apart: 22 -> 22, of which waited for: 14 -> 16; matrix products, arithmetic and copies ran while one was open for 32% -> 32% of each run, Pallas kernels for 0% -> 0%
where the time goes in v5:
time: 258 us; the launch traced here: 256 us
  waiting for transfers between devices  85.6 us (33%)
  local copies, waits for them, and re-layouts  51 us (20%)
  other arithmetic  44.4 us (17%)
  starting transfers between devices  39.9 us (15%)
  matrix products  19.3 us (7%)
  between operations  15.9 us (6%)
    ppermute x15, waiting for transfers between devices, mlp_move(): return lax.ppermute(block, 'mlp', [(i, target(i)) for i in range(n)])  43 us
    ppermute x15, starting transfers between devices, mlp_move(): return lax.ppermute(block, 'mlp', [(i, target(i)) for i in range(n)])  23.2 us
    all_gather x1, waiting for transfers between devices, local(): out_w = lax.all_gather(output_weight, 'req', axis=1, tiled=True)  13 us
    all_to_all x1, waiting for transfers between devices, local(): lax.all_to_all(send_layout(residual_input, offset, req_count), 'req', spl...  12.5 us
    slice x1, local copies, waits for them, and re-layouts, local(): down_t = both[1]  11.6 us
    all_to_all x1, waiting for transfers between devices, local(): lax.all_to_all(send_layout(attention_output, offset, req_count), 'req', s...  11.3 us
    add x1, other arithmetic, local(): 1.0 + scale_rows  10.3 us
    all_to_all x1, starting transfers between devices, local(): lax.all_to_all(send_layout(attention_output, offset, req_count), 'req', s...  8.42 us
  transfers between devices with their start and end apart: 22, of which 16 were waited for; matrix products, arithmetic and copies ran while one was open for 32% of the time, Pallas kernels for 0%

profile of v5, /device:TPU:1, one launch (start us, length us, event | category | flops | bytes accessed | tf_op | source)
XLA Modules:
  0.0 256.2 jit_solution(2811142501838222903)
XLA Ops:
  7.3 2.4 pad_maximum_fusion.1
  14.5 8.4 %all-to-all-start = ((bf16[36,16,384]{2,0,1:T(8,128)(2,1)}), bf16[36,16,384]{2,0,1:T(8,128)(2,1)S(1)}, u32[]{:S(2)}, u32[]{:S(2)}) async-start(bf16[36,16,384]{2,0,1:T(8,128)(2,1)} %copy.79), calls=%async_computation | async-start | bytes 983040 | tf_op jit(solution)/shard_map/all_to_all | solution.py:156
  25.2 11.3 %all-to-all-done = bf16[36,16,384]{2,0,1:T(8,128)(2,1)S(1)} async-done(((bf16[36,16,384]{2,0,1:T(8,128)(2,1)}), bf16[36,16,384]{2,0,1:T(8,128)(2,1)S(1)}, u32[]{:S(2)}, u32[]{:S(2)}) %all-to-all-start) | async-done | bytes 442400 | tf_op jit(solution)/shard_map/all_to_all | solution.py:156
  36.5 3.6 %all-to-all-start.1 = ((bf16[36,16,640]{2,0,1:T(8,128)(2,1)}), bf16[36,16,640]{2,0,1:T(8,128)(2,1)S(1)}, u32[]{:S(2)}, u32[]{:S(2)}) async-start(bf16[36,16,640]{2,0,1:T(8,128)(2,1)} %copy.80), calls=%async_computation.1 | async-start | bytes 1638400 | tf_op jit(solution)/shard_map/all_to_all | solution.py:159
  41.6 12.5 %all-to-all-done.1 = bf16[36,16,640]{2,0,1:T(8,128)(2,1)S(1)} async-done(((bf16[36,16,640]{2,0,1:T(8,128)(2,1)}), bf16[36,16,640]{2,0,1:T(8,128)(2,1)S(1)}, u32[]{:S(2)}, u32[]{:S(2)}) %all-to-all-start.1) | async-done | bytes 737312 | tf_op jit(solution)/shard_map/all_to_all | solution.py:159
  57.0 13.0 %all-gather.3.cloned.1.call-done = bf16[384,5120]{0,1:T(8,128)(2,1)} async-done(((bf16[384,320]{0,1:T(8,128)(2,1)}), bf16[384,5120]{0,1:T(8,128)(2,1)}) %all-gather.3.cloned.1.call-update) | async-done | bytes 3932176 | tf_op jit(solution)/shard_map/all_gather | solution.py:144
  70.0 4.4 %convolution_convert_fusion = bf16[384,8,640]{2,0,1:T(8,128)(2,1)S(1)} fusion(bf16[384,8,640]{0,2,1:T(8,128)(2,1)} %bitcast.190, bf16[384,384]{1,0:T(8,128)(2,1)S(1)} %gather_fusion.1, pred[384]{0:T(512)(128)(4,1)S(1)} %compare_and_fusion.2), kind=kOutput, calls=%fused_computation.32 | convolution fusion | flops 1512062976 | bytes 8159616 | tf_op jit(solution)/shard_map/tk,kmc->mtc/dot_general | solution.py:172
  74.6 2.4 copy.88
  77.6 4.0 %collective-permute-done = bf16[4,394,640]{2,0,1:T(4,128)(2,1)} collective-permute-done((bf16[4,394,640]{2,0,1:T(4,128)(2,1)}, bf16[4,394,640]{2,0,1:T(4,128)(2,1)}, u32[]{:S(2)}, u32[]{:S(2)}) %collective-permute-start) | collective-permute-done | bytes 2017312 | tf_op jit(solution)/shard_map/ppermute | solution.py:69
  81.6 2.8 %convert_add_fusion = f32[4,394,640]{2,1,0:T(8,128)S(1)} fusion(s32[]{:T(128)S(6)} %select_n.257, bf16[4,2,10,640]{3,2,0,1:T(8,128)(2,1)S(1)} %broadcast_in_dim.135, bf16[4,394,640]{2,0,1:T(4,128)(2,1)} %collective-permute-done, bf16[4,2,384,640]{3,2,1,0:T(8,128)(2,1)} %bitcast.181), kind=kLoop, calls=%fused_computation.25 | loop fusion | flops 7060480 | bytes 10086404 | tf_op jit(solution)/shard_map/add | solution.py:86
  90.9 4.9 %collective-permute-done.1 = bf16[197,640]{1,0:T(8,128)(2,1)S(1)} collective-permute-done((bf16[197,640]{1,0:T(8,128)(2,1)S(1)}, bf16[197,640]{1,0:T(8,128)(2,1)S(1)}, u32[]{:S(2)}, u32[]{:S(2)}) %collective-permute-start.1) | collective-permute-done | bytes 252192 | tf_op jit(solution)/shard_map/ppermute | solution.py:69
  100.9 2.3 gather_fusion
  103.2 7.6 %collective-permute-done.2 = bf16[394,640]{1,0:T(8,128)(2,1)S(1)} collective-permute-done((bf16[394,640]{1,0:T(8,128)(2,1)S(1)}, bf16[394,640]{1,0:T(8,128)(2,1)S(1)}, u32[]{:S(2)}, u32[]{:S(2)}) %collective-permute-start.2) | collective-permute-done | bytes 504352 | tf_op jit(solution)/shard_map/ppermute | solution.py:69
  114.2 2.4 collective-permute-start.5
  122.5 5.4 %gather_fusion.4 = f32[384,5120]{1,0:T(8,128)} fusion(f32[8,5120]{1,0:T(8,128)S(1)} %get-tuple-element.28, s32[1024]{0:T(1024)S(1)} %pad_clamp_fusion), kind=kCustom, calls=%fused_computation.clone | custom fusion | bytes 15730176 | tf_op jit(solution)/shard_map/jit(_take)/gather | solution.py:168
  127.9 5.5 %gather_fusion.5 = f32[384,5120]{1,0:T(8,128)} fusion(f32[8,5120]{1,0:T(8,128)S(1)} %get-tuple-element.27, s32[1024]{0:T(1024)S(1)} %pad_clamp_fusion), kind=kCustom, calls=%fused_computation.1.clone | custom fusion | bytes 15730176 | tf_op jit(solution)/shard_map/jit(_take)/gather | solution.py:167
  133.4 11.1 %collective-permute-done.6 = bf16[2,384,640]{2,1,0:T(8,128)(2,1)S(1)} collective-permute-done((bf16[2,384,640]{2,1,0:T(8,128)(2,1)}, bf16[2,384,640]{2,1,0:T(8,128)(2,1)S(1)}, u32[]{:S(2)}, u32[]{:S(2)}) %collective-permute-start.6) | collective-permute-done | bytes 983072 | tf_op jit(solution)/shard_map/ppermute | solution.py:69
  147.2 2.7 %collective-permute-start.9 = (bf16[1,384,640]{2,1,0:T(8,128)(2,1)}, bf16[1,384,640]{2,1,0:T(8,128)(2,1)}, u32[]{:S(2)}, u32[]{:S(2)}) collective-permute-start(bf16[1,384,640]{2,1,0:T(8,128)(2,1)} %slice.157), channel_id=1, source_target_pairs={{0,6},{1,7},{2,0},{3,1},{4,2},{5,3},{6,4},{7,5},{8,14},{9,15},{10,... | collective-permute-start | bytes 1474568 | tf_op jit(solution)/shard_map/ppermute | solution.py:69
  149.9 10.3 %select_add_fusion = (f32[384,5120]{1,0:T(8,128)}, f32[384,5120]{1,0:T(8,128)}) fusion(f32[384,5120]{1,0:T(8,128)} %gather_fusion.4, pred[384]{0:T(512)(128)(4,1)S(1)} %compare_and_fusion.1, f32[384,5120]{1,0:T(8,128)} %gather_fusion.5), kind=kLoop, calls=%fused_computation.16 | loop fusion | flops 5898240 | bytes 31457664 | tf_op jit(solution)/shard_map/add | solution.py:213
  161.6 3.4 %pad_maximum_fusion = bf16[4,2,384,640]{3,2,1,0:T(8,128)(2,1)} fusion(bf16[1,2,384,640]{3,2,1,0:T(8,128)(2,1)} %bitcast.34, bf16[1,2,384,640]{3,2,1,0:T(8,128)(2,1)S(1)} %maximum_bitcast_fusion, bf16[1,2,384,640]{3,2,1,0:T(8,128)(2,1)S(1)} %bitcast.191, bf16[1,2,384,640]{3,2,1,0:T(8,128)(2,1)S(1)} %get-tuple-element.22), kind=kLoop, calls=%fused_computation.26 | loop fusion | flops 5898240 | bytes 7864320 | tf_op jit(solution)/shard_map/stack | solution.py:116
  165.0 5.1 %gather_fusion.3 = bf16[8,384,640]{2,1,0:T(8,128)(2,1)} fusion(bf16[8,384,640]{2,1,0:T(8,128)(2,1)} %bitcast.186, s32[1024]{0:T(1024)S(1)} %pad_clamp_fusion.1), kind=kCustom, calls=%fused_computation.5 | custom fusion | bytes 7864352 | tf_op jit(solution)/shard_map/jit(_take)/gather | solution.py:119
  170.1 3.7 %convert_reduce_fusion = (f32[384]{0:T(512)S(1)}, f32[384]{0:T(512)S(1)}) fusion(bf16[8,384,640]{2,1,0:T(8,128)(2,1)} %gather_fusion.3, pred[8]{0:T(512)(128)(4,1)S(1)} %compare_and_fusion), kind=kLoop, calls=%fused_computation.8 | loop fusion | flops 9829632 | bytes 3935240 | tf_op jit(solution)/shard_map/reduce_sum | solution.py:210
  173.9 6.7 %fusion.3 = bf16[8,384,640]{2,1,0:T(8,128)(2,1)S(1)} fusion(f32[48,8,8,640]{3,2,1,0:T(8,128)} %bitcast.183, f32[48,8,8,640]{3,2,1,0:T(8,128)} %bitcast.182, f32[384]{0:T(512)S(1)} %get-tuple-element.32, f32[384]{0:T(512)S(1)} %get-tuple-element.31, bf16[8,384,640]{2,1,0:T(8,128)(2,1)S(1)} %copy-done.2, pred[8]{0:T(512)(128)(4,1)S(1)} %compare_and_fusion), kind=kLoop, calls=%fused_computation.12 | loop fusion | flops 13762560 | bytes 23596040 | tf_op jit(solution)/shard_map/convert_element_type | solution.py:217
  185.4 3.1 %collective-permute-done.11 = f32[384,16]{0,1:T(8,128)S(1)} collective-permute-done((f32[384,16]{0,1:T(8,128)S(1)}, f32[384,16]{0,1:T(8,128)S(1)}, u32[]{:S(2)}, u32[]{:S(2)}) %collective-permute-start.11) | collective-permute-done | bytes 24608 | tf_op jit(solution)/shard_map/ppermute | solution.py:62
  188.5 3.1 %collective-permute-start.12 = (f32[384,16]{0,1:T(8,128)S(1)}, f32[384,16]{0,1:T(8,128)S(1)}, u32[]{:S(2)}, u32[]{:S(2)}) collective-permute-start(f32[384,16]{0,1:T(8,128)S(1)} %add.393), channel_id=1, source_target_pairs={{0,4},{1,5},{2,6},{3,7},{4,0},{5,1},{6,2},{7,3},{8,12},{9,13},{10,... | collective-permute-start | bytes 73736 | tf_op jit(solution)/shard_map/ppermute | solution.py:62
  192.8 11.6 %fusion.93 = (bf16[1,5120,864]{2,1,0:T(8,128)(2,1)S(1)}, bf16[1,5120,864]{2,1,0:T(8,128)(2,1)}) fusion(bf16[2,5120,864]{2,1,0:T(8,128)(2,1)} %all-gather.5.cloned.1.call-done), kind=kLoop, calls=%fused_computation.204 | loop fusion | bytes 35389440 | tf_op jit(solution)/shard_map/slice | solution.py:148
  204.3 7.4 %convolution_bitcast_fusion.1 = f32[384,864]{0,1:T(8,128)S(1)} fusion(bf16[8,384,640]{2,1,0:T(8,128)(2,1)S(1)} %copy-done.6, bf16[8,640,864]{2,1,0:T(8,128)(2,1)} %bitcast.189), kind=kOutput, calls=%fused_computation.43 | convolution fusion | flops 3397386240 | bytes 14106624 | tf_op jit(solution)/shard_map/mtc,mch->th/dot_general | solution.py:229
  217.0 2.3 convert_bitcast_fusion.1
  223.7 2.8 %collective-permute-start.16 = (bf16[192,640]{1,0:T(8,128)(2,1)S(1)}, bf16[192,640]{1,0:T(8,128)(2,1)S(1)}, u32[]{:S(2)}, u32[]{:S(2)}) collective-permute-start(bf16[192,640]{1,0:T(8,128)(2,1)S(1)} %get-tuple-element.30), channel_id=1, source_target_pairs={{0,6},{1,7},{2,0},{3,1},{4,2},{5,3},{6,4},{7,5},{8,14},{9,15},{10,... | collective-permute-start | bytes 737288 | tf_op jit(solution)/shard_map/ppermute | solution.py:69
  227.7 4.6 %collective-permute-done.14 = bf16[192,640]{1,0:T(8,128)(2,1)S(1)} collective-permute-done((bf16[192,640]{1,0:T(8,128)(2,1)S(1)}, bf16[192,640]{1,0:T(8,128)(2,1)S(1)}, u32[]{:S(2)}, u32[]{:S(2)}) %collective-permute-start.14) | collective-permute-done | bytes 245792 | tf_op jit(solution)/shard_map/ppermute | solution.py:69
  239.1 7.6 %collective-permute-done.15 = bf16[384,640]{1,0:T(8,128)(2,1)S(1)} collective-permute-done((bf16[384,640]{1,0:T(8,128)(2,1)S(1)}, bf16[384,640]{1,0:T(8,128)(2,1)S(1)}, u32[]{:S(2)}, u32[]{:S(2)}) %collective-permute-start.15) | collective-permute-done | bytes 491552 | tf_op jit(solution)/shard_map/ppermute | solution.py:69
  246.9 2.5 fusion.43
  (148 shorter events, 59.4 us)
Async XLA Ops:
  6.5 205.2 %copy-start = (bf16[16,16,864]{2,1,0:T(8,128)(2,1)S(1)}, bf16[16,16,864]{2,1,0:T(8,128)(2,1)}, u32[]{:S(2)}) copy-start(bf16[16,16,864]{2,1,0:T(8,128)(2,1)} %param.25) | copy-start | bytes 1327108
  6.5 16.4 %copy-start.14 = (s32[16,4]{0,1:T(4,128)S(1)}, s32[16,4]{0,1:T(4,128)}, u32[]{:S(2)}) copy-start(s32[16,4]{0,1:T(4,128)} %param.17) | copy-start | bytes 772
  6.5 16.5 %copy-start.7 = (bf16[576,640]{1,0:T(8,128)(2,1)S(1)}, bf16[576,640]{1,0:T(8,128)(2,1)}, u32[]{:S(2)}) copy-start(bf16[576,640]{1,0:T(8,128)(2,1)} %param.15) | copy-start | bytes 2211844
  6.5 63.4 %all-gather.3.cloned.1.call-start = ((), (), s32[]{:S(2)}) async-start(), calls=%async_computation.2 | async-start | bytes 4177920 | tf_op jit(solution)/shard_map/all_gather | solution.py:144
  7.3 185.5 %all-gather.5.cloned.1.call-start = ((), (), s32[]{:S(2)}) async-start(), calls=%async_computation.3 | async-start | bytes 19496960 | tf_op jit(solution)/shard_map/all_gather | solution.py:146
  9.7 15.4 %copy-start.17 = (s32[64]{0:T(128)S(1)}, s32[64]{0:T(128)}, u32[]{:S(2)}) copy-start(s32[64]{0:T(128)} %param.18) | copy-start | bytes 772
  9.7 31.1 %copy-start.18 = (s32[8]{0:T(128)S(1)}, s32[8]{0:T(128)}, u32[]{:S(2)}) copy-start(s32[8]{0:T(128)} %param.19) | copy-start | bytes 100
  14.5 22.1 %all-to-all-start = ((bf16[36,16,384]{2,0,1:T(8,128)(2,1)}), bf16[36,16,384]{2,0,1:T(8,128)(2,1)S(1)}, u32[]{:S(2)}, u32[]{:S(2)}) async-start(bf16[36,16,384]{2,0,1:T(8,128)(2,1)} %copy.79), calls=%async_computation | async-start | bytes 983040 | tf_op jit(solution)/shard_map/all_to_all | solution.py:156
  23.0 33.3 %copy-start.20 = (bf16[384,16,16]{0,2,1:T(8,128)(2,1)S(1)}, bf16[384,16,16]{0,2,1:T(8,128)(2,1)}, u32[]{:S(2)}) copy-start(bf16[384,16,16]{0,2,1:T(8,128)(2,1)} %param.21) | copy-start | bytes 589828
  36.5 17.6 %all-to-all-start.1 = ((bf16[36,16,640]{2,0,1:T(8,128)(2,1)}), bf16[36,16,640]{2,0,1:T(8,128)(2,1)S(1)}, u32[]{:S(2)}, u32[]{:S(2)}) async-start(bf16[36,16,640]{2,0,1:T(8,128)(2,1)} %copy.80), calls=%async_computation.1 | async-start | bytes 1638400 | tf_op jit(solution)/shard_map/all_to_all | solution.py:159
  40.9 33.5 %copy-start.12 = (s32[1024]{0:T(1024)}, s32[1024]{0:T(1024)S(1)}, u32[]{:S(2)}) copy-start(s32[1024]{0:T(1024)S(1)} %pad_clamp_fusion.3) | copy-start | bytes 12292
  41.0 33.4 %copy-start.16 = (pred[384]{0:T(512)(128)(4,1)}, pred[384]{0:T(512)(128)(4,1)S(1)}, u32[]{:S(2)}) copy-start(pred[384]{0:T(512)(128)(4,1)S(1)} %compare_and_fusion.2) | copy-start | bytes 1156
  41.6 32.8 %copy-start.10 = (f32[384,16]{0,1:T(8,128)}, f32[384,16]{0,1:T(8,128)S(1)}, u32[]{:S(2)}) copy-start(f32[384,16]{0,1:T(8,128)S(1)} %get-tuple-element.34) | copy-start | bytes 73732
  77.0 4.5 %collective-permute-start = (bf16[4,394,640]{2,0,1:T(4,128)(2,1)}, bf16[4,394,640]{2,0,1:T(4,128)(2,1)}, u32[]{:S(2)}, u32[]{:S(2)}) collective-permute-start(bf16[4,394,640]{2,0,1:T(4,128)(2,1)} %copy.88), channel_id=1, source_target_pairs={{0,1},{1,0},{2,3},{3,2},{4,5},{5,4},{6,7},{7,6},{8,9},{9,8},{10,11... | collective-permute-start | bytes 6051848 | tf_op jit(solution)/shard_map/ppermute | solution.py:69
  86.5 9.3 %collective-permute-start.1 = (bf16[197,640]{1,0:T(8,128)(2,1)S(1)}, bf16[197,640]{1,0:T(8,128)(2,1)S(1)}, u32[]{:S(2)}, u32[]{:S(2)}) collective-permute-start(bf16[197,640]{1,0:T(8,128)(2,1)S(1)} %get-tuple-element.24), channel_id=1, source_target_pairs={{0,2},{1,3},{2,4},{3,5},{4,6},{5,7},{6,0},{7,1},{8,10},{9,11},{10,... | collective-permute-start | bytes 756488 | tf_op jit(solution)/shard_map/ppermute | solution.py:69
  87.9 7.8 %collective-permute-start.3 = (bf16[197,640]{1,0:T(8,128)(2,1)S(1)}, bf16[197,640]{1,0:T(8,128)(2,1)S(1)}, u32[]{:S(2)}, u32[]{:S(2)}) collective-permute-start(bf16[197,640]{1,0:T(8,128)(2,1)S(1)} %get-tuple-element.25), channel_id=1, source_target_pairs={{0,6},{1,7},{2,0},{3,1},{4,2},{5,3},{6,4},{7,5},{8,14},{9,15},{10,... | collective-permute-start | bytes 756488 | tf_op jit(solution)/shard_map/ppermute | solution.py:69
  97.2 13.6 %collective-permute-start.2 = (bf16[394,640]{1,0:T(8,128)(2,1)S(1)}, bf16[394,640]{1,0:T(8,128)(2,1)S(1)}, u32[]{:S(2)}, u32[]{:S(2)}) collective-permute-start(bf16[394,640]{1,0:T(8,128)(2,1)S(1)} %pad_maximum_fusion.3), channel_id=1, source_target_pairs={{0,2},{1,3},{2,4},{3,5},{4,6},{5,7},{6,0},{7,1},{8,10},{9,11},{10,... | collective-permute-start | bytes 1512968 | tf_op jit(solution)/shard_map/ppermute | solution.py:69
  98.7 12.3 %collective-permute-start.4 = (bf16[394,640]{1,0:T(8,128)(2,1)}, bf16[394,640]{1,0:T(8,128)(2,1)S(1)}, u32[]{:S(2)}, u32[]{:S(2)}) collective-permute-start(bf16[394,640]{1,0:T(8,128)(2,1)} %pad_maximum_fusion.4), channel_id=1, source_target_pairs={{0,6},{1,7},{2,0},{3,1},{4,2},{5,3},{6,4},{7,5},{8,14},{9,15},{10,... | collective-permute-start | bytes 1512968 | tf_op jit(solution)/shard_map/ppermute | solution.py:69
  114.2 3.9 %collective-permute-start.5 = (bf16[384,640]{1,0:T(8,128)(2,1)S(1)}, bf16[384,640]{1,0:T(8,128)(2,1)S(1)}, u32[]{:S(2)}, u32[]{:S(2)}) collective-permute-start(bf16[384,640]{1,0:T(8,128)(2,1)S(1)} %fusion.33), channel_id=1, source_target_pairs={{0,1},{1,0},{2,3},{3,2},{4,5},{5,4},{6,7},{7,6},{8,9},{9,8},{10,11... | collective-permute-start | bytes 1474568 | tf_op jit(solution)/shard_map/ppermute | solution.py:69
  119.2 25.4 %collective-permute-start.6 = (bf16[2,384,640]{2,1,0:T(8,128)(2,1)}, bf16[2,384,640]{2,1,0:T(8,128)(2,1)S(1)}, u32[]{:S(2)}, u32[]{:S(2)}) collective-permute-start(bf16[2,384,640]{2,1,0:T(8,128)(2,1)} %get-tuple-element.23), channel_id=1, source_target_pairs={{0,2},{1,3},{2,4},{3,5},{4,6},{5,7},{6,0},{7,1},{8,10},{9,11},{10,... | collective-permute-start | bytes 2949128 | tf_op jit(solution)/shard_map/ppermute | solution.py:69
  120.4 24.9 %collective-permute-start.8 = (bf16[2,384,640]{2,1,0:T(8,128)(2,1)}, bf16[2,384,640]{2,1,0:T(8,128)(2,1)}, u32[]{:S(2)}, u32[]{:S(2)}) collective-permute-start(bf16[2,384,640]{2,1,0:T(8,128)(2,1)} %get-tuple-element.23), channel_id=1, source_target_pairs={{0,6},{1,7},{2,0},{3,1},{4,2},{5,3},{6,4},{7,5},{8,14},{9,15},{10,... | collective-permute-start | bytes 2949128 | tf_op jit(solution)/shard_map/ppermute | solution.py:69
  145.4 14.9 %collective-permute-start.7 = (bf16[1,384,640]{2,1,0:T(8,128)(2,1)}, bf16[1,384,640]{2,1,0:T(8,128)(2,1)}, u32[]{:S(2)}, u32[]{:S(2)}) collective-permute-start(bf16[1,384,640]{2,1,0:T(8,128)(2,1)} %slice.156), channel_id=1, source_target_pairs={{0,2},{1,3},{2,4},{3,5},{4,6},{5,7},{6,0},{7,1},{8,10},{9,11},{10,... | collective-permute-start | bytes 1474568 | tf_op jit(solution)/shard_map/ppermute | solution.py:69
  147.2 13.1 %collective-permute-start.9 = (bf16[1,384,640]{2,1,0:T(8,128)(2,1)}, bf16[1,384,640]{2,1,0:T(8,128)(2,1)}, u32[]{:S(2)}, u32[]{:S(2)}) collective-permute-start(bf16[1,384,640]{2,1,0:T(8,128)(2,1)} %slice.157), channel_id=1, source_target_pairs={{0,6},{1,7},{2,0},{3,1},{4,2},{5,3},{6,4},{7,5},{8,14},{9,15},{10,... | collective-permute-start | bytes 1474568 | tf_op jit(solution)/shard_map/ppermute | solution.py:69
  183.0 2.4 collective-permute-start.10
  185.4 3.1 %collective-permute-start.11 = (f32[384,16]{0,1:T(8,128)S(1)}, f32[384,16]{0,1:T(8,128)S(1)}, u32[]{:S(2)}, u32[]{:S(2)}) collective-permute-start(f32[384,16]{0,1:T(8,128)S(1)} %fusion.89), channel_id=1, source_target_pairs={{0,2},{1,3},{2,0},{3,1},{4,6},{5,7},{6,4},{7,5},{8,10},{9,11},{10,... | collective-permute-start | bytes 73736 | tf_op jit(solution)/shard_map/ppermute | solution.py:62
  188.5 4.3 %collective-permute-start.12 = (f32[384,16]{0,1:T(8,128)S(1)}, f32[384,16]{0,1:T(8,128)S(1)}, u32[]{:S(2)}, u32[]{:S(2)}) collective-permute-start(f32[384,16]{0,1:T(8,128)S(1)} %add.393), channel_id=1, source_target_pairs={{0,4},{1,5},{2,6},{3,7},{4,0},{5,1},{6,2},{7,3},{8,12},{9,13},{10,... | collective-permute-start | bytes 73736 | tf_op jit(solution)/shard_map/ppermute | solution.py:62
  214.8 5.8 %collective-permute-start.13 = (bf16[4,384,640]{2,1,0:T(8,128)(2,1)S(1)}, bf16[4,384,640]{2,1,0:T(8,128)(2,1)S(1)}, u32[]{:S(2)}, u32[]{:S(2)}) collective-permute-start(bf16[4,384,640]{2,1,0:T(8,128)(2,1)S(1)} %convert_bitcast_fusion), channel_id=1, source_target_pairs={{0,1},{1,0},{2,3},{3,2},{4,5},{5,4},{6,7},{7,6},{8,9},{9,8},{10,11... | collective-permute-start | bytes 5898248 | tf_op jit(solution)/shard_map/ppermute | solution.py:69
  222.8 14.4 %copy-start.15 = (s32[384]{0:T(512)S(1)}, s32[384]{0:T(512)}, u32[]{:S(2)}) copy-start(s32[384]{0:T(512)} %get-tuple-element.38) | copy-start | bytes 4612
  222.9 9.4 %collective-permute-start.14 = (bf16[192,640]{1,0:T(8,128)(2,1)S(1)}, bf16[192,640]{1,0:T(8,128)(2,1)S(1)}, u32[]{:S(2)}, u32[]{:S(2)}) collective-permute-start(bf16[192,640]{1,0:T(8,128)(2,1)S(1)} %get-tuple-element.29), channel_id=1, source_target_pairs={{0,2},{1,3},{2,4},{3,5},{4,6},{5,7},{6,0},{7,1},{8,10},{9,11},{10,... | collective-permute-start | bytes 737288 | tf_op jit(solution)/shard_map/ppermute | solution.py:69
  223.7 8.6 %collective-permute-start.16 = (bf16[192,640]{1,0:T(8,128)(2,1)S(1)}, bf16[192,640]{1,0:T(8,128)(2,1)S(1)}, u32[]{:S(2)}, u32[]{:S(2)}) collective-permute-start(bf16[192,640]{1,0:T(8,128)(2,1)S(1)} %get-tuple-element.30), channel_id=1, source_target_pairs={{0,6},{1,7},{2,0},{3,1},{4,2},{5,3},{6,4},{7,5},{8,14},{9,15},{10,... | collective-permute-start | bytes 737288 | tf_op jit(solution)/shard_map/ppermute | solution.py:69
  233.6 13.1 %collective-permute-start.15 = (bf16[384,640]{1,0:T(8,128)(2,1)S(1)}, bf16[384,640]{1,0:T(8,128)(2,1)S(1)}, u32[]{:S(2)}, u32[]{:S(2)}) collective-permute-start(bf16[384,640]{1,0:T(8,128)(2,1)S(1)} %pad_maximum_fusion.5), channel_id=1, source_target_pairs={{0,2},{1,3},{2,4},{3,5},{4,6},{5,7},{6,0},{7,1},{8,10},{9,11},{10,... | collective-permute-start | bytes 1474568 | tf_op jit(solution)/shard_map/ppermute | solution.py:69
  235.1 11.8 %collective-permute-start.17 = (bf16[384,640]{1,0:T(8,128)(2,1)}, bf16[384,640]{1,0:T(8,128)(2,1)}, u32[]{:S(2)}, u32[]{:S(2)}) collective-permute-start(bf16[384,640]{1,0:T(8,128)(2,1)} %pad_maximum_fusion.6), channel_id=1, source_target_pairs={{0,6},{1,7},{2,0},{3,1},{4,2},{5,3},{6,4},{7,5},{8,14},{9,15},{10,... | collective-permute-start | bytes 1474568 | tf_op jit(solution)/shard_map/ppermute | solution.py:69
  (11 other events, 65.2 us)
Sparse Core Ops, SparseCore 0:
  9.5 60.4 all-gather.2
  72.1 118.0 all-gather.4

commit v6 on v5

--- a/solution.py
+++ b/solution.py
@@ -240,16 +240,21 @@
     hidden = jax.nn.gelu(hidden_total, approximate=True).astype(jnp.bfloat16)
     core = column_index % 2
     down_by_core = down_t.reshape(Y_COUNT, mlp_count // Y_COUNT, width, hidden_units)
-    down_parts = [
-        jnp.einsum(
-            "th,ych->ytc",
-            hidden,
-            lax.dynamic_index_in_dim(down_by_core, pick, 1, keepdims=False),
-            preferred_element_type=jnp.float32,
-        ).astype(jnp.bfloat16)
-        for pick in (1 - core, core)
-    ]
-    down_sum = scatter_pair(lax.optimization_barrier(down_parts[1]), down_parts[0])
+    half_rows = tok_dev // 2
+    halves = []
+    for start in (0, half_rows):
+        rows = hidden[start : start + half_rows]
+        down_parts = [
+            jnp.einsum(
+                "th,ych->ytc",
+                rows,
+                lax.dynamic_index_in_dim(down_by_core, pick, 1, keepdims=False),
+                preferred_element_type=jnp.float32,
+            ).astype(jnp.bfloat16)
+            for pick in (1 - core, core)
+        ]
+        halves.append(scatter_pair(lax.optimization_barrier(down_parts[1]), down_parts[0]))
+    down_sum = jnp.concatenate(halves, axis=0)
     result = (values + gate_rows * down_sum).astype(jnp.bfloat16)
     return result.reshape(tok_dev, 1, width)
 

time: 258 us -> 277 us (1.074); the launches traced: 256 us -> 272 us
  starting transfers between devices: 39.9 us -> 55.4 us
  matrix products: 19.3 us -> 30.8 us
  waiting for transfers between devices: 85.6 us -> 78.9 us
  local copies, waits for them, and re-layouts: 51 us -> 48.1 us
    ppermute x3, starting transfers between devices: 4.63 us -> 14.3 us  [mlp_sum(): total = total + lax.ppermute(total, 'mlp', [(i, i ^ bit) for i in range(n)])]
    dot_general x2 -> x4, matrix products: 4.61 us -> 12.8 us  [local(): jnp.einsum('th,ych->ytc', rows, lax.dynamic_index_in_dim(down_by_core, pi...]
    ppermute x15 -> x20, waiting for transfers between devices: 43 us -> 36.3 us  [mlp_move(): return lax.ppermute(block, 'mlp', [(i, target(i)) for i in range(n)])]
    ppermute x15 -> x20, starting transfers between devices: 23.2 us -> 29 us  [mlp_move(): return lax.ppermute(block, 'mlp', [(i, target(i)) for i in range(n)])]
    dot_general x1, matrix products: 7.36 us -> 10.7 us  [local(): jnp.einsum('mtc,mch->th', normalized, up_w.reshape(mlp_count, width, hidd...]
    unnamed x43 -> x55, local copies, waits for them, and re-layouts: 5.92 us -> 4.13 us
  transfers between devices with their start and end apart: 22 -> 27, of which waited for: 16 -> 15; matrix products, arithmetic and copies ran while one was open for 32% -> 33% of each run, Pallas kernels for 0% -> 0%
where the time goes in v6:
time: 277 us; the launch traced here: 272 us
  waiting for transfers between devices  78.9 us (28%)
  starting transfers between devices  55.4 us (20%)
  local copies, waits for them, and re-layouts  48.1 us (17%)
  other arithmetic  42.4 us (15%)
  matrix products  30.8 us (11%)
  between operations  16.3 us (6%)
    ppermute x20, waiting for transfers between devices, mlp_move(): return lax.ppermute(block, 'mlp', [(i, target(i)) for i in range(n)])  36.3 us
    ppermute x20, starting transfers between devices, mlp_move(): return lax.ppermute(block, 'mlp', [(i, target(i)) for i in range(n)])  29 us
    ppermute x3, starting transfers between devices, mlp_sum(): total = total + lax.ppermute(total, 'mlp', [(i, i ^ bit) for i in range(n)])  14.3 us
    all_gather x1, waiting for transfers between devices, local(): out_w = lax.all_gather(output_weight, 'req', axis=1, tiled=True)  12.9 us
    dot_general x4, matrix products, local(): jnp.einsum('th,ych->ytc', rows, lax.dynamic_index_in_dim(down_by_core, pi...  12.8 us
    all_to_all x1, waiting for transfers between devices, local(): lax.all_to_all(send_layout(residual_input, offset, req_count), 'req', spl...  12.6 us
    slice x1, local copies, waits for them, and re-layouts, local(): up_w = both[0]  11.5 us
    all_to_all x1, waiting for transfers between devices, local(): lax.all_to_all(send_layout(attention_output, offset, req_count), 'req', s...  11.4 us
  transfers between devices with their start and end apart: 27, of which 15 were waited for; matrix products, arithmetic and copies ran while one was open for 33% of the time, Pallas kernels for 0%

profile of v6, /device:TPU:1, one launch (start us, length us, event | category | flops | bytes accessed | tf_op | source)
XLA Modules:
  0.0 272.0 jit_solution(9549815225516014791)
XLA Ops:
  7.3 2.4 pad_maximum_fusion.1
  14.5 8.4 %all-to-all-start = ((bf16[36,16,384]{2,0,1:T(8,128)(2,1)}), bf16[36,16,384]{2,0,1:T(8,128)(2,1)S(1)}, u32[]{:S(2)}, u32[]{:S(2)}) async-start(bf16[36,16,384]{2,0,1:T(8,128)(2,1)} %copy.87), calls=%async_computation | async-start | bytes 983040 | tf_op jit(solution)/shard_map/all_to_all | solution.py:156
  25.2 11.4 %all-to-all-done = bf16[36,16,384]{2,0,1:T(8,128)(2,1)S(1)} async-done(((bf16[36,16,384]{2,0,1:T(8,128)(2,1)}), bf16[36,16,384]{2,0,1:T(8,128)(2,1)S(1)}, u32[]{:S(2)}, u32[]{:S(2)}) %all-to-all-start) | async-done | bytes 442400 | tf_op jit(solution)/shard_map/all_to_all | solution.py:156
  36.6 3.6 %all-to-all-start.1 = ((bf16[36,16,640]{2,0,1:T(8,128)(2,1)}), bf16[36,16,640]{2,0,1:T(8,128)(2,1)S(1)}, u32[]{:S(2)}, u32[]{:S(2)}) async-start(bf16[36,16,640]{2,0,1:T(8,128)(2,1)} %copy.88), calls=%async_computation.1 | async-start | bytes 1638400 | tf_op jit(solution)/shard_map/all_to_all | solution.py:159
  41.6 12.6 %all-to-all-done.1 = bf16[36,16,640]{2,0,1:T(8,128)(2,1)S(1)} async-done(((bf16[36,16,640]{2,0,1:T(8,128)(2,1)}), bf16[36,16,640]{2,0,1:T(8,128)(2,1)S(1)}, u32[]{:S(2)}, u32[]{:S(2)}) %all-to-all-start.1) | async-done | bytes 737312 | tf_op jit(solution)/shard_map/all_to_all | solution.py:159
  57.1 12.9 %all-gather.3.cloned.1.call-done = bf16[384,5120]{0,1:T(8,128)(2,1)} async-done(((bf16[384,320]{0,1:T(8,128)(2,1)}), bf16[384,5120]{0,1:T(8,128)(2,1)}) %all-gather.3.cloned.1.call-update) | async-done | bytes 3932176 | tf_op jit(solution)/shard_map/all_gather | solution.py:144
  70.0 4.4 %convolution_convert_fusion = bf16[384,8,640]{2,0,1:T(8,128)(2,1)S(1)} fusion(bf16[384,8,640]{0,2,1:T(8,128)(2,1)} %bitcast.236, bf16[384,384]{1,0:T(8,128)(2,1)S(1)} %gather_fusion.1, pred[384]{0:T(512)(128)(4,1)S(1)} %compare_and_fusion.2), kind=kOutput, calls=%fused_computation.37 | convolution fusion | flops 1512062976 | bytes 8159616 | tf_op jit(solution)/shard_map/tk,kmc->mtc/dot_general | solution.py:172
  74.6 2.5 copy.96
  77.6 4.0 %collective-permute-done = bf16[4,394,640]{2,0,1:T(4,128)(2,1)} collective-permute-done((bf16[4,394,640]{2,0,1:T(4,128)(2,1)}, bf16[4,394,640]{2,0,1:T(4,128)(2,1)}, u32[]{:S(2)}, u32[]{:S(2)}) %collective-permute-start) | collective-permute-done | bytes 2017312 | tf_op jit(solution)/shard_map/ppermute | solution.py:69
  81.6 2.8 %convert_add_fusion = f32[4,394,640]{2,1,0:T(8,128)S(1)} fusion(s32[]{:T(128)S(6)} %select_n.272, bf16[4,2,10,640]{3,2,0,1:T(8,128)(2,1)S(1)} %broadcast_in_dim.135, bf16[4,394,640]{2,0,1:T(4,128)(2,1)} %collective-permute-done, bf16[4,2,384,640]{3,2,1,0:T(8,128)(2,1)} %bitcast.223), kind=kLoop, calls=%fused_computation.27 | loop fusion | flops 7060480 | bytes 10086404 | tf_op jit(solution)/shard_map/add | solution.py:86
  90.9 4.9 %collective-permute-done.1 = bf16[197,640]{1,0:T(8,128)(2,1)S(1)} collective-permute-done((bf16[197,640]{1,0:T(8,128)(2,1)S(1)}, bf16[197,640]{1,0:T(8,128)(2,1)S(1)}, u32[]{:S(2)}, u32[]{:S(2)}) %collective-permute-start.1) | collective-permute-done | bytes 252192 | tf_op jit(solution)/shard_map/ppermute | solution.py:69
  103.3 7.6 %collective-permute-done.2 = bf16[394,640]{1,0:T(8,128)(2,1)S(1)} collective-permute-done((bf16[394,640]{1,0:T(8,128)(2,1)S(1)}, bf16[394,640]{1,0:T(8,128)(2,1)S(1)}, u32[]{:S(2)}, u32[]{:S(2)}) %collective-permute-start.2) | collective-permute-done | bytes 504352 | tf_op jit(solution)/shard_map/ppermute | solution.py:69
  114.3 2.4 collective-permute-start.5
  122.8 5.4 %gather_fusion.4 = f32[384,5120]{1,0:T(8,128)} fusion(f32[8,5120]{1,0:T(8,128)S(1)} %get-tuple-element.32, s32[1024]{0:T(1024)S(1)} %pad_clamp_fusion), kind=kCustom, calls=%fused_computation.clone | custom fusion | bytes 15730176 | tf_op jit(solution)/shard_map/jit(_take)/gather | solution.py:168
  128.2 5.5 %gather_fusion.5 = f32[384,5120]{1,0:T(8,128)} fusion(f32[8,5120]{1,0:T(8,128)S(1)} %get-tuple-element.31, s32[1024]{0:T(1024)S(1)} %pad_clamp_fusion), kind=kCustom, calls=%fused_computation.1.clone | custom fusion | bytes 15730176 | tf_op jit(solution)/shard_map/jit(_take)/gather | solution.py:167
  133.6 10.9 %collective-permute-done.6 = bf16[2,384,640]{2,1,0:T(8,128)(2,1)S(1)} collective-permute-done((bf16[2,384,640]{2,1,0:T(8,128)(2,1)}, bf16[2,384,640]{2,1,0:T(8,128)(2,1)S(1)}, u32[]{:S(2)}, u32[]{:S(2)}) %collective-permute-start.6) | collective-permute-done | bytes 983072 | tf_op jit(solution)/shard_map/ppermute | solution.py:69
  147.3 2.7 collective-permute-start.9
  150.0 10.3 %select_add_fusion = (f32[384,5120]{1,0:T(8,128)}, f32[384,5120]{1,0:T(8,128)}) fusion(f32[384,5120]{1,0:T(8,128)} %gather_fusion.4, pred[384]{0:T(512)(128)(4,1)S(1)} %compare_and_fusion.1, f32[384,5120]{1,0:T(8,128)} %gather_fusion.5), kind=kLoop, calls=%fused_computation.16 | loop fusion | flops 5898240 | bytes 31457664 | tf_op jit(solution)/shard_map/add | solution.py:213
  161.7 3.4 %pad_maximum_fusion = bf16[4,2,384,640]{3,2,1,0:T(8,128)(2,1)} fusion(bf16[1,2,384,640]{3,2,1,0:T(8,128)(2,1)} %bitcast.34, bf16[1,2,384,640]{3,2,1,0:T(8,128)(2,1)S(1)} %maximum_bitcast_fusion, bf16[1,2,384,640]{3,2,1,0:T(8,128)(2,1)S(1)} %bitcast.237, bf16[1,2,384,640]{3,2,1,0:T(8,128)(2,1)S(1)} %get-tuple-element.26), kind=kLoop, calls=%fused_computation.32 | loop fusion | flops 5898240 | bytes 7864320 | tf_op jit(solution)/shard_map/stack | solution.py:116
  165.0 5.1 %gather_fusion.3 = bf16[8,384,640]{2,1,0:T(8,128)(2,1)} fusion(bf16[8,384,640]{2,1,0:T(8,128)(2,1)} %bitcast.228, s32[1024]{0:T(1024)S(1)} %pad_clamp_fusion.1), kind=kCustom, calls=%fused_computation.5 | custom fusion | bytes 7864352 | tf_op jit(solution)/shard_map/jit(_take)/gather | solution.py:119
  170.2 3.7 %convert_reduce_fusion = (f32[384]{0:T(512)S(1)}, f32[384]{0:T(512)S(1)}) fusion(bf16[8,384,640]{2,1,0:T(8,128)(2,1)} %gather_fusion.3, pred[8]{0:T(512)(128)(4,1)S(1)} %compare_and_fusion), kind=kLoop, calls=%fused_computation.8 | loop fusion | flops 9829632 | bytes 3935240 | tf_op jit(solution)/shard_map/reduce_sum | solution.py:210
  174.0 6.7 %fusion.3 = bf16[8,384,640]{2,1,0:T(8,128)(2,1)S(1)} fusion(f32[48,8,8,640]{3,2,1,0:T(8,128)} %bitcast.225, f32[48,8,8,640]{3,2,1,0:T(8,128)} %bitcast.224, f32[384]{0:T(512)S(1)} %get-tuple-element.38, f32[384]{0:T(512)S(1)} %get-tuple-element.37, bf16[8,384,640]{2,1,0:T(8,128)(2,1)S(1)} %copy-done.2, pred[8]{0:T(512)(128)(4,1)S(1)} %compare_and_fusion), kind=kLoop, calls=%fused_computation.12 | loop fusion | flops 13762560 | bytes 23596040 | tf_op jit(solution)/shard_map/convert_element_type | solution.py:217
  185.5 3.1 %collective-permute-done.11 = f32[384,16]{0,1:T(8,128)S(1)} collective-permute-done((f32[384,16]{0,1:T(8,128)S(1)}, f32[384,16]{0,1:T(8,128)S(1)}, u32[]{:S(2)}, u32[]{:S(2)}) %collective-permute-start.11) | collective-permute-done | bytes 24608 | tf_op jit(solution)/shard_map/ppermute | solution.py:62
  188.5 12.8 %collective-permute-start.12 = (f32[384,16]{0,1:T(8,128)S(1)}, f32[384,16]{0,1:T(8,128)S(1)}, u32[]{:S(2)}, u32[]{:S(2)}) collective-permute-start(f32[384,16]{0,1:T(8,128)S(1)} %add.421), channel_id=1, source_target_pairs={{0,4},{1,5},{2,6},{3,7},{4,0},{5,1},{6,2},{7,3},{8,12},{9,13},{10,... | collective-permute-start | bytes 73736 | tf_op jit(solution)/shard_map/ppermute | solution.py:62
  202.6 11.5 %fusion.126 = (bf16[1,5120,864]{2,1,0:T(8,128)(2,1)}, bf16[1,5120,864]{2,1,0:T(8,128)(2,1)S(1)}) fusion(bf16[2,5120,864]{2,1,0:T(8,128)(2,1)} %all-gather.5.cloned.1.call-done), kind=kLoop, calls=%fused_computation.237 | loop fusion | bytes 35389440 | tf_op jit(solution)/shard_map/slice | solution.py:147
  214.1 10.7 %convolution_bitcast_fusion.1 = f32[384,864]{0,1:T(8,128)S(1)} fusion(bf16[8,384,640]{2,1,0:T(8,128)(2,1)S(1)} %copy-done.6, bf16[8,640,864]{2,1,0:T(8,128)(2,1)} %bitcast.235), kind=kOutput, calls=%fused_computation.52 | convolution fusion | flops 3397386240 | bytes 14106624 | tf_op jit(solution)/shard_map/mtc,mch->th/dot_general | solution.py:229
  225.5 2.6 fusion.37
  232.3 4.2 %fusion.34 = bf16[4,192,640]{2,1,0:T(8,128)(2,1)S(1)} fusion(bf16[4,2,640,864]{3,2,1,0:T(8,128)(2,1)} %bitcast.230, s32[]{:T(128)S(6)} %select_n.273, bf16[384,864]{0,1:T(8,128)(2,1)S(1)} %copy-done.22), kind=kOutput, calls=%fused_computation.54 | convolution fusion | flops 849838080 | bytes 6012932 | tf_op jit(solution)/shard_map/th,ych->ytc/dot_general | solution.py:248
  236.6 4.2 %fusion.43 = bf16[4,192,640]{2,1,0:T(8,128)(2,1)S(1)} fusion(bf16[4,2,640,864]{3,2,1,0:T(8,128)(2,1)} %bitcast.231, s32[]{:T(128)S(6)} %select_n.272, bf16[384,864]{0,1:T(8,128)(2,1)} %copy-done.21), kind=kOutput, calls=%fused_computation.57 | convolution fusion | flops 849838080 | bytes 6012932 | tf_op jit(solution)/shard_map/th,ych->ytc/dot_general | solution.py:248
  244.9 2.8 %collective-permute-start.16 = (bf16[96,640]{1,0:T(8,128)(2,1)S(1)}, bf16[96,640]{1,0:T(8,128)(2,1)S(1)}, u32[]{:S(2)}, u32[]{:S(2)}) collective-permute-start(bf16[96,640]{1,0:T(8,128)(2,1)S(1)} %get-tuple-element.34), channel_id=1, source_target_pairs={{0,6},{1,7},{2,0},{3,1},{4,2},{5,3},{6,4},{7,5},{8,14},{9,15},{10,... | collective-permute-start | bytes 368648 | tf_op jit(solution)/shard_map/ppermute | solution.py:69
  248.0 2.7 collective-permute-start.21
  258.7 5.2 %collective-permute-done.20 = bf16[192,640]{1,0:T(8,128)(2,1)S(1)} collective-permute-done((bf16[192,640]{1,0:T(8,128)(2,1)S(1)}, bf16[192,640]{1,0:T(8,128)(2,1)S(1)}, u32[]{:S(2)}, u32[]{:S(2)}) %collective-permute-start.20) | collective-permute-done | bytes 245792 | tf_op jit(solution)/shard_map/ppermute | solution.py:69
  (182 shorter events, 62.5 us)
Async XLA Ops:
  6.5 218.2 %copy-start = (bf16[16,16,864]{2,1,0:T(8,128)(2,1)S(1)}, bf16[16,16,864]{2,1,0:T(8,128)(2,1)}, u32[]{:S(2)}) copy-start(bf16[16,16,864]{2,1,0:T(8,128)(2,1)} %param.25) | copy-start | bytes 1327108
  6.5 63.5 %all-gather.3.cloned.1.call-start = ((), (), s32[]{:S(2)}) async-start(), calls=%async_computation.2 | async-start | bytes 4177920 | tf_op jit(solution)/shard_map/all_gather | solution.py:144
  7.3 195.3 %all-gather.5.cloned.1.call-start = ((), (), s32[]{:S(2)}) async-start(), calls=%async_computation.3 | async-start | bytes 19496960 | tf_op jit(solution)/shard_map/all_gather | solution.py:146
  14.5 22.1 %all-to-all-start = ((bf16[36,16,384]{2,0,1:T(8,128)(2,1)}), bf16[36,16,384]{2,0,1:T(8,128)(2,1)S(1)}, u32[]{:S(2)}, u32[]{:S(2)}) async-start(bf16[36,16,384]{2,0,1:T(8,128)(2,1)} %copy.87), calls=%async_computation | async-start | bytes 983040 | tf_op jit(solution)/shard_map/all_to_all | solution.py:156
  23.0 33.4 %copy-start.20 = (bf16[384,16,16]{0,2,1:T(8,128)(2,1)S(1)}, bf16[384,16,16]{0,2,1:T(8,128)(2,1)}, u32[]{:S(2)}) copy-start(bf16[384,16,16]{0,2,1:T(8,128)(2,1)} %param.21) | copy-start | bytes 589828
  36.6 17.7 %all-to-all-start.1 = ((bf16[36,16,640]{2,0,1:T(8,128)(2,1)}), bf16[36,16,640]{2,0,1:T(8,128)(2,1)S(1)}, u32[]{:S(2)}, u32[]{:S(2)}) async-start(bf16[36,16,640]{2,0,1:T(8,128)(2,1)} %copy.88), calls=%async_computation.1 | async-start | bytes 1638400 | tf_op jit(solution)/shard_map/all_to_all | solution.py:159
  40.9 33.5 %copy-start.12 = (s32[1024]{0:T(1024)}, s32[1024]{0:T(1024)S(1)}, u32[]{:S(2)}) copy-start(s32[1024]{0:T(1024)S(1)} %pad_clamp_fusion.3) | copy-start | bytes 12292
  41.0 33.4 %copy-start.16 = (pred[384]{0:T(512)(128)(4,1)}, pred[384]{0:T(512)(128)(4,1)S(1)}, u32[]{:S(2)}) copy-start(pred[384]{0:T(512)(128)(4,1)S(1)} %compare_and_fusion.2) | copy-start | bytes 1156
  41.6 32.8 %copy-start.10 = (f32[384,16]{0,1:T(8,128)}, f32[384,16]{0,1:T(8,128)S(1)}, u32[]{:S(2)}) copy-start(f32[384,16]{0,1:T(8,128)S(1)} %get-tuple-element.40) | copy-start | bytes 73732
  77.1 4.5 %collective-permute-start = (bf16[4,394,640]{2,0,1:T(4,128)(2,1)}, bf16[4,394,640]{2,0,1:T(4,128)(2,1)}, u32[]{:S(2)}, u32[]{:S(2)}) collective-permute-start(bf16[4,394,640]{2,0,1:T(4,128)(2,1)} %copy.96), channel_id=1, source_target_pairs={{0,1},{1,0},{2,3},{3,2},{4,5},{5,4},{6,7},{7,6},{8,9},{9,8},{10,11... | collective-permute-start | bytes 6051848 | tf_op jit(solution)/shard_map/ppermute | solution.py:69
  86.6 9.2 %collective-permute-start.1 = (bf16[197,640]{1,0:T(8,128)(2,1)S(1)}, bf16[197,640]{1,0:T(8,128)(2,1)S(1)}, u32[]{:S(2)}, u32[]{:S(2)}) collective-permute-start(bf16[197,640]{1,0:T(8,128)(2,1)S(1)} %get-tuple-element.28), channel_id=1, source_target_pairs={{0,2},{1,3},{2,4},{3,5},{4,6},{5,7},{6,0},{7,1},{8,10},{9,11},{10,... | collective-permute-start | bytes 756488 | tf_op jit(solution)/shard_map/ppermute | solution.py:69
  88.0 7.8 %collective-permute-start.3 = (bf16[197,640]{1,0:T(8,128)(2,1)S(1)}, bf16[197,640]{1,0:T(8,128)(2,1)S(1)}, u32[]{:S(2)}, u32[]{:S(2)}) collective-permute-start(bf16[197,640]{1,0:T(8,128)(2,1)S(1)} %get-tuple-element.29), channel_id=1, source_target_pairs={{0,6},{1,7},{2,0},{3,1},{4,2},{5,3},{6,4},{7,5},{8,14},{9,15},{10,... | collective-permute-start | bytes 756488 | tf_op jit(solution)/shard_map/ppermute | solution.py:69
  97.3 13.6 %collective-permute-start.2 = (bf16[394,640]{1,0:T(8,128)(2,1)S(1)}, bf16[394,640]{1,0:T(8,128)(2,1)S(1)}, u32[]{:S(2)}, u32[]{:S(2)}) collective-permute-start(bf16[394,640]{1,0:T(8,128)(2,1)S(1)} %pad_maximum_fusion.3), channel_id=1, source_target_pairs={{0,2},{1,3},{2,4},{3,5},{4,6},{5,7},{6,0},{7,1},{8,10},{9,11},{10,... | collective-permute-start | bytes 1512968 | tf_op jit(solution)/shard_map/ppermute | solution.py:69
  98.8 12.3 %collective-permute-start.4 = (bf16[394,640]{1,0:T(8,128)(2,1)}, bf16[394,640]{1,0:T(8,128)(2,1)S(1)}, u32[]{:S(2)}, u32[]{:S(2)}) collective-permute-start(bf16[394,640]{1,0:T(8,128)(2,1)} %pad_maximum_fusion.4), channel_id=1, source_target_pairs={{0,6},{1,7},{2,0},{3,1},{4,2},{5,3},{6,4},{7,5},{8,14},{9,15},{10,... | collective-permute-start | bytes 1512968 | tf_op jit(solution)/shard_map/ppermute | solution.py:69
  114.3 3.9 %collective-permute-start.5 = (bf16[384,640]{1,0:T(8,128)(2,1)S(1)}, bf16[384,640]{1,0:T(8,128)(2,1)S(1)}, u32[]{:S(2)}, u32[]{:S(2)}) collective-permute-start(bf16[384,640]{1,0:T(8,128)(2,1)S(1)} %fusion.58), channel_id=1, source_target_pairs={{0,1},{1,0},{2,3},{3,2},{4,5},{5,4},{6,7},{7,6},{8,9},{9,8},{10,11... | collective-permute-start | bytes 1474568 | tf_op jit(solution)/shard_map/ppermute | solution.py:69
  119.3 25.3 %collective-permute-start.6 = (bf16[2,384,640]{2,1,0:T(8,128)(2,1)}, bf16[2,384,640]{2,1,0:T(8,128)(2,1)S(1)}, u32[]{:S(2)}, u32[]{:S(2)}) collective-permute-start(bf16[2,384,640]{2,1,0:T(8,128)(2,1)} %get-tuple-element.27), channel_id=1, source_target_pairs={{0,2},{1,3},{2,4},{3,5},{4,6},{5,7},{6,0},{7,1},{8,10},{9,11},{10,... | collective-permute-start | bytes 2949128 | tf_op jit(solution)/shard_map/ppermute | solution.py:69
  120.6 24.9 %collective-permute-start.8 = (bf16[2,384,640]{2,1,0:T(8,128)(2,1)}, bf16[2,384,640]{2,1,0:T(8,128)(2,1)}, u32[]{:S(2)}, u32[]{:S(2)}) collective-permute-start(bf16[2,384,640]{2,1,0:T(8,128)(2,1)} %get-tuple-element.27), channel_id=1, source_target_pairs={{0,6},{1,7},{2,0},{3,1},{4,2},{5,3},{6,4},{7,5},{8,14},{9,15},{10,... | collective-permute-start | bytes 2949128 | tf_op jit(solution)/shard_map/ppermute | solution.py:69
  145.4 14.9 %collective-permute-start.7 = (bf16[1,384,640]{2,1,0:T(8,128)(2,1)}, bf16[1,384,640]{2,1,0:T(8,128)(2,1)}, u32[]{:S(2)}, u32[]{:S(2)}) collective-permute-start(bf16[1,384,640]{2,1,0:T(8,128)(2,1)} %slice.210), channel_id=1, source_target_pairs={{0,2},{1,3},{2,4},{3,5},{4,6},{5,7},{6,0},{7,1},{8,10},{9,11},{10,... | collective-permute-start | bytes 1474568 | tf_op jit(solution)/shard_map/ppermute | solution.py:69
  147.3 13.1 %collective-permute-start.9 = (bf16[1,384,640]{2,1,0:T(8,128)(2,1)}, bf16[1,384,640]{2,1,0:T(8,128)(2,1)}, u32[]{:S(2)}, u32[]{:S(2)}) collective-permute-start(bf16[1,384,640]{2,1,0:T(8,128)(2,1)} %slice.211), channel_id=1, source_target_pairs={{0,6},{1,7},{2,0},{3,1},{4,2},{5,3},{6,4},{7,5},{8,14},{9,15},{10,... | collective-permute-start | bytes 1474568 | tf_op jit(solution)/shard_map/ppermute | solution.py:69
  183.1 2.4 collective-permute-start.10
  185.5 3.1 %collective-permute-start.11 = (f32[384,16]{0,1:T(8,128)S(1)}, f32[384,16]{0,1:T(8,128)S(1)}, u32[]{:S(2)}, u32[]{:S(2)}) collective-permute-start(f32[384,16]{0,1:T(8,128)S(1)} %fusion.122), channel_id=1, source_target_pairs={{0,2},{1,3},{2,0},{3,1},{4,6},{5,7},{6,4},{7,5},{8,10},{9,11},{10,... | collective-permute-start | bytes 73736 | tf_op jit(solution)/shard_map/ppermute | solution.py:62
  188.5 14.0 %collective-permute-start.12 = (f32[384,16]{0,1:T(8,128)S(1)}, f32[384,16]{0,1:T(8,128)S(1)}, u32[]{:S(2)}, u32[]{:S(2)}) collective-permute-start(f32[384,16]{0,1:T(8,128)S(1)} %add.421), channel_id=1, source_target_pairs={{0,4},{1,5},{2,6},{3,7},{4,0},{5,1},{6,2},{7,3},{8,12},{9,13},{10,... | collective-permute-start | bytes 73736 | tf_op jit(solution)/shard_map/ppermute | solution.py:62
  228.2 14.5 %collective-permute-start.13 = (bf16[4,192,640]{2,1,0:T(8,128)(2,1)}, bf16[4,192,640]{2,1,0:T(8,128)(2,1)}, u32[]{:S(2)}, u32[]{:S(2)}) collective-permute-start(bf16[4,192,640]{2,1,0:T(8,128)(2,1)} %fusion.37), channel_id=1, source_target_pairs={{0,1},{1,0},{2,3},{3,2},{4,5},{5,4},{6,7},{7,6},{8,9},{9,8},{10,11... | collective-permute-start | bytes 2949128 | tf_op jit(solution)/shard_map/ppermute | solution.py:69
  236.5 11.1 %collective-permute-start.18 = (bf16[4,192,640]{2,1,0:T(8,128)(2,1)S(1)}, bf16[4,192,640]{2,1,0:T(8,128)(2,1)S(1)}, u32[]{:S(2)}, u32[]{:S(2)}) collective-permute-start(bf16[4,192,640]{2,1,0:T(8,128)(2,1)S(1)} %fusion.34), channel_id=1, source_target_pairs={{0,1},{1,0},{2,3},{3,2},{4,5},{5,4},{6,7},{7,6},{8,9},{9,8},{10,11... | collective-permute-start | bytes 2949128 | tf_op jit(solution)/shard_map/ppermute | solution.py:69
  244.1 6.7 %collective-permute-start.14 = (bf16[96,640]{1,0:T(8,128)(2,1)S(1)}, bf16[96,640]{1,0:T(8,128)(2,1)S(1)}, u32[]{:S(2)}, u32[]{:S(2)}) collective-permute-start(bf16[96,640]{1,0:T(8,128)(2,1)S(1)} %get-tuple-element.33), channel_id=1, source_target_pairs={{0,2},{1,3},{2,4},{3,5},{4,6},{5,7},{6,0},{7,1},{8,10},{9,11},{10,... | collective-permute-start | bytes 368648 | tf_op jit(solution)/shard_map/ppermute | solution.py:69
  244.9 6.0 %collective-permute-start.16 = (bf16[96,640]{1,0:T(8,128)(2,1)S(1)}, bf16[96,640]{1,0:T(8,128)(2,1)S(1)}, u32[]{:S(2)}, u32[]{:S(2)}) collective-permute-start(bf16[96,640]{1,0:T(8,128)(2,1)S(1)} %get-tuple-element.34), channel_id=1, source_target_pairs={{0,6},{1,7},{2,0},{3,1},{4,2},{5,3},{6,4},{7,5},{8,14},{9,15},{10,... | collective-permute-start | bytes 368648 | tf_op jit(solution)/shard_map/ppermute | solution.py:69
  248.0 5.8 %collective-permute-start.19 = (bf16[96,640]{1,0:T(8,128)(2,1)S(1)}, bf16[96,640]{1,0:T(8,128)(2,1)S(1)}, u32[]{:S(2)}, u32[]{:S(2)}) collective-permute-start(bf16[96,640]{1,0:T(8,128)(2,1)S(1)} %get-tuple-element.35), channel_id=1, source_target_pairs={{0,2},{1,3},{2,4},{3,5},{4,6},{5,7},{6,0},{7,1},{8,10},{9,11},{10,... | collective-permute-start | bytes 368648 | tf_op jit(solution)/shard_map/ppermute | solution.py:69
  248.0 5.7 %collective-permute-start.21 = (bf16[96,640]{1,0:T(8,128)(2,1)S(1)}, bf16[96,640]{1,0:T(8,128)(2,1)S(1)}, u32[]{:S(2)}, u32[]{:S(2)}) collective-permute-start(bf16[96,640]{1,0:T(8,128)(2,1)S(1)} %get-tuple-element.36), channel_id=1, source_target_pairs={{0,6},{1,7},{2,0},{3,1},{4,2},{5,3},{6,4},{7,5},{8,14},{9,15},{10,... | collective-permute-start | bytes 368648 | tf_op jit(solution)/shard_map/ppermute | solution.py:69
  250.9 7.6 %collective-permute-start.15 = (bf16[192,640]{1,0:T(8,128)(2,1)S(1)}, bf16[192,640]{1,0:T(8,128)(2,1)S(1)}, u32[]{:S(2)}, u32[]{:S(2)}) collective-permute-start(bf16[192,640]{1,0:T(8,128)(2,1)S(1)} %pad_maximum_fusion.5), channel_id=1, source_target_pairs={{0,2},{1,3},{2,4},{3,5},{4,6},{5,7},{6,0},{7,1},{8,10},{9,11},{10,... | collective-permute-start | bytes 737288 | tf_op jit(solution)/shard_map/ppermute | solution.py:69
  251.6 7.0 %collective-permute-start.17 = (bf16[192,640]{1,0:T(8,128)(2,1)S(1)}, bf16[192,640]{1,0:T(8,128)(2,1)S(1)}, u32[]{:S(2)}, u32[]{:S(2)}) collective-permute-start(bf16[192,640]{1,0:T(8,128)(2,1)S(1)} %pad_maximum_fusion.6), channel_id=1, source_target_pairs={{0,6},{1,7},{2,0},{3,1},{4,2},{5,3},{6,4},{7,5},{8,14},{9,15},{10,... | collective-permute-start | bytes 737288 | tf_op jit(solution)/shard_map/ppermute | solution.py:69
  253.9 10.0 %collective-permute-start.20 = (bf16[192,640]{1,0:T(8,128)(2,1)S(1)}, bf16[192,640]{1,0:T(8,128)(2,1)S(1)}, u32[]{:S(2)}, u32[]{:S(2)}) collective-permute-start(bf16[192,640]{1,0:T(8,128)(2,1)S(1)} %pad_maximum_fusion.7), channel_id=1, source_target_pairs={{0,2},{1,3},{2,4},{3,5},{4,6},{5,7},{6,0},{7,1},{8,10},{9,11},{10,... | collective-permute-start | bytes 737288 | tf_op jit(solution)/shard_map/ppermute | solution.py:69
  254.3 9.5 %collective-permute-start.22 = (bf16[192,640]{1,0:T(8,128)(2,1)S(1)}, bf16[192,640]{1,0:T(8,128)(2,1)S(1)}, u32[]{:S(2)}, u32[]{:S(2)}) collective-permute-start(bf16[192,640]{1,0:T(8,128)(2,1)S(1)} %pad_maximum_fusion.8), channel_id=1, source_target_pairs={{0,6},{1,7},{2,0},{3,1},{4,2},{5,3},{6,4},{7,5},{8,14},{9,15},{10,... | collective-permute-start | bytes 737288 | tf_op jit(solution)/shard_map/ppermute | solution.py:69
  (22 other events, 192.8 us)
Sparse Core Ops, SparseCore 0:
  9.5 60.4 all-gather.2
  72.1 118.0 all-gather.4
